TPU v7x, 256 devices: a whole 4x4x8 slice. The times are simulated.
256 devices in a mesh: in: 4 (over x), out: 64 (over z, y, core).
Axes of the slice: x: 4, y: 4, z: 8, core: 2. Of those that a mesh axis runs over, the one named last changes fastest.
Arguments:
- activations: bfloat16 [8192, 4096], P('out', 'in'), may hold values from -6 to 6
- out_grad: bfloat16 [8192, 16384], P('in', 'out'), may hold values from -0.06591797 to 0.06591797
- block_rows: int32 [4, 64, 4], P('in', 'out'), may hold values from 0 to 31, as said below
- block_cols: int32 [4, 64, 4], P('in', 'out'), may hold values from 0 to 127, as said below
- counts: int32 [4, 64], P('in', 'out'), may hold values from 1 to 4, as said below
Outputs:
- grad_blocks: float32 [4, 64, 4, 128, 128], P('in', 'out')
Inputs may be any that keep to these rules, and one draw needn't show every extreme that they name: `block_rows`: tile (i, j) lists blocks of its own region only: rows i * 8 to (i + 1) * 8 - 1; slots of one tile name different blocks, and slots past counts[i, j] also name blocks of the tile. `block_cols`: columns j * 2 to (j + 1) * 2 - 1 for tile (i, j). `counts`: some tile has a full list in every draw.
All inputs are finite; a program needn't handle non-finite values.
Results may differ from a plain program's by a relative error of at most 0.0003.
Values may be sent and summed in bfloat16 or wider, within the bound.
No kernel may reach another device: no remote copies, remote signals or barrier semaphores. Data moves between devices by JAX's collectives and lax.ppermute only.
A program may use at most 128 MiB of HBM per device.

v0:
```python
import functools

import jax
import jax.numpy as jnp
from jax import lax
from jax.experimental import pallas as pl
from jax.experimental.pallas import tpu as pltpu
from jax.sharding import PartitionSpec as P

BLK = 128
MAXB = 4


def block_kernel(n_grad, ny, rows_ref, cols_ref, use_ref, starts_ref, place_ref, *rest):
    first_hbm, second_hbm = rest[0], rest[1]
    grad_hbm = rest[2:2 + n_grad]
    out_ref, a_v, g_v, sems = rest[2 + n_grad:]
    chunks, _, tok, _ = a_v.shape[1:]

    copies = []
    for s in range(MAXB):
        r = pl.multiple_of(rows_ref[s] * BLK, BLK)
        c = pl.multiple_of(cols_ref[s] * BLK, BLK)
        slot = [
            pltpu.make_async_copy(first_hbm.at[:, :, pl.ds(r, BLK)], a_v.at[s, :, 0], sems.at[s, 0]),
            pltpu.make_async_copy(second_hbm.at[:, :, pl.ds(r, BLK)], a_v.at[s, :, 1], sems.at[s, 1]),
        ]
        for p, piece in enumerate(grad_hbm):
            slot.append(
                pltpu.make_async_copy(
                    piece.at[:, :, :, pl.ds(c, BLK)],
                    g_v.at[s, pl.ds(starts_ref[p], piece.shape[0])],
                    sems.at[s, p + 2],
                )
            )

        @pl.when(use_ref[s] == 1)
        def _(slot=slot):
            for cp in slot:
                cp.start()

        copies.append(slot)

    z_me, y_me = place_ref[0], place_ref[1]
    nz = chunks // ny
    for s in range(MAXB):

        @pl.when(use_ref[s] == 0)
        def _(s=s):
            out_ref[s] = jnp.zeros((BLK, BLK), jnp.float32)

        @pl.when(use_ref[s] == 1)
        def _(s=s):
            for cp in copies[s]:
                cp.wait()

            def body(k, acc):
                pair = ((z_me + k // ny) % nz) * ny + (y_me + k % ny) % ny
                a = a_v[s, k].reshape(2 * tok, BLK)
                g = g_v[s, pair].reshape(2 * tok, BLK)
                return acc + lax.dot_general(
                    a, g, (((0,), (0,)), ((), ())), preferred_element_type=jnp.float32
                )

            out_ref[s] = lax.fori_loop(
                0, chunks, body, jnp.zeros((BLK, BLK), jnp.float32), unroll=2
            )


def block_products(first, second, grad_pieces, starts, place, local_rows, local_cols, use, ny):
    chunks, tok, width = first.shape
    n_grad = len(grad_pieces)
    smem = pl.BlockSpec(memory_space=pltpu.SMEM)
    hbm = pl.BlockSpec(memory_space=pl.ANY)
    tokens = 2 * chunks * tok
    flops = 2 * MAXB * tokens * BLK * BLK
    moved = 2 * MAXB * tokens * BLK * 2 + MAXB * BLK * BLK * 4
    return pl.pallas_call(
        functools.partial(block_kernel, n_grad, ny),
        out_shape=jax.ShapeDtypeStruct((MAXB, BLK, BLK), jnp.float32),
        in_specs=[smem] * 5 + [hbm] * (2 + n_grad),
        out_specs=pl.BlockSpec(memory_space=pltpu.VMEM),
        scratch_shapes=[
            pltpu.VMEM((MAXB, chunks, 2, tok, BLK), jnp.bfloat16),
            pltpu.VMEM((MAXB, chunks, 2, tok, BLK), jnp.bfloat16),
            pltpu.SemaphoreType.DMA((MAXB, 2 + n_grad)),
        ],
        compiler_params=pltpu.CompilerParams(vmem_limit_bytes=48 * 1024 * 1024),
        cost_estimate=pl.CostEstimate(flops=flops, bytes_accessed=moved, transcendentals=0),
    )(local_rows, local_cols, use, starts, place, first, second, *grad_pieces)


def relative_gather(x, axis, n):
    right = [(k, (k + 1) % n) for k in range(n)]
    left = [(k, (k - 1) % n) for k in range(n)]
    rel = [x] + [None] * (n - 1)
    from_left, from_right = x, x
    for t in range(1, (n + 1) // 2):
        from_left = lax.ppermute(from_left, axis, right)
        from_right = lax.ppermute(from_right, axis, left)
        rel[n - t] = from_left
        rel[t] = from_right
    if n % 2 == 0 and n > 1:
        t = n // 2
        half = x.shape[0] // 2
        near_a = lax.ppermute(from_left[:half], axis, right)
        near_b = lax.ppermute(from_right[half:], axis, left)
        rel[t] = jnp.concatenate([near_a, near_b], 0)
    return rel


def ring_gather(own, axis, place):
    n = lax.axis_size(axis)
    length = own.shape[0]
    right = [(k, (k + 1) % n) for k in range(n)]
    left = [(k, (k - 1) % n) for k in range(n)]
    pieces, starts = [own], [place * length]
    from_left, from_right = own, own
    for d in range(1, (n + 1) // 2):
        from_left = lax.ppermute(from_left, axis, right)
        from_right = lax.ppermute(from_right, axis, left)
        pieces += [from_left, from_right]
        starts += [((place - d) % n) * length, ((place + d) % n) * length]
    if n % 2 == 0 and n > 1:
        half = length // 2
        d = n // 2
        if d == 1:
            near_a, near_b = lax.ppermute(own[:half], axis, right), lax.ppermute(own[half:], axis, left)
        else:
            near_a = lax.ppermute(from_left[:half], axis, right)
            near_b = lax.ppermute(from_right[half:], axis, left)
        far = ((place + d) % n) * length
        pieces += [near_a, near_b]
        starts += [far, far + half]
    return pieces, jnp.stack(starts).astype(jnp.int32)


def on_device(activations, out_grad, block_rows, block_cols, counts):
    in_place = lax.axis_index("in")
    core = lax.axis_index("core")
    nz, ny, ncore = lax.axis_size("z"), lax.axis_size("y"), lax.axis_size("core")
    z_me, y_me = lax.axis_index("z"), lax.axis_index("y")
    out_place = (z_me * ny + y_me) * ncore + core
    tok = activations.shape[0]
    tile_rows = activations.shape[1] // BLK
    tile_cols = out_grad.shape[1] // BLK
    half_rows = tile_rows // 2
    local_rows = jnp.clip(block_rows[0, 0] - in_place * tile_rows, 0, tile_rows - 1)
    local_cols = jnp.clip(block_cols[0, 0] - out_place * tile_cols, 0, tile_cols - 1)
    live = jnp.arange(MAXB, dtype=jnp.int32) < counts[0, 0]
    mine_half = (local_rows // half_rows) == core
    use_mine = (live & mine_half).astype(jnp.int32)
    use_other = (live & ~mine_half).astype(jnp.int32)
    in_half = (local_rows % half_rows).astype(jnp.int32)
    place = jnp.stack([z_me, y_me]).astype(jnp.int32)

    width = half_rows * BLK
    first, second = activations[:, :width], activations[:, width:]
    on_first = core == 0
    keep = jnp.where(on_first, first, second)
    send = jnp.where(on_first, second, first)
    swap = [(0, 1), (1, 0)]
    recv = lax.ppermute(send, "core", swap)
    lead = jnp.where(on_first, keep, recv)
    trail = jnp.where(on_first, recv, keep)

    lead_z = jnp.stack(relative_gather(lead, "z", nz), 0)
    lead_all = jnp.stack(relative_gather(lead_z, "y", ny), 1)
    trail_y = jnp.stack(relative_gather(trail, "y", ny), 0)
    trail_all = jnp.stack(relative_gather(trail_y, "z", nz), 0)
    lead_all = lead_all.reshape(nz * ny, tok, width)
    trail_all = trail_all.reshape(nz * ny, tok, width)

    grad_pieces, starts = ring_gather(out_grad, "in", in_place)
    lead_all, trail_all, grad_pieces = lax.optimization_barrier((lead_all, trail_all, grad_pieces))
    grad_pieces = [g.reshape(g.shape[0] // (2 * tok), 2, tok, g.shape[1]) for g in grad_pieces]
    starts = starts // (2 * tok)
    lead_other = lax.ppermute(lead_all, "core", swap)
    trail_other = lax.ppermute(trail_all, "core", swap)
    part_mine = block_products(
        lead_all, trail_all, grad_pieces, starts, place, in_half, local_cols, use_mine, ny
    )
    part_other = block_products(
        lead_other, trail_other, grad_pieces, starts, place, in_half, local_cols, use_other, ny
    )
    totals = part_mine + part_other
    return totals.reshape(1, 1, MAXB, BLK, BLK)


def solution(mesh):
    n_in, n_out = mesh.devices.shape
    row = mesh.devices[0]
    ny = len({d.coords[1] for d in row})
    ncore = n_out // len({tuple(d.coords) for d in row})
    nz = n_out // (ny * ncore)
    split = jax.sharding.Mesh(
        mesh.devices.reshape(n_in, nz, ny, ncore), ("in", "z", "y", "core")
    )
    out = ("z", "y", "core")
    return jax.shard_map(
        on_device,
        mesh=split,
        in_specs=(
            P(out, "in"),
            P("in", out),
            P("in", out, None),
            P("in", out, None),
            P("in", out),
        ),
        out_specs=P("in", out, None, None, None),
        check_vma=False,
    )
```

profile of v0, /device:TPU:6, one launch (start us, length us, event | category | flops | bytes accessed | tf_op | source)
XLA Modules:
  0.0 124.3 jit_solution(2306164976651225926)
XLA Ops:
  0.0 1.1 broadcast_select_fusion.2
  1.2 1.3 %collective-permute-done = bf16[128,512]{1,0:T(8,128)(2,1)S(1)} collective-permute-done((bf16[128,512]{1,0:T(8,128)(2,1)S(1)}, bf16[128,512]{1,0:T(8,128)(2,1)S(1)}, u32[]{:S(2)}, u32[]{:S(2)}) %collective-permute-start) | collective-permute-done | bytes 131104 | tf_op jit(solution)/shard_map/ppermute | solution.py:163
  2.5 1.0 broadcast_select_fusion
  3.5 1.6 %collective-permute-start.14 = (bf16[128,512]{1,0:T(8,128)(2,1)S(1)}, bf16[128,512]{1,0:T(8,128)(2,1)S(1)}, u32[]{:S(2)}, u32[]{:S(2)}) collective-permute-start(bf16[128,512]{1,0:T(8,128)(2,1)S(1)} %broadcast_select_fusion), channel_id=1, source_target_pairs={{0,2},{2,4},{4,6},{6,0},{1,3},{3,5},{5,7},{7,1},{8,10},{10,12},{12... | collective-permute-start | bytes 393224 | tf_op jit(solution)/shard_map/ppermute | solution.py:99
  5.2 1.7 %collective-permute-start.13 = (bf16[128,512]{1,0:T(8,128)(2,1)S(1)}, bf16[128,512]{1,0:T(8,128)(2,1)S(1)}, u32[]{:S(2)}, u32[]{:S(2)}) collective-permute-start(bf16[128,512]{1,0:T(8,128)(2,1)S(1)} %broadcast_select_fusion), channel_id=1, source_target_pairs={{0,6},{2,0},{4,2},{6,4},{1,7},{3,1},{5,3},{7,5},{8,14},{10,8},{12,... | collective-permute-start | bytes 393224 | tf_op jit(solution)/shard_map/ppermute | solution.py:100
  6.8 1.0 bitcast_dynamic-update-slice_fusion.13
  7.8 5.9 %collective-permute-start.1 = (bf16[128,512]{1,0:T(8,128)(2,1)S(1)}, bf16[128,512]{1,0:T(8,128)(2,1)S(1)}, u32[]{:S(2)}, u32[]{:S(2)}) collective-permute-start(bf16[128,512]{1,0:T(8,128)(2,1)S(1)} %get-tuple-element.23), channel_id=1, source_target_pairs={{0,56},{8,0},{16,8},{24,16},{32,24},{40,32},{48,40},{56,48},{1,57}... | collective-permute-start | bytes 393224 | tf_op jit(solution)/shard_map/ppermute | solution.py:100
  13.8 1.9 %collective-permute-start.16 = (bf16[64,512]{1,0:T(8,128)(2,1)S(1)}, bf16[64,512]{1,0:T(8,128)(2,1)S(1)}, u32[]{:S(2)}, u32[]{:S(2)}) collective-permute-start(bf16[64,512]{1,0:T(8,128)(2,1)S(1)} %slice.53), channel_id=1, source_target_pairs={{0,6},{2,0},{4,2},{6,4},{1,7},{3,1},{5,3},{7,5},{8,14},{10,8},{12,... | collective-permute-start | bytes 196616 | tf_op jit(solution)/shard_map/ppermute | solution.py:107
  16.4 3.7 %collective-permute-start.2 = (bf16[128,512]{1,0:T(8,128)(2,1)S(1)}, bf16[128,512]{1,0:T(8,128)(2,1)S(1)}, u32[]{:S(2)}, u32[]{:S(2)}) collective-permute-start(bf16[128,512]{1,0:T(8,128)(2,1)S(1)} %collective-permute-done.1), channel_id=1, source_target_pairs={{0,56},{8,0},{16,8},{24,16},{32,24},{40,32},{48,40},{56,48},{1,57}... | collective-permute-start | bytes 393224 | tf_op jit(solution)/shard_map/ppermute | solution.py:100
  21.3 3.7 %collective-permute-start.17 = (bf16[4,128,512]{2,1,0:T(8,128)(2,1)S(1)}, bf16[4,128,512]{2,1,0:T(8,128)(2,1)S(1)}, u32[]{:S(2)}, u32[]{:S(2)}) collective-permute-start(bf16[4,128,512]{2,1,0:T(8,128)(2,1)S(1)} %pad_maximum_fusion.1), channel_id=1, source_target_pairs={{0,56},{8,0},{16,8},{24,16},{32,24},{40,32},{48,40},{56,48},{1,57}... | collective-permute-start | bytes 1572872 | tf_op jit(solution)/shard_map/ppermute | solution.py:100
  25.1 3.2 %collective-permute-start.3 = (bf16[128,512]{1,0:T(8,128)(2,1)S(1)}, bf16[128,512]{1,0:T(8,128)(2,1)S(1)}, u32[]{:S(2)}, u32[]{:S(2)}) collective-permute-start(bf16[128,512]{1,0:T(8,128)(2,1)S(1)} %collective-permute-done.2), channel_id=1, source_target_pairs={{0,56},{8,0},{16,8},{24,16},{32,24},{40,32},{48,40},{56,48},{1,57}... | collective-permute-start | bytes 393224 | tf_op jit(solution)/shard_map/ppermute | solution.py:100
  28.3 8.6 %collective-permute-done.3 = bf16[128,512]{1,0:T(8,128)(2,1)S(1)} collective-permute-done((bf16[128,512]{1,0:T(8,128)(2,1)S(1)}, bf16[128,512]{1,0:T(8,128)(2,1)S(1)}, u32[]{:S(2)}, u32[]{:S(2)}) %collective-permute-start.3) | collective-permute-done | bytes 131104 | tf_op jit(solution)/shard_map/ppermute | solution.py:100
  36.9 3.7 %collective-permute-start.8 = (bf16[64,512]{1,0:T(8,128)(2,1)S(1)}, bf16[64,512]{1,0:T(8,128)(2,1)S(1)}, u32[]{:S(2)}, u32[]{:S(2)}) collective-permute-start(bf16[64,512]{1,0:T(8,128)(2,1)S(1)} %slice.49), channel_id=1, source_target_pairs={{0,56},{8,0},{16,8},{24,16},{32,24},{40,32},{48,40},{56,48},{1,57}... | collective-permute-start | bytes 196616 | tf_op jit(solution)/shard_map/ppermute | solution.py:107
  40.8 1.8 %collective-permute-done.8 = bf16[64,512]{1,0:T(8,128)(2,1)S(1)} collective-permute-done((bf16[64,512]{1,0:T(8,128)(2,1)S(1)}, bf16[64,512]{1,0:T(8,128)(2,1)S(1)}, u32[]{:S(2)}, u32[]{:S(2)}) %collective-permute-start.8) | collective-permute-done | bytes 65568 | tf_op jit(solution)/shard_map/ppermute | solution.py:107
  42.5 3.7 %collective-permute-done.7 = bf16[64,512]{1,0:T(8,128)(2,1)S(1)} collective-permute-done((bf16[64,512]{1,0:T(8,128)(2,1)S(1)}, bf16[64,512]{1,0:T(8,128)(2,1)S(1)}, u32[]{:S(2)}, u32[]{:S(2)}) %collective-permute-start.7) | collective-permute-done | bytes 65568 | tf_op jit(solution)/shard_map/ppermute | solution.py:106
  46.5 2.3 %collective-permute-start.9 = (bf16[8,128,512]{2,1,0:T(8,128)(2,1)S(1)}, bf16[8,128,512]{2,1,0:T(8,128)(2,1)S(1)}, u32[]{:S(2)}, u32[]{:S(2)}) collective-permute-start(bf16[8,128,512]{2,1,0:T(8,128)(2,1)S(1)} %bitcast_dynamic-update-slice_fusion.7), channel_id=1, source_target_pairs={{0,6},{2,0},{4,2},{6,4},{1,7},{3,1},{5,3},{7,5},{8,14},{10,8},{12,... | collective-permute-start | bytes 3145736 | tf_op jit(solution)/shard_map/ppermute | solution.py:100
  49.4 1.5 %collective-permute-start.26 = (bf16[2048,256]{1,0:T(8,128)(2,1)S(1)}, bf16[2048,256]{1,0:T(8,128)(2,1)S(1)}, u32[]{:S(2)}, u32[]{:S(2)}) collective-permute-start(bf16[2048,256]{1,0:T(8,128)(2,1)S(1)} %copy-done), channel_id=1, source_target_pairs={{0,192},{64,0},{128,64},{192,128},{1,193},{65,1},{129,65},{193,129... | collective-permute-start | bytes 3145736 | tf_op jit(solution)/shard_map/ppermute | solution.py:121
  50.9 4.9 %collective-permute-done.18 = bf16[4,128,512]{2,1,0:T(8,128)(2,1)S(1)} collective-permute-done((bf16[4,128,512]{2,1,0:T(8,128)(2,1)S(1)}, bf16[4,128,512]{2,1,0:T(8,128)(2,1)S(1)}, u32[]{:S(2)}, u32[]{:S(2)}) %collective-permute-start.18) | collective-permute-done | bytes 524320 | tf_op jit(solution)/shard_map/ppermute | solution.py:100
  55.8 10.4 %collective-permute-done.21 = bf16[4,128,512]{2,1,0:T(8,128)(2,1)S(1)} collective-permute-done((bf16[4,128,512]{2,1,0:T(8,128)(2,1)S(1)}, bf16[4,128,512]{2,1,0:T(8,128)(2,1)S(1)}, u32[]{:S(2)}, u32[]{:S(2)}) %collective-permute-start.21) | collective-permute-done | bytes 524320 | tf_op jit(solution)/shard_map/ppermute | solution.py:99
  66.5 1.9 %collective-permute-done.9 = bf16[8,128,512]{2,1,0:T(8,128)(2,1)S(1)} collective-permute-done((bf16[8,128,512]{2,1,0:T(8,128)(2,1)S(1)}, bf16[8,128,512]{2,1,0:T(8,128)(2,1)S(1)}, u32[]{:S(2)}, u32[]{:S(2)}) %collective-permute-start.9) | collective-permute-done | bytes 1048608 | tf_op jit(solution)/shard_map/ppermute | solution.py:100
  68.4 1.7 %collective-permute-start.22 = (bf16[4,128,512]{2,1,0:T(8,128)(2,1)S(1)}, bf16[4,128,512]{2,1,0:T(8,128)(2,1)S(1)}, u32[]{:S(2)}, u32[]{:S(2)}) collective-permute-start(bf16[4,128,512]{2,1,0:T(8,128)(2,1)S(1)} %collective-permute-done.21), channel_id=1, source_target_pairs={{0,8},{8,16},{16,24},{24,32},{32,40},{40,48},{48,56},{56,0},{1,9},... | collective-permute-start | bytes 1572872 | tf_op jit(solution)/shard_map/ppermute | solution.py:99
  71.8 3.0 %collective-permute-start.12 = (bf16[4,128,512]{2,1,0:T(8,128)(2,1)S(1)}, bf16[4,128,512]{2,1,0:T(8,128)(2,1)S(1)}, u32[]{:S(2)}, u32[]{:S(2)}) collective-permute-start(bf16[4,128,512]{2,1,0:T(8,128)(2,1)S(1)} %slice.51), channel_id=1, source_target_pairs={{0,6},{2,0},{4,2},{6,4},{1,7},{3,1},{5,3},{7,5},{8,14},{10,8},{12,... | collective-permute-start | bytes 1572872 | tf_op jit(solution)/shard_map/ppermute | solution.py:107
  77.2 1.5 %collective-permute-start.28 = (bf16[1024,256]{1,0:T(8,128)(2,1)S(1)}, bf16[1024,256]{1,0:T(8,128)(2,1)S(1)}, u32[]{:S(2)}, u32[]{:S(2)}) collective-permute-start(bf16[1024,256]{1,0:T(8,128)(2,1)S(1)} %slice.57), channel_id=1, source_target_pairs={{0,192},{64,0},{128,64},{192,128},{1,193},{65,1},{129,65},{193,129... | collective-permute-start | bytes 1572872 | tf_op jit(solution)/shard_map/ppermute | solution.py:131
  81.7 1.2 collective-permute-start.23
  82.9 2.4 %collective-permute-done.11 = bf16[4,128,512]{2,1,0:T(8,128)(2,1)S(1)} collective-permute-done((bf16[4,128,512]{2,1,0:T(8,128)(2,1)S(1)}, bf16[4,128,512]{2,1,0:T(8,128)(2,1)S(1)}, u32[]{:S(2)}, u32[]{:S(2)}) %collective-permute-start.11) | collective-permute-done | bytes 524320 | tf_op jit(solution)/shard_map/ppermute | solution.py:106
  86.0 3.3 %collective-permute-done.23 = bf16[2,128,512]{2,1,0:T(8,128)(2,1)S(1)} collective-permute-done((bf16[2,128,512]{2,1,0:T(8,128)(2,1)S(1)}, bf16[2,128,512]{2,1,0:T(8,128)(2,1)S(1)}, u32[]{:S(2)}, u32[]{:S(2)}) %collective-permute-start.23) | collective-permute-done | bytes 262176 | tf_op jit(solution)/shard_map/ppermute | solution.py:106
  90.9 2.4 %copy.6 = bf16[8,4,128,512]{3,2,1,0:T(8,128)(2,1)} copy(bf16[8,4,128,512]{3,2,0,1:T(8,128)(2,1)S(1)} %pad_maximum_fusion) | data formatting | bytes 8388608 | tf_op jit(solution)/shard_map/stack | solution.py:168
  98.1 1.0 copy-done.2
  99.1 1.0 copy-done.4
  100.2 6.1 %shard_map.55 = f32[4,128,128]{2,1,0:T(8,128)S(1)} custom-call(s32[4]{0:T(128)S(1)} %and_select_fusion.2.rows_ref, s32[4]{0:T(128)S(1)} %clamp_bitcast_fusion.cols_ref, s32[4]{0:T(128)S(1)} %and_convert_fusion.1.use_ref, s32[5]{0:T(128)S(1)} %and_select_fusion.starts_ref, s32[2]{0:T(128)S(1)} %pad_add_fusion.place_ref, ...), custom_call_target="tpu_custom_call" | custom-call | flops 1073741824 | bytes 17039360 | tf_op jit(solution)/shard_map/pallas_call | solution.py:78
  106.3 3.9 %collective-permute-done.30.rest_1_ = bf16[32,128,512]{2,1,0:T(8,128)(2,1)} collective-permute-done((bf16[32,128,512]{2,1,0:T(8,128)(2,1)}, bf16[32,128,512]{2,1,0:T(8,128)(2,1)}, u32[]{:S(2)}, u32[]{:S(2)}) %collective-permute-start.30) | collective-permute-done | bytes 4194336 | tf_op jit(solution)/shard_map/ppermute | solution.py:179
  110.2 13.4 %shard_map.56 = f32[4,128,128]{2,1,0:T(8,128)S(1)} custom-call(s32[4]{0:T(128)S(1)} %and_select_fusion.2.rows_ref, s32[4]{0:T(128)S(1)} %clamp_bitcast_fusion.cols_ref, s32[4]{0:T(128)S(1)} %get-tuple-element.19.use_ref, s32[5]{0:T(128)S(1)} %and_select_fusion.starts_ref, s32[2]{0:T(128)S(1)} %pad_add_fusion.place_ref, ...), custom_call_target="tpu_custom_call" | custom-call | flops 1073741824 | bytes 17039360 | tf_op jit(solution)/shard_map/pallas_call | solution.py:78
  (87 shorter events, 17.3 us)
Async XLA Ops:
  0.0 48.9 %copy-start = (bf16[2048,256]{1,0:T(8,128)(2,1)S(1)}, bf16[2048,256]{1,0:T(8,128)(2,1)}, u32[]{:S(2)}) copy-start(bf16[2048,256]{1,0:T(8,128)(2,1)} %param.6) | copy-start | bytes 3145732
  1.1 1.4 %collective-permute-start = (bf16[128,512]{1,0:T(8,128)(2,1)S(1)}, bf16[128,512]{1,0:T(8,128)(2,1)S(1)}, u32[]{:S(2)}, u32[]{:S(2)}) collective-permute-start(bf16[128,512]{1,0:T(8,128)(2,1)S(1)} %broadcast_select_fusion.2), channel_id=1, source_target_pairs={{0,1},{1,0},{2,3},{3,2},{4,5},{5,4},{6,7},{7,6},{8,9},{9,8},{10,11... | collective-permute-start | bytes 393224 | tf_op jit(solution)/shard_map/ppermute | solution.py:163
  3.5 12.2 %collective-permute-start.14 = (bf16[128,512]{1,0:T(8,128)(2,1)S(1)}, bf16[128,512]{1,0:T(8,128)(2,1)S(1)}, u32[]{:S(2)}, u32[]{:S(2)}) collective-permute-start(bf16[128,512]{1,0:T(8,128)(2,1)S(1)} %broadcast_select_fusion), channel_id=1, source_target_pairs={{0,2},{2,4},{4,6},{6,0},{1,3},{3,5},{5,7},{7,1},{8,10},{10,12},{12... | collective-permute-start | bytes 393224 | tf_op jit(solution)/shard_map/ppermute | solution.py:99
  5.2 8.6 %collective-permute-start.13 = (bf16[128,512]{1,0:T(8,128)(2,1)S(1)}, bf16[128,512]{1,0:T(8,128)(2,1)S(1)}, u32[]{:S(2)}, u32[]{:S(2)}) collective-permute-start(bf16[128,512]{1,0:T(8,128)(2,1)S(1)} %broadcast_select_fusion), channel_id=1, source_target_pairs={{0,6},{2,0},{4,2},{6,4},{1,7},{3,1},{5,3},{7,5},{8,14},{10,8},{12,... | collective-permute-start | bytes 393224 | tf_op jit(solution)/shard_map/ppermute | solution.py:100
  7.8 8.6 %collective-permute-start.1 = (bf16[128,512]{1,0:T(8,128)(2,1)S(1)}, bf16[128,512]{1,0:T(8,128)(2,1)S(1)}, u32[]{:S(2)}, u32[]{:S(2)}) collective-permute-start(bf16[128,512]{1,0:T(8,128)(2,1)S(1)} %get-tuple-element.23), channel_id=1, source_target_pairs={{0,56},{8,0},{16,8},{24,16},{32,24},{40,32},{48,40},{56,48},{1,57}... | collective-permute-start | bytes 393224 | tf_op jit(solution)/shard_map/ppermute | solution.py:100
  13.8 6.4 %collective-permute-start.4 = (bf16[128,512]{1,0:T(8,128)(2,1)S(1)}, bf16[128,512]{1,0:T(8,128)(2,1)S(1)}, u32[]{:S(2)}, u32[]{:S(2)}) collective-permute-start(bf16[128,512]{1,0:T(8,128)(2,1)S(1)} %get-tuple-element.23), channel_id=1, source_target_pairs={{0,8},{8,16},{16,24},{24,32},{32,40},{40,48},{48,56},{56,0},{1,9},... | collective-permute-start | bytes 393224 | tf_op jit(solution)/shard_map/ppermute | solution.py:99
  13.8 6.5 %collective-permute-start.16 = (bf16[64,512]{1,0:T(8,128)(2,1)S(1)}, bf16[64,512]{1,0:T(8,128)(2,1)S(1)}, u32[]{:S(2)}, u32[]{:S(2)}) collective-permute-start(bf16[64,512]{1,0:T(8,128)(2,1)S(1)} %slice.53), channel_id=1, source_target_pairs={{0,6},{2,0},{4,2},{6,4},{1,7},{3,1},{5,3},{7,5},{8,14},{10,8},{12,... | collective-permute-start | bytes 196616 | tf_op jit(solution)/shard_map/ppermute | solution.py:107
  15.7 5.6 %collective-permute-start.15 = (bf16[64,512]{1,0:T(8,128)(2,1)S(1)}, bf16[64,512]{1,0:T(8,128)(2,1)S(1)}, u32[]{:S(2)}, u32[]{:S(2)}) collective-permute-start(bf16[64,512]{1,0:T(8,128)(2,1)S(1)} %slice.52), channel_id=1, source_target_pairs={{0,2},{2,4},{4,6},{6,0},{1,3},{3,5},{5,7},{7,1},{8,10},{10,12},{12... | collective-permute-start | bytes 196616 | tf_op jit(solution)/shard_map/ppermute | solution.py:106
  16.4 8.6 %collective-permute-start.2 = (bf16[128,512]{1,0:T(8,128)(2,1)S(1)}, bf16[128,512]{1,0:T(8,128)(2,1)S(1)}, u32[]{:S(2)}, u32[]{:S(2)}) collective-permute-start(bf16[128,512]{1,0:T(8,128)(2,1)S(1)} %collective-permute-done.1), channel_id=1, source_target_pairs={{0,56},{8,0},{16,8},{24,16},{32,24},{40,32},{48,40},{56,48},{1,57}... | collective-permute-start | bytes 393224 | tf_op jit(solution)/shard_map/ppermute | solution.py:100
  20.2 8.1 %collective-permute-start.5 = (bf16[128,512]{1,0:T(8,128)(2,1)S(1)}, bf16[128,512]{1,0:T(8,128)(2,1)S(1)}, u32[]{:S(2)}, u32[]{:S(2)}) collective-permute-start(bf16[128,512]{1,0:T(8,128)(2,1)S(1)} %collective-permute-done.4), channel_id=1, source_target_pairs={{0,8},{8,16},{16,24},{24,32},{32,40},{40,48},{48,56},{56,0},{1,9},... | collective-permute-start | bytes 393224 | tf_op jit(solution)/shard_map/ppermute | solution.py:99
  21.3 24.9 %collective-permute-start.17 = (bf16[4,128,512]{2,1,0:T(8,128)(2,1)S(1)}, bf16[4,128,512]{2,1,0:T(8,128)(2,1)S(1)}, u32[]{:S(2)}, u32[]{:S(2)}) collective-permute-start(bf16[4,128,512]{2,1,0:T(8,128)(2,1)S(1)} %pad_maximum_fusion.1), channel_id=1, source_target_pairs={{0,56},{8,0},{16,8},{24,16},{32,24},{40,32},{48,40},{56,48},{1,57}... | collective-permute-start | bytes 1572872 | tf_op jit(solution)/shard_map/ppermute | solution.py:100
  25.0 24.3 %collective-permute-start.20 = (bf16[4,128,512]{2,1,0:T(8,128)(2,1)S(1)}, bf16[4,128,512]{2,1,0:T(8,128)(2,1)S(1)}, u32[]{:S(2)}, u32[]{:S(2)}) collective-permute-start(bf16[4,128,512]{2,1,0:T(8,128)(2,1)S(1)} %pad_maximum_fusion.1), channel_id=1, source_target_pairs={{0,8},{8,16},{16,24},{24,32},{32,40},{40,48},{48,56},{56,0},{1,9},... | collective-permute-start | bytes 1572872 | tf_op jit(solution)/shard_map/ppermute | solution.py:99
  25.1 11.9 %collective-permute-start.3 = (bf16[128,512]{1,0:T(8,128)(2,1)S(1)}, bf16[128,512]{1,0:T(8,128)(2,1)S(1)}, u32[]{:S(2)}, u32[]{:S(2)}) collective-permute-start(bf16[128,512]{1,0:T(8,128)(2,1)S(1)} %collective-permute-done.2), channel_id=1, source_target_pairs={{0,56},{8,0},{16,8},{24,16},{32,24},{40,32},{48,40},{56,48},{1,57}... | collective-permute-start | bytes 393224 | tf_op jit(solution)/shard_map/ppermute | solution.py:100
  28.3 12.3 %collective-permute-start.6 = (bf16[128,512]{1,0:T(8,128)(2,1)S(1)}, bf16[128,512]{1,0:T(8,128)(2,1)S(1)}, u32[]{:S(2)}, u32[]{:S(2)}) collective-permute-start(bf16[128,512]{1,0:T(8,128)(2,1)S(1)} %collective-permute-done.5), channel_id=1, source_target_pairs={{0,8},{8,16},{16,24},{24,32},{32,40},{40,48},{48,56},{56,0},{1,9},... | collective-permute-start | bytes 393224 | tf_op jit(solution)/shard_map/ppermute | solution.py:99
  36.9 5.6 %collective-permute-start.8 = (bf16[64,512]{1,0:T(8,128)(2,1)S(1)}, bf16[64,512]{1,0:T(8,128)(2,1)S(1)}, u32[]{:S(2)}, u32[]{:S(2)}) collective-permute-start(bf16[64,512]{1,0:T(8,128)(2,1)S(1)} %slice.49), channel_id=1, source_target_pairs={{0,56},{8,0},{16,8},{24,16},{32,24},{40,32},{48,40},{56,48},{1,57}... | collective-permute-start | bytes 196616 | tf_op jit(solution)/shard_map/ppermute | solution.py:107
  40.6 5.6 %collective-permute-start.7 = (bf16[64,512]{1,0:T(8,128)(2,1)S(1)}, bf16[64,512]{1,0:T(8,128)(2,1)S(1)}, u32[]{:S(2)}, u32[]{:S(2)}) collective-permute-start(bf16[64,512]{1,0:T(8,128)(2,1)S(1)} %slice.48), channel_id=1, source_target_pairs={{0,8},{8,16},{16,24},{24,32},{32,40},{40,48},{48,56},{56,0},{1,9},... | collective-permute-start | bytes 196616 | tf_op jit(solution)/shard_map/ppermute | solution.py:106
  46.3 9.5 %collective-permute-start.18 = (bf16[4,128,512]{2,1,0:T(8,128)(2,1)S(1)}, bf16[4,128,512]{2,1,0:T(8,128)(2,1)S(1)}, u32[]{:S(2)}, u32[]{:S(2)}) collective-permute-start(bf16[4,128,512]{2,1,0:T(8,128)(2,1)S(1)} %collective-permute-done.17), channel_id=1, source_target_pairs={{0,56},{8,0},{16,8},{24,16},{32,24},{40,32},{48,40},{56,48},{1,57}... | collective-permute-start | bytes 1572872 | tf_op jit(solution)/shard_map/ppermute | solution.py:100
  46.5 21.9 %collective-permute-start.9 = (bf16[8,128,512]{2,1,0:T(8,128)(2,1)S(1)}, bf16[8,128,512]{2,1,0:T(8,128)(2,1)S(1)}, u32[]{:S(2)}, u32[]{:S(2)}) collective-permute-start(bf16[8,128,512]{2,1,0:T(8,128)(2,1)S(1)} %bitcast_dynamic-update-slice_fusion.7), channel_id=1, source_target_pairs={{0,6},{2,0},{4,2},{6,4},{1,7},{3,1},{5,3},{7,5},{8,14},{10,8},{12,... | collective-permute-start | bytes 3145736 | tf_op jit(solution)/shard_map/ppermute | solution.py:100
  48.9 22.9 %collective-permute-start.10 = (bf16[8,128,512]{2,1,0:T(8,128)(2,1)S(1)}, bf16[8,128,512]{2,1,0:T(8,128)(2,1)S(1)}, u32[]{:S(2)}, u32[]{:S(2)}) collective-permute-start(bf16[8,128,512]{2,1,0:T(8,128)(2,1)S(1)} %bitcast_dynamic-update-slice_fusion.7), channel_id=1, source_target_pairs={{0,2},{2,4},{4,6},{6,0},{1,3},{3,5},{5,7},{7,1},{8,10},{10,12},{12... | collective-permute-start | bytes 3145736 | tf_op jit(solution)/shard_map/ppermute | solution.py:99
  48.9 26.0 %collective-permute-start.25 = (bf16[2048,256]{1,0:T(8,128)(2,1)S(1)}, bf16[2048,256]{1,0:T(8,128)(2,1)S(1)}, u32[]{:S(2)}, u32[]{:S(2)}) collective-permute-start(bf16[2048,256]{1,0:T(8,128)(2,1)S(1)} %copy-done), channel_id=1, source_target_pairs={{0,64},{64,128},{128,192},{192,0},{1,65},{65,129},{129,193},{193,1... | collective-permute-start | bytes 3145736 | tf_op jit(solution)/shard_map/ppermute | solution.py:120
  49.4 26.4 %collective-permute-start.26 = (bf16[2048,256]{1,0:T(8,128)(2,1)S(1)}, bf16[2048,256]{1,0:T(8,128)(2,1)S(1)}, u32[]{:S(2)}, u32[]{:S(2)}) collective-permute-start(bf16[2048,256]{1,0:T(8,128)(2,1)S(1)} %copy-done), channel_id=1, source_target_pairs={{0,192},{64,0},{128,64},{192,128},{1,193},{65,1},{129,65},{193,129... | collective-permute-start | bytes 3145736 | tf_op jit(solution)/shard_map/ppermute | solution.py:121
  55.8 10.4 %collective-permute-start.21 = (bf16[4,128,512]{2,1,0:T(8,128)(2,1)S(1)}, bf16[4,128,512]{2,1,0:T(8,128)(2,1)S(1)}, u32[]{:S(2)}, u32[]{:S(2)}) collective-permute-start(bf16[4,128,512]{2,1,0:T(8,128)(2,1)S(1)} %collective-permute-done.20), channel_id=1, source_target_pairs={{0,8},{8,16},{16,24},{24,32},{32,40},{40,48},{48,56},{56,0},{1,9},... | collective-permute-start | bytes 1572872 | tf_op jit(solution)/shard_map/ppermute | solution.py:99
  66.2 11.1 %collective-permute-start.19 = (bf16[4,128,512]{2,1,0:T(8,128)(2,1)S(1)}, bf16[4,128,512]{2,1,0:T(8,128)(2,1)S(1)}, u32[]{:S(2)}, u32[]{:S(2)}) collective-permute-start(bf16[4,128,512]{2,1,0:T(8,128)(2,1)S(1)} %collective-permute-done.18), channel_id=1, source_target_pairs={{0,56},{8,0},{16,8},{24,16},{32,24},{40,32},{48,40},{56,48},{1,57}... | collective-permute-start | bytes 1572872 | tf_op jit(solution)/shard_map/ppermute | solution.py:100
  68.4 11.1 %collective-permute-start.22 = (bf16[4,128,512]{2,1,0:T(8,128)(2,1)S(1)}, bf16[4,128,512]{2,1,0:T(8,128)(2,1)S(1)}, u32[]{:S(2)}, u32[]{:S(2)}) collective-permute-start(bf16[4,128,512]{2,1,0:T(8,128)(2,1)S(1)} %collective-permute-done.21), channel_id=1, source_target_pairs={{0,8},{8,16},{16,24},{24,32},{32,40},{40,48},{48,56},{56,0},{1,9},... | collective-permute-start | bytes 1572872 | tf_op jit(solution)/shard_map/ppermute | solution.py:99
  71.8 9.9 %collective-permute-start.12 = (bf16[4,128,512]{2,1,0:T(8,128)(2,1)S(1)}, bf16[4,128,512]{2,1,0:T(8,128)(2,1)S(1)}, u32[]{:S(2)}, u32[]{:S(2)}) collective-permute-start(bf16[4,128,512]{2,1,0:T(8,128)(2,1)S(1)} %slice.51), channel_id=1, source_target_pairs={{0,6},{2,0},{4,2},{6,4},{1,7},{3,1},{5,3},{7,5},{8,14},{10,8},{12,... | collective-permute-start | bytes 1572872 | tf_op jit(solution)/shard_map/ppermute | solution.py:107
  74.9 10.5 %collective-permute-start.11 = (bf16[4,128,512]{2,1,0:T(8,128)(2,1)S(1)}, bf16[4,128,512]{2,1,0:T(8,128)(2,1)S(1)}, u32[]{:S(2)}, u32[]{:S(2)}) collective-permute-start(bf16[4,128,512]{2,1,0:T(8,128)(2,1)S(1)} %slice.50), channel_id=1, source_target_pairs={{0,2},{2,4},{4,6},{6,0},{1,3},{3,5},{5,7},{7,1},{8,10},{10,12},{12... | collective-permute-start | bytes 1572872 | tf_op jit(solution)/shard_map/ppermute | solution.py:106
  75.8 19.2 %collective-permute-start.27 = (bf16[1024,256]{1,0:T(8,128)(2,1)S(1)}, bf16[1024,256]{1,0:T(8,128)(2,1)S(1)}, u32[]{:S(2)}, u32[]{:S(2)}) collective-permute-start(bf16[1024,256]{1,0:T(8,128)(2,1)S(1)} %slice.56), channel_id=1, source_target_pairs={{0,64},{64,128},{128,192},{192,0},{1,65},{65,129},{129,193},{193,1... | collective-permute-start | bytes 1572872 | tf_op jit(solution)/shard_map/ppermute | solution.py:130
  77.2 18.6 %collective-permute-start.28 = (bf16[1024,256]{1,0:T(8,128)(2,1)S(1)}, bf16[1024,256]{1,0:T(8,128)(2,1)S(1)}, u32[]{:S(2)}, u32[]{:S(2)}) collective-permute-start(bf16[1024,256]{1,0:T(8,128)(2,1)S(1)} %slice.57), channel_id=1, source_target_pairs={{0,192},{64,0},{128,64},{192,128},{1,193},{65,1},{129,65},{193,129... | collective-permute-start | bytes 1572872 | tf_op jit(solution)/shard_map/ppermute | solution.py:131
  79.5 6.5 %collective-permute-start.24 = (bf16[2,128,512]{2,1,0:T(8,128)(2,1)S(1)}, bf16[2,128,512]{2,1,0:T(8,128)(2,1)S(1)}, u32[]{:S(2)}, u32[]{:S(2)}) collective-permute-start(bf16[2,128,512]{2,1,0:T(8,128)(2,1)S(1)} %slice.55), channel_id=1, source_target_pairs={{0,56},{8,0},{16,8},{24,16},{32,24},{40,32},{48,40},{56,48},{1,57}... | collective-permute-start | bytes 786440 | tf_op jit(solution)/shard_map/ppermute | solution.py:107
  81.7 7.6 %collective-permute-start.23 = (bf16[2,128,512]{2,1,0:T(8,128)(2,1)S(1)}, bf16[2,128,512]{2,1,0:T(8,128)(2,1)S(1)}, u32[]{:S(2)}, u32[]{:S(2)}) collective-permute-start(bf16[2,128,512]{2,1,0:T(8,128)(2,1)S(1)} %slice.54), channel_id=1, source_target_pairs={{0,8},{8,16},{16,24},{24,32},{32,40},{40,48},{48,56},{56,0},{1,9},... | collective-permute-start | bytes 786440 | tf_op jit(solution)/shard_map/ppermute | solution.py:106
  96.7 9.6 %collective-permute-start.29 = (bf16[32,128,512]{2,1,0:T(8,128)(2,1)}, bf16[32,128,512]{2,1,0:T(8,128)(2,1)}, u32[]{:S(2)}, u32[]{:S(2)}) collective-permute-start(bf16[32,128,512]{2,1,0:T(8,128)(2,1)} %bitcast.22.rest_0_), channel_id=1, source_target_pairs={{0,1},{1,0},{2,3},{3,2},{4,5},{5,4},{6,7},{7,6},{8,9},{9,8},{10,11... | collective-permute-start | bytes 12582920 | tf_op jit(solution)/shard_map/ppermute | solution.py:178
  96.7 13.5 %collective-permute-start.30 = (bf16[32,128,512]{2,1,0:T(8,128)(2,1)}, bf16[32,128,512]{2,1,0:T(8,128)(2,1)}, u32[]{:S(2)}, u32[]{:S(2)}) collective-permute-start(bf16[32,128,512]{2,1,0:T(8,128)(2,1)} %bitcast.35.rest_1_), channel_id=1, source_target_pairs={{0,1},{1,0},{2,3},{3,2},{4,5},{5,4},{6,7},{7,6},{8,9},{9,8},{10,11... | collective-permute-start | bytes 12582920 | tf_op jit(solution)/shard_map/ppermute | solution.py:179
  (6 other events, 17.9 us)
where the time goes:
time: 125 us; the launch traced here: 124 us
  waiting for transfers between devices  45.5 us (36%)
  starting transfers between devices  40.5 us (32%)
  Pallas kernels  19.5 us (16%)
  local copies, waits for them, and re-layouts  11.4 us (9%)
  other arithmetic  6.39 us (5%)
    ppermute x8, starting transfers between devices, relative_gather(): from_right = lax.ppermute(from_right, axis, left)  21.2 us
    pallas_call x2, Pallas kernels, block_products(): pl.pallas_call(functools.partial(block_kernel, n_grad, ny), out_shape=jax...  19.5 us
    ppermute x8, waiting for transfers between devices, relative_gather(): from_right = lax.ppermute(from_right, axis, left)  15.8 us
    ppermute x8, waiting for transfers between devices, relative_gather(): from_left = lax.ppermute(from_left, axis, right)  11.9 us
    ppermute x4, waiting for transfers between devices, relative_gather(): near_a = lax.ppermute(from_left[:half], axis, right)  10.3 us
    ppermute x4, starting transfers between devices, relative_gather(): near_b = lax.ppermute(from_right[half:], axis, left)  9.41 us
    unnamed x24, local copies, waits for them, and re-layouts  7.88 us
    ppermute x1, waiting for transfers between devices, on_device(): trail_other = lax.ppermute(trail_all, 'core', swap)  3.86 us
  transfers between devices with their start and end apart: 31, of which 15 were waited for; matrix products, arithmetic and copies ran while one was open for 9% of the time, Pallas kernels for 5%

commit v1 on v0

--- a/solution.py
+++ b/solution.py
@@ -9,81 +9,107 @@
 
 BLK = 128
 MAXB = 4
+GROUP = 4
 
 
 def block_kernel(n_grad, ny, rows_ref, cols_ref, use_ref, starts_ref, place_ref, *rest):
     first_hbm, second_hbm = rest[0], rest[1]
     grad_hbm = rest[2:2 + n_grad]
-    out_ref, a_v, g_v, sems = rest[2 + n_grad:]
-    chunks, _, tok, _ = a_v.shape[1:]
-
-    copies = []
+    out_ref, a_v, g_v, act_sems, grad_sems = rest[2 + n_grad:]
+    chunks = a_v.shape[0]
+    nz = chunks // ny
+    z_me, y_me = place_ref[0], place_ref[1]
+    any_use = use_ref[0] + use_ref[1] + use_ref[2] + use_ref[3] > 0
+
+    act_copies = []
     for s in range(MAXB):
         r = pl.multiple_of(rows_ref[s] * BLK, BLK)
-        c = pl.multiple_of(cols_ref[s] * BLK, BLK)
+        lanes = pl.ds(s * BLK, BLK)
         slot = [
-            pltpu.make_async_copy(first_hbm.at[:, :, pl.ds(r, BLK)], a_v.at[s, :, 0], sems.at[s, 0]),
-            pltpu.make_async_copy(second_hbm.at[:, :, pl.ds(r, BLK)], a_v.at[s, :, 1], sems.at[s, 1]),
+            pltpu.make_async_copy(
+                first_hbm.at[:, :, pl.ds(r, BLK)], a_v.at[:, 0, :, lanes], act_sems.at[s, 0]
+            ),
+            pltpu.make_async_copy(
+                second_hbm.at[:, :, pl.ds(r, BLK)], a_v.at[:, 1, :, lanes], act_sems.at[s, 1]
+            ),
         ]
-        for p, piece in enumerate(grad_hbm):
-            slot.append(
-                pltpu.make_async_copy(
-                    piece.at[:, :, :, pl.ds(c, BLK)],
-                    g_v.at[s, pl.ds(starts_ref[p], piece.shape[0])],
-                    sems.at[s, p + 2],
-                )
-            )
 
         @pl.when(use_ref[s] == 1)
         def _(slot=slot):
             for cp in slot:
                 cp.start()
 
-        copies.append(slot)
-
-    z_me, y_me = place_ref[0], place_ref[1]
-    nz = chunks // ny
+        act_copies.append(slot)
+
+    grad_copies = []
+    for p, piece in enumerate(grad_hbm):
+        for j in range(piece.shape[0]):
+            q = starts_ref[p] + j
+            k = ((q // ny - z_me + nz) % nz) * ny + (q % ny - y_me + ny) % ny
+            grad_copies.append(
+                pltpu.make_async_copy(piece.at[j], g_v.at[k], grad_sems.at[len(grad_copies)])
+            )
+
+    @pl.when(any_use)
+    def _():
+        for cp in grad_copies:
+            cp.start()
+
     for s in range(MAXB):
-
-        @pl.when(use_ref[s] == 0)
-        def _(s=s):
-            out_ref[s] = jnp.zeros((BLK, BLK), jnp.float32)
 
         @pl.when(use_ref[s] == 1)
         def _(s=s):
-            for cp in copies[s]:
+            for cp in act_copies[s]:
                 cp.wait()
 
-            def body(k, acc):
-                pair = ((z_me + k // ny) % nz) * ny + (y_me + k % ny) % ny
-                a = a_v[s, k].reshape(2 * tok, BLK)
-                g = g_v[s, pair].reshape(2 * tok, BLK)
-                return acc + lax.dot_general(
-                    a, g, (((0,), (0,)), ((), ())), preferred_element_type=jnp.float32
-                )
-
-            out_ref[s] = lax.fori_loop(
-                0, chunks, body, jnp.zeros((BLK, BLK), jnp.float32), unroll=2
+    @pl.when(jnp.logical_not(any_use))
+    def _():
+        out_ref[...] = jnp.zeros(out_ref.shape, jnp.float32)
+
+    @pl.when(any_use)
+    def _():
+        for cp in grad_copies:
+            cp.wait()
+        step = GROUP
+        rows = step * a_v.shape[1] * a_v.shape[2]
+
+        def body(kb, acc):
+            k0 = pl.multiple_of(kb * step, step)
+            a = a_v[pl.ds(k0, step)].reshape(rows, a_v.shape[3])
+            g = g_v[pl.ds(k0, step)].reshape(rows, g_v.shape[3])
+            return acc + lax.dot_general(
+                a, g, (((0,), (0,)), ((), ())), preferred_element_type=jnp.float32
             )
+
+        acc = lax.fori_loop(
+            0, chunks // step, body, jnp.zeros((a_v.shape[3], g_v.shape[3]), jnp.float32)
+        )
+        for s in range(MAXB):
+            blk = acc[s * BLK:(s + 1) * BLK]
+            pick = jnp.where(cols_ref[s] == 0, blk[:, :BLK], blk[:, BLK:2 * BLK])
+            out_ref[s] = jnp.where(use_ref[s] == 1, pick, jnp.zeros_like(pick))
 
 
 def block_products(first, second, grad_pieces, starts, place, local_rows, local_cols, use, ny):
     chunks, tok, width = first.shape
     n_grad = len(grad_pieces)
+    n_pairs = sum(g.shape[0] for g in grad_pieces)
+    cols = grad_pieces[0].shape[3]
     smem = pl.BlockSpec(memory_space=pltpu.SMEM)
     hbm = pl.BlockSpec(memory_space=pl.ANY)
     tokens = 2 * chunks * tok
-    flops = 2 * MAXB * tokens * BLK * BLK
-    moved = 2 * MAXB * tokens * BLK * 2 + MAXB * BLK * BLK * 4
+    flops = 2 * tokens * MAXB * BLK * cols
+    moved = MAXB * tokens * BLK * 2 + tokens * cols * 2 + MAXB * BLK * BLK * 4
     return pl.pallas_call(
         functools.partial(block_kernel, n_grad, ny),
         out_shape=jax.ShapeDtypeStruct((MAXB, BLK, BLK), jnp.float32),
         in_specs=[smem] * 5 + [hbm] * (2 + n_grad),
         out_specs=pl.BlockSpec(memory_space=pltpu.VMEM),
         scratch_shapes=[
-            pltpu.VMEM((MAXB, chunks, 2, tok, BLK), jnp.bfloat16),
-            pltpu.VMEM((MAXB, chunks, 2, tok, BLK), jnp.bfloat16),
-            pltpu.SemaphoreType.DMA((MAXB, 2 + n_grad)),
+            pltpu.VMEM((chunks, 2, tok, MAXB * BLK), jnp.bfloat16),
+            pltpu.VMEM((chunks, 2, tok, cols), jnp.bfloat16),
+            pltpu.SemaphoreType.DMA((MAXB, 2)),
+            pltpu.SemaphoreType.DMA((n_pairs,)),
         ],
         compiler_params=pltpu.CompilerParams(vmem_limit_bytes=48 * 1024 * 1024),
         cost_estimate=pl.CostEstimate(flops=flops, bytes_accessed=moved, transcendentals=0),

time: 125 us -> 127 us (1.016)
  the two profiles are of different devices: /device:TPU:6 before, /device:TPU:25 now
where the time goes in v1:
time: 127 us; the launch traced here: 124 us
  waiting for transfers between devices  47.7 us (38%)
  starting transfers between devices  44.4 us (35%)
  Pallas kernels  13.4 us (11%)
  local copies, waits for them, and re-layouts  11.4 us (9%)
  other arithmetic  6.39 us (5%)
    ppermute x8, waiting for transfers between devices, relative_gather(): from_right = lax.ppermute(from_right, axis, left)  16.7 us
    ppermute x8, starting transfers between devices, relative_gather(): from_right = lax.ppermute(from_right, axis, left)  15 us
    pallas_call x2, Pallas kernels, block_products(): pl.pallas_call(functools.partial(block_kernel, n_grad, ny), out_shape=jax...  13.4 us
    ppermute x8, waiting for transfers between devices, relative_gather(): from_left = lax.ppermute(from_left, axis, right)  11.6 us
    unnamed x24, local copies, waits for them, and re-layouts  7.88 us
    ppermute x1, starting transfers between devices, on_device(): lead_other = lax.ppermute(lead_all, 'core', swap)  7.06 us
    ppermute x4, waiting for transfers between devices, relative_gather(): near_a = lax.ppermute(from_left[:half], axis, right)  6.33 us
    ppermute x1, waiting for transfers between devices, on_device(): trail_other = lax.ppermute(trail_all, 'core', swap)  6 us
  transfers between devices with their start and end apart: 31, of which 13 were waited for; matrix products, arithmetic and copies ran while one was open for 9% of the time, Pallas kernels for 1%

profile of v1, /device:TPU:25, one launch (start us, length us, event | category | flops | bytes accessed | tf_op | source)
XLA Modules:
  0.0 124.3 jit_solution(10994180451190364447)
XLA Ops:
  0.0 1.1 broadcast_select_fusion.2
  2.8 1.0 broadcast_select_fusion
  3.8 1.7 %collective-permute-start.14 = (bf16[128,512]{1,0:T(8,128)(2,1)S(1)}, bf16[128,512]{1,0:T(8,128)(2,1)S(1)}, u32[]{:S(2)}, u32[]{:S(2)}) collective-permute-start(bf16[128,512]{1,0:T(8,128)(2,1)S(1)} %broadcast_select_fusion), channel_id=1, source_target_pairs={{0,2},{2,4},{4,6},{6,0},{1,3},{3,5},{5,7},{7,1},{8,10},{10,12},{12... | collective-permute-start | bytes 393224 | tf_op jit(solution)/shard_map/ppermute | solution.py:125
  5.6 1.0 bitcast_dynamic-update-slice_fusion.13
  6.6 5.5 %collective-permute-start.1 = (bf16[128,512]{1,0:T(8,128)(2,1)S(1)}, bf16[128,512]{1,0:T(8,128)(2,1)S(1)}, u32[]{:S(2)}, u32[]{:S(2)}) collective-permute-start(bf16[128,512]{1,0:T(8,128)(2,1)S(1)} %get-tuple-element.23), channel_id=1, source_target_pairs={{0,56},{8,0},{16,8},{24,16},{32,24},{40,32},{48,40},{56,48},{1,57}... | collective-permute-start | bytes 393224 | tf_op jit(solution)/shard_map/ppermute | solution.py:126
  12.6 2.3 %collective-permute-start.15 = (bf16[64,512]{1,0:T(8,128)(2,1)S(1)}, bf16[64,512]{1,0:T(8,128)(2,1)S(1)}, u32[]{:S(2)}, u32[]{:S(2)}) collective-permute-start(bf16[64,512]{1,0:T(8,128)(2,1)S(1)} %slice.52), channel_id=1, source_target_pairs={{0,2},{2,4},{4,6},{6,0},{1,3},{3,5},{5,7},{7,1},{8,10},{10,12},{12... | collective-permute-start | bytes 196616 | tf_op jit(solution)/shard_map/ppermute | solution.py:132
  14.9 3.2 %collective-permute-start.2 = (bf16[128,512]{1,0:T(8,128)(2,1)S(1)}, bf16[128,512]{1,0:T(8,128)(2,1)S(1)}, u32[]{:S(2)}, u32[]{:S(2)}) collective-permute-start(bf16[128,512]{1,0:T(8,128)(2,1)S(1)} %collective-permute-done.1), channel_id=1, source_target_pairs={{0,56},{8,0},{16,8},{24,16},{32,24},{40,32},{48,40},{56,48},{1,57}... | collective-permute-start | bytes 393224 | tf_op jit(solution)/shard_map/ppermute | solution.py:126
  18.3 2.7 %collective-permute-start.17 = (bf16[4,128,512]{2,1,0:T(8,128)(2,1)S(1)}, bf16[4,128,512]{2,1,0:T(8,128)(2,1)S(1)}, u32[]{:S(2)}, u32[]{:S(2)}) collective-permute-start(bf16[4,128,512]{2,1,0:T(8,128)(2,1)S(1)} %pad_maximum_fusion.1), channel_id=1, source_target_pairs={{0,56},{8,0},{16,8},{24,16},{32,24},{40,32},{48,40},{56,48},{1,57}... | collective-permute-start | bytes 1572872 | tf_op jit(solution)/shard_map/ppermute | solution.py:126
  21.1 2.7 %collective-permute-start.3 = (bf16[128,512]{1,0:T(8,128)(2,1)S(1)}, bf16[128,512]{1,0:T(8,128)(2,1)S(1)}, u32[]{:S(2)}, u32[]{:S(2)}) collective-permute-start(bf16[128,512]{1,0:T(8,128)(2,1)S(1)} %collective-permute-done.2), channel_id=1, source_target_pairs={{0,56},{8,0},{16,8},{24,16},{32,24},{40,32},{48,40},{56,48},{1,57}... | collective-permute-start | bytes 393224 | tf_op jit(solution)/shard_map/ppermute | solution.py:126
  23.8 10.6 %collective-permute-done.3 = bf16[128,512]{1,0:T(8,128)(2,1)S(1)} collective-permute-done((bf16[128,512]{1,0:T(8,128)(2,1)S(1)}, bf16[128,512]{1,0:T(8,128)(2,1)S(1)}, u32[]{:S(2)}, u32[]{:S(2)}) %collective-permute-start.3) | collective-permute-done | bytes 131104 | tf_op jit(solution)/shard_map/ppermute | solution.py:126
  34.3 3.4 %collective-permute-start.8 = (bf16[64,512]{1,0:T(8,128)(2,1)S(1)}, bf16[64,512]{1,0:T(8,128)(2,1)S(1)}, u32[]{:S(2)}, u32[]{:S(2)}) collective-permute-start(bf16[64,512]{1,0:T(8,128)(2,1)S(1)} %slice.49), channel_id=1, source_target_pairs={{0,56},{8,0},{16,8},{24,16},{32,24},{40,32},{48,40},{56,48},{1,57}... | collective-permute-start | bytes 196616 | tf_op jit(solution)/shard_map/ppermute | solution.py:133
  39.1 3.5 %collective-permute-done.7 = bf16[64,512]{1,0:T(8,128)(2,1)S(1)} collective-permute-done((bf16[64,512]{1,0:T(8,128)(2,1)S(1)}, bf16[64,512]{1,0:T(8,128)(2,1)S(1)}, u32[]{:S(2)}, u32[]{:S(2)}) %collective-permute-start.7) | collective-permute-done | bytes 65568 | tf_op jit(solution)/shard_map/ppermute | solution.py:132
  43.0 2.7 %collective-permute-start.10 = (bf16[8,128,512]{2,1,0:T(8,128)(2,1)S(1)}, bf16[8,128,512]{2,1,0:T(8,128)(2,1)S(1)}, u32[]{:S(2)}, u32[]{:S(2)}) collective-permute-start(bf16[8,128,512]{2,1,0:T(8,128)(2,1)S(1)} %bitcast_dynamic-update-slice_fusion.7), channel_id=1, source_target_pairs={{0,2},{2,4},{4,6},{6,0},{1,3},{3,5},{5,7},{7,1},{8,10},{10,12},{12... | collective-permute-start | bytes 3145736 | tf_op jit(solution)/shard_map/ppermute | solution.py:125
  45.7 1.2 collective-permute-start.25
  46.9 1.5 %collective-permute-start.26 = (bf16[2048,256]{1,0:T(8,128)(2,1)S(1)}, bf16[2048,256]{1,0:T(8,128)(2,1)S(1)}, u32[]{:S(2)}, u32[]{:S(2)}) collective-permute-start(bf16[2048,256]{1,0:T(8,128)(2,1)S(1)} %copy-done), channel_id=1, source_target_pairs={{0,192},{64,0},{128,64},{192,128},{1,193},{65,1},{129,65},{193,129... | collective-permute-start | bytes 3145736 | tf_op jit(solution)/shard_map/ppermute | solution.py:147
  48.3 4.4 %collective-permute-done.18 = bf16[4,128,512]{2,1,0:T(8,128)(2,1)S(1)} collective-permute-done((bf16[4,128,512]{2,1,0:T(8,128)(2,1)S(1)}, bf16[4,128,512]{2,1,0:T(8,128)(2,1)S(1)}, u32[]{:S(2)}, u32[]{:S(2)}) %collective-permute-start.18) | collective-permute-done | bytes 524320 | tf_op jit(solution)/shard_map/ppermute | solution.py:126
  52.8 10.3 %collective-permute-done.21 = bf16[4,128,512]{2,1,0:T(8,128)(2,1)S(1)} collective-permute-done((bf16[4,128,512]{2,1,0:T(8,128)(2,1)S(1)}, bf16[4,128,512]{2,1,0:T(8,128)(2,1)S(1)}, u32[]{:S(2)}, u32[]{:S(2)}) %collective-permute-start.21) | collective-permute-done | bytes 524320 | tf_op jit(solution)/shard_map/ppermute | solution.py:125
  63.6 1.7 %collective-permute-done.9 = bf16[8,128,512]{2,1,0:T(8,128)(2,1)S(1)} collective-permute-done((bf16[8,128,512]{2,1,0:T(8,128)(2,1)S(1)}, bf16[8,128,512]{2,1,0:T(8,128)(2,1)S(1)}, u32[]{:S(2)}, u32[]{:S(2)}) %collective-permute-start.9) | collective-permute-done | bytes 1048608 | tf_op jit(solution)/shard_map/ppermute | solution.py:126
  65.3 1.2 collective-permute-start.22
  67.6 2.7 %collective-permute-start.11 = (bf16[4,128,512]{2,1,0:T(8,128)(2,1)S(1)}, bf16[4,128,512]{2,1,0:T(8,128)(2,1)S(1)}, u32[]{:S(2)}, u32[]{:S(2)}) collective-permute-start(bf16[4,128,512]{2,1,0:T(8,128)(2,1)S(1)} %slice.50), channel_id=1, source_target_pairs={{0,2},{2,4},{4,6},{6,0},{1,3},{3,5},{5,7},{7,1},{8,10},{10,12},{12... | collective-permute-start | bytes 1572872 | tf_op jit(solution)/shard_map/ppermute | solution.py:132
  71.2 1.3 %collective-permute-start.27 = (bf16[1024,256]{1,0:T(8,128)(2,1)S(1)}, bf16[1024,256]{1,0:T(8,128)(2,1)S(1)}, u32[]{:S(2)}, u32[]{:S(2)}) collective-permute-start(bf16[1024,256]{1,0:T(8,128)(2,1)S(1)} %slice.56), channel_id=1, source_target_pairs={{0,64},{64,128},{128,192},{192,0},{1,65},{65,129},{129,193},{193,1... | collective-permute-start | bytes 1572872 | tf_op jit(solution)/shard_map/ppermute | solution.py:156
  73.3 1.5 %collective-permute-start.28 = (bf16[1024,256]{1,0:T(8,128)(2,1)S(1)}, bf16[1024,256]{1,0:T(8,128)(2,1)S(1)}, u32[]{:S(2)}, u32[]{:S(2)}) collective-permute-start(bf16[1024,256]{1,0:T(8,128)(2,1)S(1)} %slice.57), channel_id=1, source_target_pairs={{0,192},{64,0},{128,64},{192,128},{1,193},{65,1},{129,65},{193,129... | collective-permute-start | bytes 1572872 | tf_op jit(solution)/shard_map/ppermute | solution.py:157
  78.6 2.5 %collective-permute-done.24 = bf16[2,128,512]{2,1,0:T(8,128)(2,1)S(1)} collective-permute-done((bf16[2,128,512]{2,1,0:T(8,128)(2,1)S(1)}, bf16[2,128,512]{2,1,0:T(8,128)(2,1)S(1)}, u32[]{:S(2)}, u32[]{:S(2)}) %collective-permute-start.24) | collective-permute-done | bytes 262176 | tf_op jit(solution)/shard_map/ppermute | solution.py:133
  81.1 2.8 %collective-permute-done.23 = bf16[2,128,512]{2,1,0:T(8,128)(2,1)S(1)} collective-permute-done((bf16[2,128,512]{2,1,0:T(8,128)(2,1)S(1)}, bf16[2,128,512]{2,1,0:T(8,128)(2,1)S(1)}, u32[]{:S(2)}, u32[]{:S(2)}) %collective-permute-start.23) | collective-permute-done | bytes 262176 | tf_op jit(solution)/shard_map/ppermute | solution.py:132
  85.7 2.4 %copy.6 = bf16[8,4,128,512]{3,2,1,0:T(8,128)(2,1)} copy(bf16[8,4,128,512]{3,2,0,1:T(8,128)(2,1)S(1)} %pad_maximum_fusion) | data formatting | bytes 8388608 | tf_op jit(solution)/shard_map/stack | solution.py:194
  91.4 7.1 %collective-permute-start.29 = (bf16[32,128,512]{2,1,0:T(8,128)(2,1)}, bf16[32,128,512]{2,1,0:T(8,128)(2,1)}, u32[]{:S(2)}, u32[]{:S(2)}) collective-permute-start(bf16[32,128,512]{2,1,0:T(8,128)(2,1)} %bitcast.22.rest_0_), channel_id=1, source_target_pairs={{0,1},{1,0},{2,3},{3,2},{4,5},{5,4},{6,7},{7,6},{8,9},{9,8},{10,11... | collective-permute-start | bytes 12582920 | tf_op jit(solution)/shard_map/ppermute | solution.py:204
  99.4 1.0 copy-done.2
  100.4 1.0 copy-done.4
  101.4 1.4 %shard_map.55 = f32[4,128,128]{2,1,0:T(8,128)S(1)} custom-call(s32[4]{0:T(128)S(1)} %and_select_fusion.2.rows_ref, s32[4]{0:T(128)S(1)} %clamp_bitcast_fusion.cols_ref, s32[4]{0:T(128)S(1)} %and_convert_fusion.1.use_ref, s32[5]{0:T(128)S(1)} %and_select_fusion.starts_ref, s32[2]{0:T(128)S(1)} %pad_add_fusion.place_ref, ...), custom_call_target="tpu_custom_call" | custom-call | flops 2147483648 | bytes 12845056 | tf_op jit(solution)/shard_map/pallas_call | solution.py:103
  102.9 2.7 %collective-permute-done.29.rest_0_ = bf16[32,128,512]{2,1,0:T(8,128)(2,1)} collective-permute-done((bf16[32,128,512]{2,1,0:T(8,128)(2,1)}, bf16[32,128,512]{2,1,0:T(8,128)(2,1)}, u32[]{:S(2)}, u32[]{:S(2)}) %collective-permute-start.29) | collective-permute-done | bytes 4194336 | tf_op jit(solution)/shard_map/ppermute | solution.py:204
  105.6 6.0 %collective-permute-done.30.rest_1_ = bf16[32,128,512]{2,1,0:T(8,128)(2,1)} collective-permute-done((bf16[32,128,512]{2,1,0:T(8,128)(2,1)}, bf16[32,128,512]{2,1,0:T(8,128)(2,1)}, u32[]{:S(2)}, u32[]{:S(2)}) %collective-permute-start.30) | collective-permute-done | bytes 4194336 | tf_op jit(solution)/shard_map/ppermute | solution.py:205
  111.6 12.0 %shard_map.56 = f32[4,128,128]{2,1,0:T(8,128)S(1)} custom-call(s32[4]{0:T(128)S(1)} %and_select_fusion.2.rows_ref, s32[4]{0:T(128)S(1)} %clamp_bitcast_fusion.cols_ref, s32[4]{0:T(128)S(1)} %get-tuple-element.19.use_ref, s32[5]{0:T(128)S(1)} %and_select_fusion.starts_ref, s32[2]{0:T(128)S(1)} %pad_add_fusion.place_ref, ...), custom_call_target="tpu_custom_call" | custom-call | flops 2147483648 | bytes 12845056 | tf_op jit(solution)/shard_map/pallas_call | solution.py:103
  (87 shorter events, 17.2 us)
Async XLA Ops:
  0.0 45.7 %copy-start = (bf16[2048,256]{1,0:T(8,128)(2,1)S(1)}, bf16[2048,256]{1,0:T(8,128)(2,1)}, u32[]{:S(2)}) copy-start(bf16[2048,256]{1,0:T(8,128)(2,1)} %param.6) | copy-start | bytes 3145732
  1.1 1.7 %collective-permute-start = (bf16[128,512]{1,0:T(8,128)(2,1)S(1)}, bf16[128,512]{1,0:T(8,128)(2,1)S(1)}, u32[]{:S(2)}, u32[]{:S(2)}) collective-permute-start(bf16[128,512]{1,0:T(8,128)(2,1)S(1)} %broadcast_select_fusion.2), channel_id=1, source_target_pairs={{0,1},{1,0},{2,3},{3,2},{4,5},{5,4},{6,7},{7,6},{8,9},{9,8},{10,11... | collective-permute-start | bytes 393224 | tf_op jit(solution)/shard_map/ppermute | solution.py:189
  3.8 8.8 %collective-permute-start.14 = (bf16[128,512]{1,0:T(8,128)(2,1)S(1)}, bf16[128,512]{1,0:T(8,128)(2,1)S(1)}, u32[]{:S(2)}, u32[]{:S(2)}) collective-permute-start(bf16[128,512]{1,0:T(8,128)(2,1)S(1)} %broadcast_select_fusion), channel_id=1, source_target_pairs={{0,2},{2,4},{4,6},{6,0},{1,3},{3,5},{5,7},{7,1},{8,10},{10,12},{12... | collective-permute-start | bytes 393224 | tf_op jit(solution)/shard_map/ppermute | solution.py:125
  5.6 6.5 %collective-permute-start.13 = (bf16[128,512]{1,0:T(8,128)(2,1)S(1)}, bf16[128,512]{1,0:T(8,128)(2,1)S(1)}, u32[]{:S(2)}, u32[]{:S(2)}) collective-permute-start(bf16[128,512]{1,0:T(8,128)(2,1)S(1)} %broadcast_select_fusion), channel_id=1, source_target_pairs={{0,6},{2,0},{4,2},{6,4},{1,7},{3,1},{5,3},{7,5},{8,14},{10,8},{12,... | collective-permute-start | bytes 393224 | tf_op jit(solution)/shard_map/ppermute | solution.py:126
  6.6 8.3 %collective-permute-start.1 = (bf16[128,512]{1,0:T(8,128)(2,1)S(1)}, bf16[128,512]{1,0:T(8,128)(2,1)S(1)}, u32[]{:S(2)}, u32[]{:S(2)}) collective-permute-start(bf16[128,512]{1,0:T(8,128)(2,1)S(1)} %get-tuple-element.23), channel_id=1, source_target_pairs={{0,56},{8,0},{16,8},{24,16},{32,24},{40,32},{48,40},{56,48},{1,57}... | collective-permute-start | bytes 393224 | tf_op jit(solution)/shard_map/ppermute | solution.py:126
  12.0 6.1 %collective-permute-start.4 = (bf16[128,512]{1,0:T(8,128)(2,1)S(1)}, bf16[128,512]{1,0:T(8,128)(2,1)S(1)}, u32[]{:S(2)}, u32[]{:S(2)}) collective-permute-start(bf16[128,512]{1,0:T(8,128)(2,1)S(1)} %get-tuple-element.23), channel_id=1, source_target_pairs={{0,8},{8,16},{16,24},{24,32},{32,40},{40,48},{48,56},{56,0},{1,9},... | collective-permute-start | bytes 393224 | tf_op jit(solution)/shard_map/ppermute | solution.py:125
  12.1 6.2 %collective-permute-start.16 = (bf16[64,512]{1,0:T(8,128)(2,1)S(1)}, bf16[64,512]{1,0:T(8,128)(2,1)S(1)}, u32[]{:S(2)}, u32[]{:S(2)}) collective-permute-start(bf16[64,512]{1,0:T(8,128)(2,1)S(1)} %slice.53), channel_id=1, source_target_pairs={{0,6},{2,0},{4,2},{6,4},{1,7},{3,1},{5,3},{7,5},{8,14},{10,8},{12,... | collective-permute-start | bytes 196616 | tf_op jit(solution)/shard_map/ppermute | solution.py:133
  12.6 5.6 %collective-permute-start.15 = (bf16[64,512]{1,0:T(8,128)(2,1)S(1)}, bf16[64,512]{1,0:T(8,128)(2,1)S(1)}, u32[]{:S(2)}, u32[]{:S(2)}) collective-permute-start(bf16[64,512]{1,0:T(8,128)(2,1)S(1)} %slice.52), channel_id=1, source_target_pairs={{0,2},{2,4},{4,6},{6,0},{1,3},{3,5},{5,7},{7,1},{8,10},{10,12},{12... | collective-permute-start | bytes 196616 | tf_op jit(solution)/shard_map/ppermute | solution.py:132
  14.9 6.2 %collective-permute-start.2 = (bf16[128,512]{1,0:T(8,128)(2,1)S(1)}, bf16[128,512]{1,0:T(8,128)(2,1)S(1)}, u32[]{:S(2)}, u32[]{:S(2)}) collective-permute-start(bf16[128,512]{1,0:T(8,128)(2,1)S(1)} %collective-permute-done.1), channel_id=1, source_target_pairs={{0,56},{8,0},{16,8},{24,16},{32,24},{40,32},{48,40},{56,48},{1,57}... | collective-permute-start | bytes 393224 | tf_op jit(solution)/shard_map/ppermute | solution.py:126
  18.1 5.6 %collective-permute-start.5 = (bf16[128,512]{1,0:T(8,128)(2,1)S(1)}, bf16[128,512]{1,0:T(8,128)(2,1)S(1)}, u32[]{:S(2)}, u32[]{:S(2)}) collective-permute-start(bf16[128,512]{1,0:T(8,128)(2,1)S(1)} %collective-permute-done.4), channel_id=1, source_target_pairs={{0,8},{8,16},{16,24},{24,32},{32,40},{40,48},{48,56},{56,0},{1,9},... | collective-permute-start | bytes 393224 | tf_op jit(solution)/shard_map/ppermute | solution.py:125
  18.3 24.3 %collective-permute-start.17 = (bf16[4,128,512]{2,1,0:T(8,128)(2,1)S(1)}, bf16[4,128,512]{2,1,0:T(8,128)(2,1)S(1)}, u32[]{:S(2)}, u32[]{:S(2)}) collective-permute-start(bf16[4,128,512]{2,1,0:T(8,128)(2,1)S(1)} %pad_maximum_fusion.1), channel_id=1, source_target_pairs={{0,56},{8,0},{16,8},{24,16},{32,24},{40,32},{48,40},{56,48},{1,57}... | collective-permute-start | bytes 1572872 | tf_op jit(solution)/shard_map/ppermute | solution.py:126
  21.1 25.8 %collective-permute-start.20 = (bf16[4,128,512]{2,1,0:T(8,128)(2,1)S(1)}, bf16[4,128,512]{2,1,0:T(8,128)(2,1)S(1)}, u32[]{:S(2)}, u32[]{:S(2)}) collective-permute-start(bf16[4,128,512]{2,1,0:T(8,128)(2,1)S(1)} %pad_maximum_fusion.1), channel_id=1, source_target_pairs={{0,8},{8,16},{16,24},{24,32},{32,40},{40,48},{48,56},{56,0},{1,9},... | collective-permute-start | bytes 1572872 | tf_op jit(solution)/shard_map/ppermute | solution.py:125
  21.1 13.3 %collective-permute-start.3 = (bf16[128,512]{1,0:T(8,128)(2,1)S(1)}, bf16[128,512]{1,0:T(8,128)(2,1)S(1)}, u32[]{:S(2)}, u32[]{:S(2)}) collective-permute-start(bf16[128,512]{1,0:T(8,128)(2,1)S(1)} %collective-permute-done.2), channel_id=1, source_target_pairs={{0,56},{8,0},{16,8},{24,16},{32,24},{40,32},{48,40},{56,48},{1,57}... | collective-permute-start | bytes 393224 | tf_op jit(solution)/shard_map/ppermute | solution.py:126
  23.7 14.5 %collective-permute-start.6 = (bf16[128,512]{1,0:T(8,128)(2,1)S(1)}, bf16[128,512]{1,0:T(8,128)(2,1)S(1)}, u32[]{:S(2)}, u32[]{:S(2)}) collective-permute-start(bf16[128,512]{1,0:T(8,128)(2,1)S(1)} %collective-permute-done.5), channel_id=1, source_target_pairs={{0,8},{8,16},{16,24},{24,32},{32,40},{40,48},{48,56},{56,0},{1,9},... | collective-permute-start | bytes 393224 | tf_op jit(solution)/shard_map/ppermute | solution.py:125
  34.3 4.7 %collective-permute-start.8 = (bf16[64,512]{1,0:T(8,128)(2,1)S(1)}, bf16[64,512]{1,0:T(8,128)(2,1)S(1)}, u32[]{:S(2)}, u32[]{:S(2)}) collective-permute-start(bf16[64,512]{1,0:T(8,128)(2,1)S(1)} %slice.49), channel_id=1, source_target_pairs={{0,56},{8,0},{16,8},{24,16},{32,24},{40,32},{48,40},{56,48},{1,57}... | collective-permute-start | bytes 196616 | tf_op jit(solution)/shard_map/ppermute | solution.py:133
  38.2 4.3 %collective-permute-start.7 = (bf16[64,512]{1,0:T(8,128)(2,1)S(1)}, bf16[64,512]{1,0:T(8,128)(2,1)S(1)}, u32[]{:S(2)}, u32[]{:S(2)}) collective-permute-start(bf16[64,512]{1,0:T(8,128)(2,1)S(1)} %slice.48), channel_id=1, source_target_pairs={{0,8},{8,16},{16,24},{24,32},{32,40},{40,48},{48,56},{56,0},{1,9},... | collective-permute-start | bytes 196616 | tf_op jit(solution)/shard_map/ppermute | solution.py:132
  42.6 10.2 %collective-permute-start.18 = (bf16[4,128,512]{2,1,0:T(8,128)(2,1)S(1)}, bf16[4,128,512]{2,1,0:T(8,128)(2,1)S(1)}, u32[]{:S(2)}, u32[]{:S(2)}) collective-permute-start(bf16[4,128,512]{2,1,0:T(8,128)(2,1)S(1)} %collective-permute-done.17), channel_id=1, source_target_pairs={{0,56},{8,0},{16,8},{24,16},{32,24},{40,32},{48,40},{56,48},{1,57}... | collective-permute-start | bytes 1572872 | tf_op jit(solution)/shard_map/ppermute | solution.py:126
  42.9 22.4 %collective-permute-start.9 = (bf16[8,128,512]{2,1,0:T(8,128)(2,1)S(1)}, bf16[8,128,512]{2,1,0:T(8,128)(2,1)S(1)}, u32[]{:S(2)}, u32[]{:S(2)}) collective-permute-start(bf16[8,128,512]{2,1,0:T(8,128)(2,1)S(1)} %bitcast_dynamic-update-slice_fusion.7), channel_id=1, source_target_pairs={{0,6},{2,0},{4,2},{6,4},{1,7},{3,1},{5,3},{7,5},{8,14},{10,8},{12,... | collective-permute-start | bytes 3145736 | tf_op jit(solution)/shard_map/ppermute | solution.py:126
  43.0 24.4 %collective-permute-start.10 = (bf16[8,128,512]{2,1,0:T(8,128)(2,1)S(1)}, bf16[8,128,512]{2,1,0:T(8,128)(2,1)S(1)}, u32[]{:S(2)}, u32[]{:S(2)}) collective-permute-start(bf16[8,128,512]{2,1,0:T(8,128)(2,1)S(1)} %bitcast_dynamic-update-slice_fusion.7), channel_id=1, source_target_pairs={{0,2},{2,4},{4,6},{6,0},{1,3},{3,5},{5,7},{7,1},{8,10},{10,12},{12... | collective-permute-start | bytes 3145736 | tf_op jit(solution)/shard_map/ppermute | solution.py:125
  45.7 21.9 %collective-permute-start.25 = (bf16[2048,256]{1,0:T(8,128)(2,1)S(1)}, bf16[2048,256]{1,0:T(8,128)(2,1)S(1)}, u32[]{:S(2)}, u32[]{:S(2)}) collective-permute-start(bf16[2048,256]{1,0:T(8,128)(2,1)S(1)} %copy-done), channel_id=1, source_target_pairs={{0,64},{64,128},{128,192},{192,0},{1,65},{65,129},{129,193},{193,1... | collective-permute-start | bytes 3145736 | tf_op jit(solution)/shard_map/ppermute | solution.py:146
  46.9 24.3 %collective-permute-start.26 = (bf16[2048,256]{1,0:T(8,128)(2,1)S(1)}, bf16[2048,256]{1,0:T(8,128)(2,1)S(1)}, u32[]{:S(2)}, u32[]{:S(2)}) collective-permute-start(bf16[2048,256]{1,0:T(8,128)(2,1)S(1)} %copy-done), channel_id=1, source_target_pairs={{0,192},{64,0},{128,64},{192,128},{1,193},{65,1},{129,65},{193,129... | collective-permute-start | bytes 3145736 | tf_op jit(solution)/shard_map/ppermute | solution.py:147
  52.8 10.3 %collective-permute-start.21 = (bf16[4,128,512]{2,1,0:T(8,128)(2,1)S(1)}, bf16[4,128,512]{2,1,0:T(8,128)(2,1)S(1)}, u32[]{:S(2)}, u32[]{:S(2)}) collective-permute-start(bf16[4,128,512]{2,1,0:T(8,128)(2,1)S(1)} %collective-permute-done.20), channel_id=1, source_target_pairs={{0,8},{8,16},{16,24},{24,32},{32,40},{40,48},{48,56},{56,0},{1,9},... | collective-permute-start | bytes 1572872 | tf_op jit(solution)/shard_map/ppermute | solution.py:125
  63.1 10.2 %collective-permute-start.19 = (bf16[4,128,512]{2,1,0:T(8,128)(2,1)S(1)}, bf16[4,128,512]{2,1,0:T(8,128)(2,1)S(1)}, u32[]{:S(2)}, u32[]{:S(2)}) collective-permute-start(bf16[4,128,512]{2,1,0:T(8,128)(2,1)S(1)} %collective-permute-done.18), channel_id=1, source_target_pairs={{0,56},{8,0},{16,8},{24,16},{32,24},{40,32},{48,40},{56,48},{1,57}... | collective-permute-start | bytes 1572872 | tf_op jit(solution)/shard_map/ppermute | solution.py:126
  65.3 10.3 %collective-permute-start.22 = (bf16[4,128,512]{2,1,0:T(8,128)(2,1)S(1)}, bf16[4,128,512]{2,1,0:T(8,128)(2,1)S(1)}, u32[]{:S(2)}, u32[]{:S(2)}) collective-permute-start(bf16[4,128,512]{2,1,0:T(8,128)(2,1)S(1)} %collective-permute-done.21), channel_id=1, source_target_pairs={{0,8},{8,16},{16,24},{24,32},{32,40},{40,48},{48,56},{56,0},{1,9},... | collective-permute-start | bytes 1572872 | tf_op jit(solution)/shard_map/ppermute | solution.py:125
  67.4 9.8 %collective-permute-start.12 = (bf16[4,128,512]{2,1,0:T(8,128)(2,1)S(1)}, bf16[4,128,512]{2,1,0:T(8,128)(2,1)S(1)}, u32[]{:S(2)}, u32[]{:S(2)}) collective-permute-start(bf16[4,128,512]{2,1,0:T(8,128)(2,1)S(1)} %slice.51), channel_id=1, source_target_pairs={{0,6},{2,0},{4,2},{6,4},{1,7},{3,1},{5,3},{7,5},{8,14},{10,8},{12,... | collective-permute-start | bytes 1572872 | tf_op jit(solution)/shard_map/ppermute | solution.py:133
  67.6 10.4 %collective-permute-start.11 = (bf16[4,128,512]{2,1,0:T(8,128)(2,1)S(1)}, bf16[4,128,512]{2,1,0:T(8,128)(2,1)S(1)}, u32[]{:S(2)}, u32[]{:S(2)}) collective-permute-start(bf16[4,128,512]{2,1,0:T(8,128)(2,1)S(1)} %slice.50), channel_id=1, source_target_pairs={{0,2},{2,4},{4,6},{6,0},{1,3},{3,5},{5,7},{7,1},{8,10},{10,12},{12... | collective-permute-start | bytes 1572872 | tf_op jit(solution)/shard_map/ppermute | solution.py:132
  71.2 18.6 %collective-permute-start.27 = (bf16[1024,256]{1,0:T(8,128)(2,1)S(1)}, bf16[1024,256]{1,0:T(8,128)(2,1)S(1)}, u32[]{:S(2)}, u32[]{:S(2)}) collective-permute-start(bf16[1024,256]{1,0:T(8,128)(2,1)S(1)} %slice.56), channel_id=1, source_target_pairs={{0,64},{64,128},{128,192},{192,0},{1,65},{65,129},{129,193},{193,1... | collective-permute-start | bytes 1572872 | tf_op jit(solution)/shard_map/ppermute | solution.py:156
  73.3 17.3 %collective-permute-start.28 = (bf16[1024,256]{1,0:T(8,128)(2,1)S(1)}, bf16[1024,256]{1,0:T(8,128)(2,1)S(1)}, u32[]{:S(2)}, u32[]{:S(2)}) collective-permute-start(bf16[1024,256]{1,0:T(8,128)(2,1)S(1)} %slice.57), channel_id=1, source_target_pairs={{0,192},{64,0},{128,64},{192,128},{1,193},{65,1},{129,65},{193,129... | collective-permute-start | bytes 1572872 | tf_op jit(solution)/shard_map/ppermute | solution.py:157
  75.6 5.5 %collective-permute-start.24 = (bf16[2,128,512]{2,1,0:T(8,128)(2,1)S(1)}, bf16[2,128,512]{2,1,0:T(8,128)(2,1)S(1)}, u32[]{:S(2)}, u32[]{:S(2)}) collective-permute-start(bf16[2,128,512]{2,1,0:T(8,128)(2,1)S(1)} %slice.55), channel_id=1, source_target_pairs={{0,56},{8,0},{16,8},{24,16},{32,24},{40,32},{48,40},{56,48},{1,57}... | collective-permute-start | bytes 786440 | tf_op jit(solution)/shard_map/ppermute | solution.py:133
  77.3 6.7 %collective-permute-start.23 = (bf16[2,128,512]{2,1,0:T(8,128)(2,1)S(1)}, bf16[2,128,512]{2,1,0:T(8,128)(2,1)S(1)}, u32[]{:S(2)}, u32[]{:S(2)}) collective-permute-start(bf16[2,128,512]{2,1,0:T(8,128)(2,1)S(1)} %slice.54), channel_id=1, source_target_pairs={{0,8},{8,16},{16,24},{24,32},{32,40},{40,48},{48,56},{56,0},{1,9},... | collective-permute-start | bytes 786440 | tf_op jit(solution)/shard_map/ppermute | solution.py:132
  91.4 14.2 %collective-permute-start.29 = (bf16[32,128,512]{2,1,0:T(8,128)(2,1)}, bf16[32,128,512]{2,1,0:T(8,128)(2,1)}, u32[]{:S(2)}, u32[]{:S(2)}) collective-permute-start(bf16[32,128,512]{2,1,0:T(8,128)(2,1)} %bitcast.22.rest_0_), channel_id=1, source_target_pairs={{0,1},{1,0},{2,3},{3,2},{4,5},{5,4},{6,7},{7,6},{8,9},{9,8},{10,11... | collective-permute-start | bytes 12582920 | tf_op jit(solution)/shard_map/ppermute | solution.py:204
  98.4 13.1 %collective-permute-start.30 = (bf16[32,128,512]{2,1,0:T(8,128)(2,1)}, bf16[32,128,512]{2,1,0:T(8,128)(2,1)}, u32[]{:S(2)}, u32[]{:S(2)}) collective-permute-start(bf16[32,128,512]{2,1,0:T(8,128)(2,1)} %bitcast.35.rest_1_), channel_id=1, source_target_pairs={{0,1},{1,0},{2,3},{3,2},{4,5},{5,4},{6,7},{7,6},{8,9},{9,8},{10,11... | collective-permute-start | bytes 12582920 | tf_op jit(solution)/shard_map/ppermute | solution.py:205
  (6 other events, 31.0 us)

commit v2 on v0

--- a/solution.py
+++ b/solution.py
@@ -12,9 +12,9 @@
 
 
 def block_kernel(n_grad, ny, rows_ref, cols_ref, use_ref, starts_ref, place_ref, *rest):
-    first_hbm, second_hbm = rest[0], rest[1]
-    grad_hbm = rest[2:2 + n_grad]
-    out_ref, a_v, g_v, sems = rest[2 + n_grad:]
+    act_hbm = rest[0]
+    grad_hbm = rest[1:1 + n_grad]
+    out_ref, a_v, g_v, sems = rest[1 + n_grad:]
     chunks, _, tok, _ = a_v.shape[1:]
 
     copies = []
@@ -22,8 +22,8 @@
         r = pl.multiple_of(rows_ref[s] * BLK, BLK)
         c = pl.multiple_of(cols_ref[s] * BLK, BLK)
         slot = [
-            pltpu.make_async_copy(first_hbm.at[:, :, pl.ds(r, BLK)], a_v.at[s, :, 0], sems.at[s, 0]),
-            pltpu.make_async_copy(second_hbm.at[:, :, pl.ds(r, BLK)], a_v.at[s, :, 1], sems.at[s, 1]),
+            pltpu.make_async_copy(act_hbm.at[0, :, :, pl.ds(r, BLK)], a_v.at[s, :, 0], sems.at[s, 0]),
+            pltpu.make_async_copy(act_hbm.at[1, :, :, pl.ds(r, BLK)], a_v.at[s, :, 1], sems.at[s, 1]),
         ]
         for p, piece in enumerate(grad_hbm):
             slot.append(
@@ -63,12 +63,12 @@
                 )
 
             out_ref[s] = lax.fori_loop(
-                0, chunks, body, jnp.zeros((BLK, BLK), jnp.float32), unroll=2
+                0, chunks, body, jnp.zeros((BLK, BLK), jnp.float32), unroll=8
             )
 
 
-def block_products(first, second, grad_pieces, starts, place, local_rows, local_cols, use, ny):
-    chunks, tok, width = first.shape
+def block_products(both, grad_pieces, starts, place, local_rows, local_cols, use, ny):
+    _, chunks, tok, width = both.shape
     n_grad = len(grad_pieces)
     smem = pl.BlockSpec(memory_space=pltpu.SMEM)
     hbm = pl.BlockSpec(memory_space=pl.ANY)
@@ -78,7 +78,7 @@
     return pl.pallas_call(
         functools.partial(block_kernel, n_grad, ny),
         out_shape=jax.ShapeDtypeStruct((MAXB, BLK, BLK), jnp.float32),
-        in_specs=[smem] * 5 + [hbm] * (2 + n_grad),
+        in_specs=[smem] * 5 + [hbm] * (1 + n_grad),
         out_specs=pl.BlockSpec(memory_space=pltpu.VMEM),
         scratch_shapes=[
             pltpu.VMEM((MAXB, chunks, 2, tok, BLK), jnp.bfloat16),
@@ -87,10 +87,10 @@
         ],
         compiler_params=pltpu.CompilerParams(vmem_limit_bytes=48 * 1024 * 1024),
         cost_estimate=pl.CostEstimate(flops=flops, bytes_accessed=moved, transcendentals=0),
-    )(local_rows, local_cols, use, starts, place, first, second, *grad_pieces)
-
-
-def relative_gather(x, axis, n):
+    )(local_rows, local_cols, use, starts, place, both, *grad_pieces)
+
+
+def relative_gather(x, axis, n, split=True):
     right = [(k, (k + 1) % n) for k in range(n)]
     left = [(k, (k - 1) % n) for k in range(n)]
     rel = [x] + [None] * (n - 1)
@@ -100,7 +100,9 @@
         from_right = lax.ppermute(from_right, axis, left)
         rel[n - t] = from_left
         rel[t] = from_right
-    if n % 2 == 0 and n > 1:
+    if n % 2 == 0 and n > 1 and not split:
+        rel[n // 2] = lax.ppermute(from_left, axis, right)
+    elif n % 2 == 0 and n > 1:
         t = n // 2
         half = x.shape[0] // 2
         near_a = lax.ppermute(from_left[:half], axis, right)
@@ -164,25 +166,21 @@
     lead = jnp.where(on_first, keep, recv)
     trail = jnp.where(on_first, recv, keep)
 
-    lead_z = jnp.stack(relative_gather(lead, "z", nz), 0)
+    lead_z = jnp.stack(relative_gather(lead, "z", nz, split=False), 0)
     lead_all = jnp.stack(relative_gather(lead_z, "y", ny), 1)
-    trail_y = jnp.stack(relative_gather(trail, "y", ny), 0)
+    trail_y = jnp.stack(relative_gather(trail, "y", ny, split=False), 0)
     trail_all = jnp.stack(relative_gather(trail_y, "z", nz), 0)
     lead_all = lead_all.reshape(nz * ny, tok, width)
     trail_all = trail_all.reshape(nz * ny, tok, width)
 
     grad_pieces, starts = ring_gather(out_grad, "in", in_place)
-    lead_all, trail_all, grad_pieces = lax.optimization_barrier((lead_all, trail_all, grad_pieces))
+    both = jnp.stack([lead_all, trail_all], 0)
+    both, grad_pieces = lax.optimization_barrier((both, grad_pieces))
     grad_pieces = [g.reshape(g.shape[0] // (2 * tok), 2, tok, g.shape[1]) for g in grad_pieces]
     starts = starts // (2 * tok)
-    lead_other = lax.ppermute(lead_all, "core", swap)
-    trail_other = lax.ppermute(trail_all, "core", swap)
-    part_mine = block_products(
-        lead_all, trail_all, grad_pieces, starts, place, in_half, local_cols, use_mine, ny
-    )
-    part_other = block_products(
-        lead_other, trail_other, grad_pieces, starts, place, in_half, local_cols, use_other, ny
-    )
+    other = lax.ppermute(both, "core", swap)
+    part_mine = block_products(both, grad_pieces, starts, place, in_half, local_cols, use_mine, ny)
+    part_other = block_products(other, grad_pieces, starts, place, in_half, local_cols, use_other, ny)
     totals = part_mine + part_other
     return totals.reshape(1, 1, MAXB, BLK, BLK)
 

time: 125 us -> 126 us (level)
  the two profiles are of different devices: /device:TPU:6 before, /device:TPU:1 now
where the time goes in v2:
time: 126 us; the launch traced here: 128 us
  waiting for transfers between devices  53.1 us (42%)
  starting transfers between devices  45.9 us (36%)
  other arithmetic  12.3 us (10%)
  local copies, waits for them, and re-layouts  9.08 us (7%)
  Pallas kernels  6.41 us (5%)
    ppermute x8, waiting for transfers between devices, relative_gather(): from_left = lax.ppermute(from_left, axis, right)  26.1 us
    ppermute x8, starting transfers between devices, relative_gather(): from_right = lax.ppermute(from_right, axis, left)  16.4 us
    ppermute x1, starting transfers between devices, on_device(): other = lax.ppermute(both, 'core', swap)  11.7 us
    ppermute x2, waiting for transfers between devices, relative_gather(): rel[n // 2] = lax.ppermute(from_left, axis, right)  9.55 us
    ppermute x1, waiting for transfers between devices, on_device(): other = lax.ppermute(both, 'core', swap)  8.97 us
    another operation x1, other arithmetic, on_device(): both = jnp.stack([lead_all, trail_all], 0)  7.53 us
    pallas_call x2, Pallas kernels, block_products(): pl.pallas_call(functools.partial(block_kernel, n_grad, ny), out_shape=jax...  6.41 us
    ppermute x2, starting transfers between devices, relative_gather(): near_b = lax.ppermute(from_right[half:], axis, left)  4.52 us
  transfers between devices with their start and end apart: 28, of which 12 were waited for; matrix products, arithmetic and copies ran while one was open for 11% of the time, Pallas kernels for 1%

profile of v2, /device:TPU:1, one launch (start us, length us, event | category | flops | bytes accessed | tf_op | source)
XLA Modules:
  0.0 127.8 jit_solution(10322808040219495850)
XLA Ops:
  0.0 1.1 broadcast_select_fusion.2
  1.1 3.3 %collective-permute-start = (bf16[128,512]{1,0:T(8,128)(2,1)S(1)}, bf16[128,512]{1,0:T(8,128)(2,1)S(1)}, u32[]{:S(2)}, u32[]{:S(2)}) collective-permute-start(bf16[128,512]{1,0:T(8,128)(2,1)S(1)} %broadcast_select_fusion.2), channel_id=1, source_target_pairs={{0,1},{1,0},{2,3},{3,2},{4,5},{5,4},{6,7},{7,6},{8,9},{9,8},{10,11... | collective-permute-start | bytes 393224 | tf_op jit(solution)/shard_map/ppermute | solution.py:165
  6.4 3.9 %collective-permute-start.1 = (bf16[128,512]{1,0:T(8,128)(2,1)S(1)}, bf16[128,512]{1,0:T(8,128)(2,1)S(1)}, u32[]{:S(2)}, u32[]{:S(2)}) collective-permute-start(bf16[128,512]{1,0:T(8,128)(2,1)S(1)} %get-tuple-element.21), channel_id=1, source_target_pairs={{0,56},{8,0},{16,8},{24,16},{32,24},{40,32},{48,40},{56,48},{1,57}... | collective-permute-start | bytes 393224 | tf_op jit(solution)/shard_map/ppermute | solution.py:100
  11.3 1.4 %collective-permute-start.13 = (bf16[128,512]{1,0:T(8,128)(2,1)S(1)}, bf16[128,512]{1,0:T(8,128)(2,1)S(1)}, u32[]{:S(2)}, u32[]{:S(2)}) collective-permute-start(bf16[128,512]{1,0:T(8,128)(2,1)S(1)} %broadcast_select_fusion), channel_id=1, source_target_pairs={{0,2},{2,4},{4,6},{6,0},{1,3},{3,5},{5,7},{7,1},{8,10},{10,12},{12... | collective-permute-start | bytes 393224 | tf_op jit(solution)/shard_map/ppermute | solution.py:99
  12.7 1.5 %collective-permute-start.12 = (bf16[128,512]{1,0:T(8,128)(2,1)S(1)}, bf16[128,512]{1,0:T(8,128)(2,1)S(1)}, u32[]{:S(2)}, u32[]{:S(2)}) collective-permute-start(bf16[128,512]{1,0:T(8,128)(2,1)S(1)} %broadcast_select_fusion), channel_id=1, source_target_pairs={{0,6},{2,0},{4,2},{6,4},{1,7},{3,1},{5,3},{7,5},{8,14},{10,8},{12,... | collective-permute-start | bytes 393224 | tf_op jit(solution)/shard_map/ppermute | solution.py:100
  14.2 2.7 %collective-permute-start.2 = (bf16[128,512]{1,0:T(8,128)(2,1)S(1)}, bf16[128,512]{1,0:T(8,128)(2,1)S(1)}, u32[]{:S(2)}, u32[]{:S(2)}) collective-permute-start(bf16[128,512]{1,0:T(8,128)(2,1)S(1)} %collective-permute-done.1), channel_id=1, source_target_pairs={{0,56},{8,0},{16,8},{24,16},{32,24},{40,32},{48,40},{56,48},{1,57}... | collective-permute-start | bytes 393224 | tf_op jit(solution)/shard_map/ppermute | solution.py:100
  17.6 4.5 %collective-permute-done.14 = bf16[128,512]{1,0:T(8,128)(2,1)S(1)} collective-permute-done((bf16[128,512]{1,0:T(8,128)(2,1)S(1)}, bf16[128,512]{1,0:T(8,128)(2,1)S(1)}, u32[]{:S(2)}, u32[]{:S(2)}) %collective-permute-start.14) | collective-permute-done | bytes 131104 | tf_op jit(solution)/shard_map/ppermute | solution.py:104
  22.2 2.5 %collective-permute-start.15 = (bf16[4,128,512]{2,1,0:T(8,128)(2,1)S(1)}, bf16[4,128,512]{2,1,0:T(8,128)(2,1)S(1)}, u32[]{:S(2)}, u32[]{:S(2)}) collective-permute-start(bf16[4,128,512]{2,1,0:T(8,128)(2,1)S(1)} %pad_maximum_fusion.2), channel_id=1, source_target_pairs={{0,56},{8,0},{16,8},{24,16},{32,24},{40,32},{48,40},{56,48},{1,57}... | collective-permute-start | bytes 1572872 | tf_op jit(solution)/shard_map/ppermute | solution.py:100
  24.8 2.7 %collective-permute-start.3 = (bf16[128,512]{1,0:T(8,128)(2,1)S(1)}, bf16[128,512]{1,0:T(8,128)(2,1)S(1)}, u32[]{:S(2)}, u32[]{:S(2)}) collective-permute-start(bf16[128,512]{1,0:T(8,128)(2,1)S(1)} %collective-permute-done.2), channel_id=1, source_target_pairs={{0,56},{8,0},{16,8},{24,16},{32,24},{40,32},{48,40},{56,48},{1,57}... | collective-permute-start | bytes 393224 | tf_op jit(solution)/shard_map/ppermute | solution.py:100
  27.5 11.5 %collective-permute-done.6 = bf16[128,512]{1,0:T(8,128)(2,1)S(1)} collective-permute-done((bf16[128,512]{1,0:T(8,128)(2,1)S(1)}, bf16[128,512]{1,0:T(8,128)(2,1)S(1)}, u32[]{:S(2)}, u32[]{:S(2)}) %collective-permute-start.6) | collective-permute-done | bytes 131104 | tf_op jit(solution)/shard_map/ppermute | solution.py:99
  39.0 5.0 %collective-permute-done.7 = bf16[128,512]{1,0:T(8,128)(2,1)S(1)} collective-permute-done((bf16[128,512]{1,0:T(8,128)(2,1)S(1)}, bf16[128,512]{1,0:T(8,128)(2,1)S(1)}, u32[]{:S(2)}, u32[]{:S(2)}) %collective-permute-start.7) | collective-permute-done | bytes 131104 | tf_op jit(solution)/shard_map/ppermute | solution.py:104
  44.3 2.6 %collective-permute-start.8 = (bf16[8,128,512]{2,1,0:T(8,128)(2,1)S(1)}, bf16[8,128,512]{2,1,0:T(8,128)(2,1)S(1)}, u32[]{:S(2)}, u32[]{:S(2)}) collective-permute-start(bf16[8,128,512]{2,1,0:T(8,128)(2,1)S(1)} %bitcast_dynamic-update-slice_fusion.7), channel_id=1, source_target_pairs={{0,6},{2,0},{4,2},{6,4},{1,7},{3,1},{5,3},{7,5},{8,14},{10,8},{12,... | collective-permute-start | bytes 3145736 | tf_op jit(solution)/shard_map/ppermute | solution.py:100
  46.9 1.2 collective-permute-start.23
  48.1 1.5 %collective-permute-start.24 = (bf16[2048,256]{1,0:T(8,128)(2,1)S(1)}, bf16[2048,256]{1,0:T(8,128)(2,1)S(1)}, u32[]{:S(2)}, u32[]{:S(2)}) collective-permute-start(bf16[2048,256]{1,0:T(8,128)(2,1)S(1)} %copy-done), channel_id=1, source_target_pairs={{0,192},{64,0},{128,64},{192,128},{1,193},{65,1},{129,65},{193,129... | collective-permute-start | bytes 3145736 | tf_op jit(solution)/shard_map/ppermute | solution.py:123
  49.6 2.6 %collective-permute-done.16 = bf16[4,128,512]{2,1,0:T(8,128)(2,1)S(1)} collective-permute-done((bf16[4,128,512]{2,1,0:T(8,128)(2,1)S(1)}, bf16[4,128,512]{2,1,0:T(8,128)(2,1)S(1)}, u32[]{:S(2)}, u32[]{:S(2)}) %collective-permute-start.16) | collective-permute-done | bytes 524320 | tf_op jit(solution)/shard_map/ppermute | solution.py:100
  52.1 9.5 %collective-permute-done.19 = bf16[4,128,512]{2,1,0:T(8,128)(2,1)S(1)} collective-permute-done((bf16[4,128,512]{2,1,0:T(8,128)(2,1)S(1)}, bf16[4,128,512]{2,1,0:T(8,128)(2,1)S(1)}, u32[]{:S(2)}, u32[]{:S(2)}) %collective-permute-start.19) | collective-permute-done | bytes 524320 | tf_op jit(solution)/shard_map/ppermute | solution.py:99
  62.1 2.7 %collective-permute-done.9 = bf16[8,128,512]{2,1,0:T(8,128)(2,1)S(1)} collective-permute-done((bf16[8,128,512]{2,1,0:T(8,128)(2,1)S(1)}, bf16[8,128,512]{2,1,0:T(8,128)(2,1)S(1)}, u32[]{:S(2)}, u32[]{:S(2)}) %collective-permute-start.9) | collective-permute-done | bytes 1048608 | tf_op jit(solution)/shard_map/ppermute | solution.py:99
  64.8 1.2 collective-permute-start.20
  66.9 2.0 %collective-permute-start.11 = (bf16[4,128,512]{2,1,0:T(8,128)(2,1)S(1)}, bf16[4,128,512]{2,1,0:T(8,128)(2,1)S(1)}, u32[]{:S(2)}, u32[]{:S(2)}) collective-permute-start(bf16[4,128,512]{2,1,0:T(8,128)(2,1)S(1)} %slice.33), channel_id=1, source_target_pairs={{0,6},{2,0},{4,2},{6,4},{1,7},{3,1},{5,3},{7,5},{8,14},{10,8},{12,... | collective-permute-start | bytes 1572872 | tf_op jit(solution)/shard_map/ppermute | solution.py:109
  69.8 1.2 collective-permute-start.25
  71.9 2.1 %collective-permute-done.20 = bf16[4,128,512]{2,1,0:T(8,128)(2,1)S(1)} collective-permute-done((bf16[4,128,512]{2,1,0:T(8,128)(2,1)S(1)}, bf16[4,128,512]{2,1,0:T(8,128)(2,1)S(1)}, u32[]{:S(2)}, u32[]{:S(2)}) %collective-permute-start.20) | collective-permute-done | bytes 524320 | tf_op jit(solution)/shard_map/ppermute | solution.py:99
  74.1 2.5 %collective-permute-start.26 = (bf16[1024,256]{1,0:T(8,128)(2,1)}, bf16[1024,256]{1,0:T(8,128)(2,1)S(1)}, u32[]{:S(2)}, u32[]{:S(2)}) collective-permute-start(bf16[1024,256]{1,0:T(8,128)(2,1)} %slice.37), channel_id=1, source_target_pairs={{0,192},{64,0},{128,64},{192,128},{1,193},{65,1},{129,65},{193,129... | collective-permute-start | bytes 1572872 | tf_op jit(solution)/shard_map/ppermute | solution.py:133
  77.0 2.5 %collective-permute-start.22 = (bf16[2,128,512]{2,1,0:T(8,128)(2,1)S(1)}, bf16[2,128,512]{2,1,0:T(8,128)(2,1)S(1)}, u32[]{:S(2)}, u32[]{:S(2)}) collective-permute-start(bf16[2,128,512]{2,1,0:T(8,128)(2,1)S(1)} %slice.35), channel_id=1, source_target_pairs={{0,56},{8,0},{16,8},{24,16},{32,24},{40,32},{48,40},{56,48},{1,57}... | collective-permute-start | bytes 786440 | tf_op jit(solution)/shard_map/ppermute | solution.py:109
  80.2 4.2 %collective-permute-done.21 = bf16[2,128,512]{2,1,0:T(8,128)(2,1)S(1)} collective-permute-done((bf16[2,128,512]{2,1,0:T(8,128)(2,1)S(1)}, bf16[2,128,512]{2,1,0:T(8,128)(2,1)S(1)}, u32[]{:S(2)}, u32[]{:S(2)}) %collective-permute-start.21) | collective-permute-done | bytes 262176 | tf_op jit(solution)/shard_map/ppermute | solution.py:108
  84.5 2.7 %copy.6 = bf16[8,4,128,512]{3,2,1,0:T(8,128)(2,1)} copy(bf16[8,4,128,512]{3,2,0,1:T(8,128)(2,1)S(1)} %pad_maximum_fusion.1) | data formatting | bytes 8388608 | tf_op jit(solution)/shard_map/stack | solution.py:170
  87.8 7.5 %pad_maximum_fusion.rest_0_ = bf16[2,32,128,512]{3,2,1,0:T(8,128)(2,1)} fusion(bf16[1,32,128,512]{3,2,1,0:T(8,128)(2,1)} %bitcast.88, bf16[1,32,128,512]{3,2,1,0:T(8,128)(2,1)} %bitcast.87), kind=kLoop, calls=%fused_computation | loop fusion | flops 4194304 | bytes 16777216 | tf_op jit(solution)/shard_map/stack | solution.py:177
  96.9 11.7 %collective-permute-start.27 = (bf16[2,32,128,512]{3,2,1,0:T(8,128)(2,1)}, bf16[2,32,128,512]{3,2,1,0:T(8,128)(2,1)}, u32[]{:S(2)}, u32[]{:S(2)}) collective-permute-start(bf16[2,32,128,512]{3,2,1,0:T(8,128)(2,1)} %pad_maximum_fusion.rest_0_), channel_id=1, source_target_pairs={{0,1},{1,0},{2,3},{3,2},{4,5},{5,4},{6,7},{7,6},{8,9},{9,8},{10,11... | collective-permute-start | bytes 25165832 | tf_op jit(solution)/shard_map/ppermute | solution.py:181
  109.6 1.0 copy-done.2
  110.6 1.0 copy-done.4
  111.7 1.2 shard_map.55
  112.8 9.0 %collective-permute-done.27.rest_0_ = bf16[2,32,128,512]{3,2,1,0:T(8,128)(2,1)} collective-permute-done((bf16[2,32,128,512]{3,2,1,0:T(8,128)(2,1)}, bf16[2,32,128,512]{3,2,1,0:T(8,128)(2,1)}, u32[]{:S(2)}, u32[]{:S(2)}) %collective-permute-start.27) | collective-permute-done | bytes 8388640 | tf_op jit(solution)/shard_map/ppermute | solution.py:181
  121.8 5.3 %shard_map.56 = f32[4,128,128]{2,1,0:T(8,128)S(1)} custom-call(s32[4]{0:T(128)S(1)} %and_select_fusion.2.rows_ref, s32[4]{0:T(128)S(1)} %clamp_bitcast_fusion.cols_ref, s32[4]{0:T(128)S(1)} %get-tuple-element.17.use_ref, s32[5]{0:T(128)S(1)} %and_select_fusion.starts_ref, s32[2]{0:T(128)S(1)} %pad_add_fusion.place_ref, ...), custom_call_target="tpu_custom_call" | custom-call | flops 1073741824 | bytes 17039360 | tf_op jit(solution)/shard_map/pallas_call | solution.py:78
  (79 shorter events, 11.6 us)
Async XLA Ops:
  0.0 46.9 %copy-start = (bf16[2048,256]{1,0:T(8,128)(2,1)S(1)}, bf16[2048,256]{1,0:T(8,128)(2,1)}, u32[]{:S(2)}) copy-start(bf16[2048,256]{1,0:T(8,128)(2,1)} %param.6) | copy-start | bytes 3145732
  1.1 4.3 %collective-permute-start = (bf16[128,512]{1,0:T(8,128)(2,1)S(1)}, bf16[128,512]{1,0:T(8,128)(2,1)S(1)}, u32[]{:S(2)}, u32[]{:S(2)}) collective-permute-start(bf16[128,512]{1,0:T(8,128)(2,1)S(1)} %broadcast_select_fusion.2), channel_id=1, source_target_pairs={{0,1},{1,0},{2,3},{3,2},{4,5},{5,4},{6,7},{7,6},{8,9},{9,8},{10,11... | collective-permute-start | bytes 393224 | tf_op jit(solution)/shard_map/ppermute | solution.py:165
  6.4 7.9 %collective-permute-start.1 = (bf16[128,512]{1,0:T(8,128)(2,1)S(1)}, bf16[128,512]{1,0:T(8,128)(2,1)S(1)}, u32[]{:S(2)}, u32[]{:S(2)}) collective-permute-start(bf16[128,512]{1,0:T(8,128)(2,1)S(1)} %get-tuple-element.21), channel_id=1, source_target_pairs={{0,56},{8,0},{16,8},{24,16},{32,24},{40,32},{48,40},{56,48},{1,57}... | collective-permute-start | bytes 393224 | tf_op jit(solution)/shard_map/ppermute | solution.py:100
  10.3 6.6 %collective-permute-start.4 = (bf16[128,512]{1,0:T(8,128)(2,1)S(1)}, bf16[128,512]{1,0:T(8,128)(2,1)S(1)}, u32[]{:S(2)}, u32[]{:S(2)}) collective-permute-start(bf16[128,512]{1,0:T(8,128)(2,1)S(1)} %get-tuple-element.21), channel_id=1, source_target_pairs={{0,8},{8,16},{16,24},{24,32},{32,40},{40,48},{48,56},{56,0},{1,9},... | collective-permute-start | bytes 393224 | tf_op jit(solution)/shard_map/ppermute | solution.py:99
  11.3 5.8 %collective-permute-start.13 = (bf16[128,512]{1,0:T(8,128)(2,1)S(1)}, bf16[128,512]{1,0:T(8,128)(2,1)S(1)}, u32[]{:S(2)}, u32[]{:S(2)}) collective-permute-start(bf16[128,512]{1,0:T(8,128)(2,1)S(1)} %broadcast_select_fusion), channel_id=1, source_target_pairs={{0,2},{2,4},{4,6},{6,0},{1,3},{3,5},{5,7},{7,1},{8,10},{10,12},{12... | collective-permute-start | bytes 393224 | tf_op jit(solution)/shard_map/ppermute | solution.py:99
  12.7 4.9 %collective-permute-start.12 = (bf16[128,512]{1,0:T(8,128)(2,1)S(1)}, bf16[128,512]{1,0:T(8,128)(2,1)S(1)}, u32[]{:S(2)}, u32[]{:S(2)}) collective-permute-start(bf16[128,512]{1,0:T(8,128)(2,1)S(1)} %broadcast_select_fusion), channel_id=1, source_target_pairs={{0,6},{2,0},{4,2},{6,4},{1,7},{3,1},{5,3},{7,5},{8,14},{10,8},{12,... | collective-permute-start | bytes 393224 | tf_op jit(solution)/shard_map/ppermute | solution.py:100
  14.2 10.5 %collective-permute-start.2 = (bf16[128,512]{1,0:T(8,128)(2,1)S(1)}, bf16[128,512]{1,0:T(8,128)(2,1)S(1)}, u32[]{:S(2)}, u32[]{:S(2)}) collective-permute-start(bf16[128,512]{1,0:T(8,128)(2,1)S(1)} %collective-permute-done.1), channel_id=1, source_target_pairs={{0,56},{8,0},{16,8},{24,16},{32,24},{40,32},{48,40},{56,48},{1,57}... | collective-permute-start | bytes 393224 | tf_op jit(solution)/shard_map/ppermute | solution.py:100
  16.9 10.5 %collective-permute-start.5 = (bf16[128,512]{1,0:T(8,128)(2,1)S(1)}, bf16[128,512]{1,0:T(8,128)(2,1)S(1)}, u32[]{:S(2)}, u32[]{:S(2)}) collective-permute-start(bf16[128,512]{1,0:T(8,128)(2,1)S(1)} %collective-permute-done.4), channel_id=1, source_target_pairs={{0,8},{8,16},{16,24},{24,32},{32,40},{40,48},{48,56},{56,0},{1,9},... | collective-permute-start | bytes 393224 | tf_op jit(solution)/shard_map/ppermute | solution.py:99
  17.1 5.0 %collective-permute-start.14 = (bf16[128,512]{1,0:T(8,128)(2,1)S(1)}, bf16[128,512]{1,0:T(8,128)(2,1)S(1)}, u32[]{:S(2)}, u32[]{:S(2)}) collective-permute-start(bf16[128,512]{1,0:T(8,128)(2,1)S(1)} %collective-permute-done.13), channel_id=1, source_target_pairs={{0,2},{2,4},{4,6},{6,0},{1,3},{3,5},{5,7},{7,1},{8,10},{10,12},{12... | collective-permute-start | bytes 393224 | tf_op jit(solution)/shard_map/ppermute | solution.py:104
  22.2 21.8 %collective-permute-start.15 = (bf16[4,128,512]{2,1,0:T(8,128)(2,1)S(1)}, bf16[4,128,512]{2,1,0:T(8,128)(2,1)S(1)}, u32[]{:S(2)}, u32[]{:S(2)}) collective-permute-start(bf16[4,128,512]{2,1,0:T(8,128)(2,1)S(1)} %pad_maximum_fusion.2), channel_id=1, source_target_pairs={{0,56},{8,0},{16,8},{24,16},{32,24},{40,32},{48,40},{56,48},{1,57}... | collective-permute-start | bytes 1572872 | tf_op jit(solution)/shard_map/ppermute | solution.py:100
  24.8 23.4 %collective-permute-start.18 = (bf16[4,128,512]{2,1,0:T(8,128)(2,1)S(1)}, bf16[4,128,512]{2,1,0:T(8,128)(2,1)S(1)}, u32[]{:S(2)}, u32[]{:S(2)}) collective-permute-start(bf16[4,128,512]{2,1,0:T(8,128)(2,1)S(1)} %pad_maximum_fusion.2), channel_id=1, source_target_pairs={{0,8},{8,16},{16,24},{24,32},{32,40},{40,48},{48,56},{56,0},{1,9},... | collective-permute-start | bytes 1572872 | tf_op jit(solution)/shard_map/ppermute | solution.py:99
  24.8 14.2 %collective-permute-start.3 = (bf16[128,512]{1,0:T(8,128)(2,1)S(1)}, bf16[128,512]{1,0:T(8,128)(2,1)S(1)}, u32[]{:S(2)}, u32[]{:S(2)}) collective-permute-start(bf16[128,512]{1,0:T(8,128)(2,1)S(1)} %collective-permute-done.2), channel_id=1, source_target_pairs={{0,56},{8,0},{16,8},{24,16},{32,24},{40,32},{48,40},{56,48},{1,57}... | collective-permute-start | bytes 393224 | tf_op jit(solution)/shard_map/ppermute | solution.py:100
  27.4 11.5 %collective-permute-start.6 = (bf16[128,512]{1,0:T(8,128)(2,1)S(1)}, bf16[128,512]{1,0:T(8,128)(2,1)S(1)}, u32[]{:S(2)}, u32[]{:S(2)}) collective-permute-start(bf16[128,512]{1,0:T(8,128)(2,1)S(1)} %collective-permute-done.5), channel_id=1, source_target_pairs={{0,8},{8,16},{16,24},{24,32},{32,40},{40,48},{48,56},{56,0},{1,9},... | collective-permute-start | bytes 393224 | tf_op jit(solution)/shard_map/ppermute | solution.py:99
  38.9 5.0 %collective-permute-start.7 = (bf16[128,512]{1,0:T(8,128)(2,1)S(1)}, bf16[128,512]{1,0:T(8,128)(2,1)S(1)}, u32[]{:S(2)}, u32[]{:S(2)}) collective-permute-start(bf16[128,512]{1,0:T(8,128)(2,1)S(1)} %collective-permute-done.6), channel_id=1, source_target_pairs={{0,8},{8,16},{16,24},{24,32},{32,40},{40,48},{48,56},{56,0},{1,9},... | collective-permute-start | bytes 393224 | tf_op jit(solution)/shard_map/ppermute | solution.py:104
  44.0 8.1 %collective-permute-start.16 = (bf16[4,128,512]{2,1,0:T(8,128)(2,1)S(1)}, bf16[4,128,512]{2,1,0:T(8,128)(2,1)S(1)}, u32[]{:S(2)}, u32[]{:S(2)}) collective-permute-start(bf16[4,128,512]{2,1,0:T(8,128)(2,1)S(1)} %collective-permute-done.15), channel_id=1, source_target_pairs={{0,56},{8,0},{16,8},{24,16},{32,24},{40,32},{48,40},{56,48},{1,57}... | collective-permute-start | bytes 1572872 | tf_op jit(solution)/shard_map/ppermute | solution.py:100
  44.1 20.7 %collective-permute-start.9 = (bf16[8,128,512]{2,1,0:T(8,128)(2,1)S(1)}, bf16[8,128,512]{2,1,0:T(8,128)(2,1)S(1)}, u32[]{:S(2)}, u32[]{:S(2)}) collective-permute-start(bf16[8,128,512]{2,1,0:T(8,128)(2,1)S(1)} %bitcast_dynamic-update-slice_fusion.7), channel_id=1, source_target_pairs={{0,2},{2,4},{4,6},{6,0},{1,3},{3,5},{5,7},{7,1},{8,10},{10,12},{12... | collective-permute-start | bytes 3145736 | tf_op jit(solution)/shard_map/ppermute | solution.py:99
  44.3 21.7 %collective-permute-start.8 = (bf16[8,128,512]{2,1,0:T(8,128)(2,1)S(1)}, bf16[8,128,512]{2,1,0:T(8,128)(2,1)S(1)}, u32[]{:S(2)}, u32[]{:S(2)}) collective-permute-start(bf16[8,128,512]{2,1,0:T(8,128)(2,1)S(1)} %bitcast_dynamic-update-slice_fusion.7), channel_id=1, source_target_pairs={{0,6},{2,0},{4,2},{6,4},{1,7},{3,1},{5,3},{7,5},{8,14},{10,8},{12,... | collective-permute-start | bytes 3145736 | tf_op jit(solution)/shard_map/ppermute | solution.py:100
  46.9 20.0 %collective-permute-start.23 = (bf16[2048,256]{1,0:T(8,128)(2,1)S(1)}, bf16[2048,256]{1,0:T(8,128)(2,1)S(1)}, u32[]{:S(2)}, u32[]{:S(2)}) collective-permute-start(bf16[2048,256]{1,0:T(8,128)(2,1)S(1)} %copy-done), channel_id=1, source_target_pairs={{0,64},{64,128},{128,192},{192,0},{1,65},{65,129},{129,193},{193,1... | collective-permute-start | bytes 3145736 | tf_op jit(solution)/shard_map/ppermute | solution.py:122
  48.1 21.7 %collective-permute-start.24 = (bf16[2048,256]{1,0:T(8,128)(2,1)S(1)}, bf16[2048,256]{1,0:T(8,128)(2,1)S(1)}, u32[]{:S(2)}, u32[]{:S(2)}) collective-permute-start(bf16[2048,256]{1,0:T(8,128)(2,1)S(1)} %copy-done), channel_id=1, source_target_pairs={{0,192},{64,0},{128,64},{192,128},{1,193},{65,1},{129,65},{193,129... | collective-permute-start | bytes 3145736 | tf_op jit(solution)/shard_map/ppermute | solution.py:123
  52.1 9.5 %collective-permute-start.19 = (bf16[4,128,512]{2,1,0:T(8,128)(2,1)S(1)}, bf16[4,128,512]{2,1,0:T(8,128)(2,1)S(1)}, u32[]{:S(2)}, u32[]{:S(2)}) collective-permute-start(bf16[4,128,512]{2,1,0:T(8,128)(2,1)S(1)} %collective-permute-done.18), channel_id=1, source_target_pairs={{0,8},{8,16},{16,24},{24,32},{32,40},{40,48},{48,56},{56,0},{1,9},... | collective-permute-start | bytes 1572872 | tf_op jit(solution)/shard_map/ppermute | solution.py:99
  61.7 14.9 %collective-permute-start.17 = (bf16[4,128,512]{2,1,0:T(8,128)(2,1)S(1)}, bf16[4,128,512]{2,1,0:T(8,128)(2,1)S(1)}, u32[]{:S(2)}, u32[]{:S(2)}) collective-permute-start(bf16[4,128,512]{2,1,0:T(8,128)(2,1)S(1)} %collective-permute-done.16), channel_id=1, source_target_pairs={{0,56},{8,0},{16,8},{24,16},{32,24},{40,32},{48,40},{56,48},{1,57}... | collective-permute-start | bytes 1572872 | tf_op jit(solution)/shard_map/ppermute | solution.py:100
  64.8 9.2 %collective-permute-start.20 = (bf16[4,128,512]{2,1,0:T(8,128)(2,1)S(1)}, bf16[4,128,512]{2,1,0:T(8,128)(2,1)S(1)}, u32[]{:S(2)}, u32[]{:S(2)}) collective-permute-start(bf16[4,128,512]{2,1,0:T(8,128)(2,1)S(1)} %collective-permute-done.19), channel_id=1, source_target_pairs={{0,8},{8,16},{16,24},{24,32},{32,40},{40,48},{48,56},{56,0},{1,9},... | collective-permute-start | bytes 1572872 | tf_op jit(solution)/shard_map/ppermute | solution.py:99
  66.1 10.9 %collective-permute-start.10 = (bf16[4,128,512]{2,1,0:T(8,128)(2,1)S(1)}, bf16[4,128,512]{2,1,0:T(8,128)(2,1)S(1)}, u32[]{:S(2)}, u32[]{:S(2)}) collective-permute-start(bf16[4,128,512]{2,1,0:T(8,128)(2,1)S(1)} %slice.32), channel_id=1, source_target_pairs={{0,2},{2,4},{4,6},{6,0},{1,3},{3,5},{5,7},{7,1},{8,10},{10,12},{12... | collective-permute-start | bytes 1572872 | tf_op jit(solution)/shard_map/ppermute | solution.py:108
  66.9 12.5 %collective-permute-start.11 = (bf16[4,128,512]{2,1,0:T(8,128)(2,1)S(1)}, bf16[4,128,512]{2,1,0:T(8,128)(2,1)S(1)}, u32[]{:S(2)}, u32[]{:S(2)}) collective-permute-start(bf16[4,128,512]{2,1,0:T(8,128)(2,1)S(1)} %slice.33), channel_id=1, source_target_pairs={{0,6},{2,0},{4,2},{6,4},{1,7},{3,1},{5,3},{7,5},{8,14},{10,8},{12,... | collective-permute-start | bytes 1572872 | tf_op jit(solution)/shard_map/ppermute | solution.py:109
  69.8 25.5 %collective-permute-start.25 = (bf16[1024,256]{1,0:T(8,128)(2,1)}, bf16[1024,256]{1,0:T(8,128)(2,1)S(1)}, u32[]{:S(2)}, u32[]{:S(2)}) collective-permute-start(bf16[1024,256]{1,0:T(8,128)(2,1)} %slice.36), channel_id=1, source_target_pairs={{0,64},{64,128},{128,192},{192,0},{1,65},{65,129},{129,193},{193,1... | collective-permute-start | bytes 1572872 | tf_op jit(solution)/shard_map/ppermute | solution.py:132
  74.1 22.1 %collective-permute-start.26 = (bf16[1024,256]{1,0:T(8,128)(2,1)}, bf16[1024,256]{1,0:T(8,128)(2,1)S(1)}, u32[]{:S(2)}, u32[]{:S(2)}) collective-permute-start(bf16[1024,256]{1,0:T(8,128)(2,1)} %slice.37), channel_id=1, source_target_pairs={{0,192},{64,0},{128,64},{192,128},{1,193},{65,1},{129,65},{193,129... | collective-permute-start | bytes 1572872 | tf_op jit(solution)/shard_map/ppermute | solution.py:133
  76.6 7.8 %collective-permute-start.21 = (bf16[2,128,512]{2,1,0:T(8,128)(2,1)S(1)}, bf16[2,128,512]{2,1,0:T(8,128)(2,1)S(1)}, u32[]{:S(2)}, u32[]{:S(2)}) collective-permute-start(bf16[2,128,512]{2,1,0:T(8,128)(2,1)S(1)} %slice.34), channel_id=1, source_target_pairs={{0,8},{8,16},{16,24},{24,32},{32,40},{40,48},{48,56},{56,0},{1,9},... | collective-permute-start | bytes 786440 | tf_op jit(solution)/shard_map/ppermute | solution.py:108
  77.0 7.4 %collective-permute-start.22 = (bf16[2,128,512]{2,1,0:T(8,128)(2,1)S(1)}, bf16[2,128,512]{2,1,0:T(8,128)(2,1)S(1)}, u32[]{:S(2)}, u32[]{:S(2)}) collective-permute-start(bf16[2,128,512]{2,1,0:T(8,128)(2,1)S(1)} %slice.35), channel_id=1, source_target_pairs={{0,56},{8,0},{16,8},{24,16},{32,24},{40,32},{48,40},{56,48},{1,57}... | collective-permute-start | bytes 786440 | tf_op jit(solution)/shard_map/ppermute | solution.py:109
  84.5 3.3 %copy-start.5 = (bf16[8,4,128,512]{3,2,1,0:T(8,128)(2,1)}, bf16[8,4,128,512]{3,2,1,0:T(8,128)(2,1)S(1)}, u32[]{:S(2)}) copy-start(bf16[8,4,128,512]{3,2,1,0:T(8,128)(2,1)S(1)} %bitcast_dynamic-update-slice_fusion) | copy-start | bytes 12582916
  87.8 21.7 %copy-start.6 = (s32[1,1,4]{2,1,0:T(1,128)S(1)}, s32[1,1,4]{2,1,0:T(1,128)}, u32[]{:S(2)}) copy-start(s32[1,1,4]{2,1,0:T(1,128)} %param.7) | copy-start | bytes 52
  87.8 21.8 %copy-start.7 = (s32[1,1,4]{2,1,0:T(1,128)S(1)}, s32[1,1,4]{2,1,0:T(1,128)}, u32[]{:S(2)}) copy-start(s32[1,1,4]{2,1,0:T(1,128)} %param.8) | copy-start | bytes 52
  96.9 24.9 %collective-permute-start.27 = (bf16[2,32,128,512]{3,2,1,0:T(8,128)(2,1)}, bf16[2,32,128,512]{3,2,1,0:T(8,128)(2,1)}, u32[]{:S(2)}, u32[]{:S(2)}) collective-permute-start(bf16[2,32,128,512]{3,2,1,0:T(8,128)(2,1)} %pad_maximum_fusion.rest_0_), channel_id=1, source_target_pairs={{0,1},{1,0},{2,3},{3,2},{4,5},{5,4},{6,7},{7,6},{8,9},{9,8},{10,11... | collective-permute-start | bytes 25165832 | tf_op jit(solution)/shard_map/ppermute | solution.py:181
  (4 other events, 3.7 us)

commit v3 on v0

--- a/solution.py
+++ b/solution.py
@@ -63,7 +63,7 @@
                 )
 
             out_ref[s] = lax.fori_loop(
-                0, chunks, body, jnp.zeros((BLK, BLK), jnp.float32), unroll=2
+                0, chunks, body, jnp.zeros((BLK, BLK), jnp.float32), unroll=8
             )
 
 
@@ -90,7 +90,7 @@
     )(local_rows, local_cols, use, starts, place, first, second, *grad_pieces)
 
 
-def relative_gather(x, axis, n):
+def relative_gather(x, axis, n, split=True):
     right = [(k, (k + 1) % n) for k in range(n)]
     left = [(k, (k - 1) % n) for k in range(n)]
     rel = [x] + [None] * (n - 1)
@@ -100,7 +100,9 @@
         from_right = lax.ppermute(from_right, axis, left)
         rel[n - t] = from_left
         rel[t] = from_right
-    if n % 2 == 0 and n > 1:
+    if n % 2 == 0 and n > 1 and not split:
+        rel[n // 2] = lax.ppermute(from_left, axis, right)
+    elif n % 2 == 0 and n > 1:
         t = n // 2
         half = x.shape[0] // 2
         near_a = lax.ppermute(from_left[:half], axis, right)
@@ -164,9 +166,9 @@
     lead = jnp.where(on_first, keep, recv)
     trail = jnp.where(on_first, recv, keep)
 
-    lead_z = jnp.stack(relative_gather(lead, "z", nz), 0)
+    lead_z = jnp.stack(relative_gather(lead, "z", nz, split=False), 0)
     lead_all = jnp.stack(relative_gather(lead_z, "y", ny), 1)
-    trail_y = jnp.stack(relative_gather(trail, "y", ny), 0)
+    trail_y = jnp.stack(relative_gather(trail, "y", ny, split=False), 0)
     trail_all = jnp.stack(relative_gather(trail_y, "z", nz), 0)
     lead_all = lead_all.reshape(nz * ny, tok, width)
     trail_all = trail_all.reshape(nz * ny, tok, width)

time: 125 us -> 122 us (0.976)
  the two profiles are of different devices: /device:TPU:6 before, /device:TPU:1 now
where the time goes in v3:
time: 122 us; the launch traced here: 121 us
  waiting for transfers between devices  54.2 us (44%)
  starting transfers between devices  43.1 us (35%)
  local copies, waits for them, and re-layouts  11.4 us (9%)
  other arithmetic  6.38 us (5%)
  Pallas kernels  5.01 us (4%)
    ppermute x8, waiting for transfers between devices, relative_gather(): from_left = lax.ppermute(from_left, axis, right)  22.5 us
    ppermute x8, starting transfers between devices, relative_gather(): from_right = lax.ppermute(from_right, axis, left)  15.5 us
    ppermute x1, starting transfers between devices, on_device(): lead_other = lax.ppermute(lead_all, 'core', swap)  11.7 us
    ppermute x2, waiting for transfers between devices, relative_gather(): rel[n // 2] = lax.ppermute(from_left, axis, right)  9.55 us
    unnamed x25, local copies, waits for them, and re-layouts  7.89 us
    ppermute x1, waiting for transfers between devices, on_device(): trail_other = lax.ppermute(trail_all, 'core', swap)  6 us
    ppermute x8, waiting for transfers between devices, relative_gather(): from_right = lax.ppermute(from_right, axis, left)  5.21 us
    pallas_call x2, Pallas kernels, block_products(): pl.pallas_call(functools.partial(block_kernel, n_grad, ny), out_shape=jax...  5.01 us
  transfers between devices with their start and end apart: 29, of which 15 were waited for; matrix products, arithmetic and copies ran while one was open for 9% of the time, Pallas kernels for 1%

profile of v3, /device:TPU:1, one launch (start us, length us, event | category | flops | bytes accessed | tf_op | source)
XLA Modules:
  0.0 121.0 jit_solution(12838102445929764052)
XLA Ops:
  0.0 1.1 broadcast_select_fusion.2
  1.1 3.3 %collective-permute-start = (bf16[128,512]{1,0:T(8,128)(2,1)S(1)}, bf16[128,512]{1,0:T(8,128)(2,1)S(1)}, u32[]{:S(2)}, u32[]{:S(2)}) collective-permute-start(bf16[128,512]{1,0:T(8,128)(2,1)S(1)} %broadcast_select_fusion.2), channel_id=1, source_target_pairs={{0,1},{1,0},{2,3},{3,2},{4,5},{5,4},{6,7},{7,6},{8,9},{9,8},{10,11... | collective-permute-start | bytes 393224 | tf_op jit(solution)/shard_map/ppermute | solution.py:165
  6.4 3.9 %collective-permute-start.1 = (bf16[128,512]{1,0:T(8,128)(2,1)S(1)}, bf16[128,512]{1,0:T(8,128)(2,1)S(1)}, u32[]{:S(2)}, u32[]{:S(2)}) collective-permute-start(bf16[128,512]{1,0:T(8,128)(2,1)S(1)} %get-tuple-element.23), channel_id=1, source_target_pairs={{0,56},{8,0},{16,8},{24,16},{32,24},{40,32},{48,40},{56,48},{1,57}... | collective-permute-start | bytes 393224 | tf_op jit(solution)/shard_map/ppermute | solution.py:100
  11.3 1.4 %collective-permute-start.13 = (bf16[128,512]{1,0:T(8,128)(2,1)S(1)}, bf16[128,512]{1,0:T(8,128)(2,1)S(1)}, u32[]{:S(2)}, u32[]{:S(2)}) collective-permute-start(bf16[128,512]{1,0:T(8,128)(2,1)S(1)} %broadcast_select_fusion), channel_id=1, source_target_pairs={{0,2},{2,4},{4,6},{6,0},{1,3},{3,5},{5,7},{7,1},{8,10},{10,12},{12... | collective-permute-start | bytes 393224 | tf_op jit(solution)/shard_map/ppermute | solution.py:99
  12.7 1.5 %collective-permute-start.12 = (bf16[128,512]{1,0:T(8,128)(2,1)S(1)}, bf16[128,512]{1,0:T(8,128)(2,1)S(1)}, u32[]{:S(2)}, u32[]{:S(2)}) collective-permute-start(bf16[128,512]{1,0:T(8,128)(2,1)S(1)} %broadcast_select_fusion), channel_id=1, source_target_pairs={{0,6},{2,0},{4,2},{6,4},{1,7},{3,1},{5,3},{7,5},{8,14},{10,8},{12,... | collective-permute-start | bytes 393224 | tf_op jit(solution)/shard_map/ppermute | solution.py:100
  14.2 2.7 %collective-permute-start.2 = (bf16[128,512]{1,0:T(8,128)(2,1)S(1)}, bf16[128,512]{1,0:T(8,128)(2,1)S(1)}, u32[]{:S(2)}, u32[]{:S(2)}) collective-permute-start(bf16[128,512]{1,0:T(8,128)(2,1)S(1)} %collective-permute-done.1), channel_id=1, source_target_pairs={{0,56},{8,0},{16,8},{24,16},{32,24},{40,32},{48,40},{56,48},{1,57}... | collective-permute-start | bytes 393224 | tf_op jit(solution)/shard_map/ppermute | solution.py:100
  17.6 4.5 %collective-permute-done.14 = bf16[128,512]{1,0:T(8,128)(2,1)S(1)} collective-permute-done((bf16[128,512]{1,0:T(8,128)(2,1)S(1)}, bf16[128,512]{1,0:T(8,128)(2,1)S(1)}, u32[]{:S(2)}, u32[]{:S(2)}) %collective-permute-start.14) | collective-permute-done | bytes 131104 | tf_op jit(solution)/shard_map/ppermute | solution.py:104
  22.2 2.5 %collective-permute-start.15 = (bf16[4,128,512]{2,1,0:T(8,128)(2,1)S(1)}, bf16[4,128,512]{2,1,0:T(8,128)(2,1)S(1)}, u32[]{:S(2)}, u32[]{:S(2)}) collective-permute-start(bf16[4,128,512]{2,1,0:T(8,128)(2,1)S(1)} %pad_maximum_fusion.1), channel_id=1, source_target_pairs={{0,56},{8,0},{16,8},{24,16},{32,24},{40,32},{48,40},{56,48},{1,57}... | collective-permute-start | bytes 1572872 | tf_op jit(solution)/shard_map/ppermute | solution.py:100
  24.8 2.7 %collective-permute-start.3 = (bf16[128,512]{1,0:T(8,128)(2,1)S(1)}, bf16[128,512]{1,0:T(8,128)(2,1)S(1)}, u32[]{:S(2)}, u32[]{:S(2)}) collective-permute-start(bf16[128,512]{1,0:T(8,128)(2,1)S(1)} %collective-permute-done.2), channel_id=1, source_target_pairs={{0,56},{8,0},{16,8},{24,16},{32,24},{40,32},{48,40},{56,48},{1,57}... | collective-permute-start | bytes 393224 | tf_op jit(solution)/shard_map/ppermute | solution.py:100
  27.5 11.5 %collective-permute-done.6 = bf16[128,512]{1,0:T(8,128)(2,1)S(1)} collective-permute-done((bf16[128,512]{1,0:T(8,128)(2,1)S(1)}, bf16[128,512]{1,0:T(8,128)(2,1)S(1)}, u32[]{:S(2)}, u32[]{:S(2)}) %collective-permute-start.6) | collective-permute-done | bytes 131104 | tf_op jit(solution)/shard_map/ppermute | solution.py:99
  39.0 5.0 %collective-permute-done.7 = bf16[128,512]{1,0:T(8,128)(2,1)S(1)} collective-permute-done((bf16[128,512]{1,0:T(8,128)(2,1)S(1)}, bf16[128,512]{1,0:T(8,128)(2,1)S(1)}, u32[]{:S(2)}, u32[]{:S(2)}) %collective-permute-start.7) | collective-permute-done | bytes 131104 | tf_op jit(solution)/shard_map/ppermute | solution.py:104
  44.1 1.6 %collective-permute-start.8 = (bf16[8,128,512]{2,1,0:T(8,128)(2,1)S(1)}, bf16[8,128,512]{2,1,0:T(8,128)(2,1)S(1)}, u32[]{:S(2)}, u32[]{:S(2)}) collective-permute-start(bf16[8,128,512]{2,1,0:T(8,128)(2,1)S(1)} %bitcast_dynamic-update-slice_fusion.7), channel_id=1, source_target_pairs={{0,6},{2,0},{4,2},{6,4},{1,7},{3,1},{5,3},{7,5},{8,14},{10,8},{12,... | collective-permute-start | bytes 3145736 | tf_op jit(solution)/shard_map/ppermute | solution.py:100
  45.8 1.2 %collective-permute-start.23 = (bf16[2048,256]{1,0:T(8,128)(2,1)S(1)}, bf16[2048,256]{1,0:T(8,128)(2,1)S(1)}, u32[]{:S(2)}, u32[]{:S(2)}) collective-permute-start(bf16[2048,256]{1,0:T(8,128)(2,1)S(1)} %copy-done), channel_id=1, source_target_pairs={{0,64},{64,128},{128,192},{192,0},{1,65},{65,129},{129,193},{193,1... | collective-permute-start | bytes 3145736 | tf_op jit(solution)/shard_map/ppermute | solution.py:122
  47.0 1.5 %collective-permute-start.24 = (bf16[2048,256]{1,0:T(8,128)(2,1)S(1)}, bf16[2048,256]{1,0:T(8,128)(2,1)S(1)}, u32[]{:S(2)}, u32[]{:S(2)}) collective-permute-start(bf16[2048,256]{1,0:T(8,128)(2,1)S(1)} %copy-done), channel_id=1, source_target_pairs={{0,192},{64,0},{128,64},{192,128},{1,193},{65,1},{129,65},{193,129... | collective-permute-start | bytes 3145736 | tf_op jit(solution)/shard_map/ppermute | solution.py:123
  48.5 3.7 %collective-permute-done.16 = bf16[4,128,512]{2,1,0:T(8,128)(2,1)S(1)} collective-permute-done((bf16[4,128,512]{2,1,0:T(8,128)(2,1)S(1)}, bf16[4,128,512]{2,1,0:T(8,128)(2,1)S(1)}, u32[]{:S(2)}, u32[]{:S(2)}) %collective-permute-start.16) | collective-permute-done | bytes 524320 | tf_op jit(solution)/shard_map/ppermute | solution.py:100
  52.1 9.5 %collective-permute-done.19 = bf16[4,128,512]{2,1,0:T(8,128)(2,1)S(1)} collective-permute-done((bf16[4,128,512]{2,1,0:T(8,128)(2,1)S(1)}, bf16[4,128,512]{2,1,0:T(8,128)(2,1)S(1)}, u32[]{:S(2)}, u32[]{:S(2)}) %collective-permute-start.19) | collective-permute-done | bytes 524320 | tf_op jit(solution)/shard_map/ppermute | solution.py:99
  62.1 1.5 %collective-permute-done.8 = bf16[8,128,512]{2,1,0:T(8,128)(2,1)S(1)} collective-permute-done((bf16[8,128,512]{2,1,0:T(8,128)(2,1)S(1)}, bf16[8,128,512]{2,1,0:T(8,128)(2,1)S(1)}, u32[]{:S(2)}, u32[]{:S(2)}) %collective-permute-start.8) | collective-permute-done | bytes 1048608 | tf_op jit(solution)/shard_map/ppermute | solution.py:100
  63.6 1.2 collective-permute-start.20
  66.5 2.4 %collective-permute-start.11 = (bf16[4,128,512]{2,1,0:T(8,128)(2,1)S(1)}, bf16[4,128,512]{2,1,0:T(8,128)(2,1)S(1)}, u32[]{:S(2)}, u32[]{:S(2)}) collective-permute-start(bf16[4,128,512]{2,1,0:T(8,128)(2,1)S(1)} %slice.33), channel_id=1, source_target_pairs={{0,6},{2,0},{4,2},{6,4},{1,7},{3,1},{5,3},{7,5},{8,14},{10,8},{12,... | collective-permute-start | bytes 1572872 | tf_op jit(solution)/shard_map/ppermute | solution.py:109
  69.9 1.3 %collective-permute-start.25 = (bf16[1024,256]{1,0:T(8,128)(2,1)S(1)}, bf16[1024,256]{1,0:T(8,128)(2,1)S(1)}, u32[]{:S(2)}, u32[]{:S(2)}) collective-permute-start(bf16[1024,256]{1,0:T(8,128)(2,1)S(1)} %slice.36), channel_id=1, source_target_pairs={{0,64},{64,128},{128,192},{192,0},{1,65},{65,129},{129,193},{193,1... | collective-permute-start | bytes 1572872 | tf_op jit(solution)/shard_map/ppermute | solution.py:132
  72.1 1.5 %collective-permute-start.26 = (bf16[1024,256]{1,0:T(8,128)(2,1)S(1)}, bf16[1024,256]{1,0:T(8,128)(2,1)S(1)}, u32[]{:S(2)}, u32[]{:S(2)}) collective-permute-start(bf16[1024,256]{1,0:T(8,128)(2,1)S(1)} %slice.37), channel_id=1, source_target_pairs={{0,192},{64,0},{128,64},{192,128},{1,193},{65,1},{129,65},{193,129... | collective-permute-start | bytes 1572872 | tf_op jit(solution)/shard_map/ppermute | solution.py:133
  73.9 1.2 %collective-permute-start.22 = (bf16[2,128,512]{2,1,0:T(8,128)(2,1)S(1)}, bf16[2,128,512]{2,1,0:T(8,128)(2,1)S(1)}, u32[]{:S(2)}, u32[]{:S(2)}) collective-permute-start(bf16[2,128,512]{2,1,0:T(8,128)(2,1)S(1)} %slice.35), channel_id=1, source_target_pairs={{0,56},{8,0},{16,8},{24,16},{32,24},{40,32},{48,40},{56,48},{1,57}... | collective-permute-start | bytes 786440 | tf_op jit(solution)/shard_map/ppermute | solution.py:109
  76.5 2.1 %collective-permute-done.10 = bf16[4,128,512]{2,1,0:T(8,128)(2,1)S(1)} collective-permute-done((bf16[4,128,512]{2,1,0:T(8,128)(2,1)S(1)}, bf16[4,128,512]{2,1,0:T(8,128)(2,1)S(1)}, u32[]{:S(2)}, u32[]{:S(2)}) %collective-permute-start.10) | collective-permute-done | bytes 524320 | tf_op jit(solution)/shard_map/ppermute | solution.py:108
  79.3 2.4 %collective-permute-done.22 = bf16[2,128,512]{2,1,0:T(8,128)(2,1)S(1)} collective-permute-done((bf16[2,128,512]{2,1,0:T(8,128)(2,1)S(1)}, bf16[2,128,512]{2,1,0:T(8,128)(2,1)S(1)}, u32[]{:S(2)}, u32[]{:S(2)}) %collective-permute-start.22) | collective-permute-done | bytes 262176 | tf_op jit(solution)/shard_map/ppermute | solution.py:109
  81.7 2.5 %collective-permute-done.21 = bf16[2,128,512]{2,1,0:T(8,128)(2,1)S(1)} collective-permute-done((bf16[2,128,512]{2,1,0:T(8,128)(2,1)S(1)}, bf16[2,128,512]{2,1,0:T(8,128)(2,1)S(1)}, u32[]{:S(2)}, u32[]{:S(2)}) %collective-permute-start.21) | collective-permute-done | bytes 262176 | tf_op jit(solution)/shard_map/ppermute | solution.py:108
  85.9 2.4 %copy.6 = bf16[8,4,128,512]{3,2,1,0:T(8,128)(2,1)} copy(bf16[8,4,128,512]{3,2,0,1:T(8,128)(2,1)S(1)} %pad_maximum_fusion) | data formatting | bytes 8388608 | tf_op jit(solution)/shard_map/stack | solution.py:170
  91.6 11.7 %collective-permute-start.27 = (bf16[32,128,512]{2,1,0:T(8,128)(2,1)}, bf16[32,128,512]{2,1,0:T(8,128)(2,1)}, u32[]{:S(2)}, u32[]{:S(2)}) collective-permute-start(bf16[32,128,512]{2,1,0:T(8,128)(2,1)} %bitcast.22.rest_0_), channel_id=1, source_target_pairs={{0,1},{1,0},{2,3},{3,2},{4,5},{5,4},{6,7},{7,6},{8,9},{9,8},{10,11... | collective-permute-start | bytes 12582920 | tf_op jit(solution)/shard_map/ppermute | solution.py:180
  105.3 1.0 copy-done.4
  106.3 1.2 shard_map.55
  107.5 3.0 %collective-permute-done.27.rest_0_ = bf16[32,128,512]{2,1,0:T(8,128)(2,1)} collective-permute-done((bf16[32,128,512]{2,1,0:T(8,128)(2,1)}, bf16[32,128,512]{2,1,0:T(8,128)(2,1)}, u32[]{:S(2)}, u32[]{:S(2)}) %collective-permute-start.27) | collective-permute-done | bytes 4194336 | tf_op jit(solution)/shard_map/ppermute | solution.py:180
  110.4 6.0 %collective-permute-done.28.rest_1_ = bf16[32,128,512]{2,1,0:T(8,128)(2,1)} collective-permute-done((bf16[32,128,512]{2,1,0:T(8,128)(2,1)}, bf16[32,128,512]{2,1,0:T(8,128)(2,1)}, u32[]{:S(2)}, u32[]{:S(2)}) %collective-permute-start.28) | collective-permute-done | bytes 4194336 | tf_op jit(solution)/shard_map/ppermute | solution.py:181
  116.4 3.9 %shard_map.56 = f32[4,128,128]{2,1,0:T(8,128)S(1)} custom-call(s32[4]{0:T(128)S(1)} %and_select_fusion.2.rows_ref, s32[4]{0:T(128)S(1)} %clamp_bitcast_fusion.cols_ref, s32[4]{0:T(128)S(1)} %get-tuple-element.19.use_ref, s32[5]{0:T(128)S(1)} %and_select_fusion.starts_ref, s32[2]{0:T(128)S(1)} %pad_add_fusion.place_ref, ...), custom_call_target="tpu_custom_call" | custom-call | flops 1073741824 | bytes 17039360 | tf_op jit(solution)/shard_map/pallas_call | solution.py:78
  (78 shorter events, 17.2 us)
Async XLA Ops:
  0.0 45.8 %copy-start = (bf16[2048,256]{1,0:T(8,128)(2,1)S(1)}, bf16[2048,256]{1,0:T(8,128)(2,1)}, u32[]{:S(2)}) copy-start(bf16[2048,256]{1,0:T(8,128)(2,1)} %param.6) | copy-start | bytes 3145732
  1.1 4.3 %collective-permute-start = (bf16[128,512]{1,0:T(8,128)(2,1)S(1)}, bf16[128,512]{1,0:T(8,128)(2,1)S(1)}, u32[]{:S(2)}, u32[]{:S(2)}) collective-permute-start(bf16[128,512]{1,0:T(8,128)(2,1)S(1)} %broadcast_select_fusion.2), channel_id=1, source_target_pairs={{0,1},{1,0},{2,3},{3,2},{4,5},{5,4},{6,7},{7,6},{8,9},{9,8},{10,11... | collective-permute-start | bytes 393224 | tf_op jit(solution)/shard_map/ppermute | solution.py:165
  6.4 7.9 %collective-permute-start.1 = (bf16[128,512]{1,0:T(8,128)(2,1)S(1)}, bf16[128,512]{1,0:T(8,128)(2,1)S(1)}, u32[]{:S(2)}, u32[]{:S(2)}) collective-permute-start(bf16[128,512]{1,0:T(8,128)(2,1)S(1)} %get-tuple-element.23), channel_id=1, source_target_pairs={{0,56},{8,0},{16,8},{24,16},{32,24},{40,32},{48,40},{56,48},{1,57}... | collective-permute-start | bytes 393224 | tf_op jit(solution)/shard_map/ppermute | solution.py:100
  10.3 6.6 %collective-permute-start.4 = (bf16[128,512]{1,0:T(8,128)(2,1)S(1)}, bf16[128,512]{1,0:T(8,128)(2,1)S(1)}, u32[]{:S(2)}, u32[]{:S(2)}) collective-permute-start(bf16[128,512]{1,0:T(8,128)(2,1)S(1)} %get-tuple-element.23), channel_id=1, source_target_pairs={{0,8},{8,16},{16,24},{24,32},{32,40},{40,48},{48,56},{56,0},{1,9},... | collective-permute-start | bytes 393224 | tf_op jit(solution)/shard_map/ppermute | solution.py:99
  11.3 5.8 %collective-permute-start.13 = (bf16[128,512]{1,0:T(8,128)(2,1)S(1)}, bf16[128,512]{1,0:T(8,128)(2,1)S(1)}, u32[]{:S(2)}, u32[]{:S(2)}) collective-permute-start(bf16[128,512]{1,0:T(8,128)(2,1)S(1)} %broadcast_select_fusion), channel_id=1, source_target_pairs={{0,2},{2,4},{4,6},{6,0},{1,3},{3,5},{5,7},{7,1},{8,10},{10,12},{12... | collective-permute-start | bytes 393224 | tf_op jit(solution)/shard_map/ppermute | solution.py:99
  12.7 4.9 %collective-permute-start.12 = (bf16[128,512]{1,0:T(8,128)(2,1)S(1)}, bf16[128,512]{1,0:T(8,128)(2,1)S(1)}, u32[]{:S(2)}, u32[]{:S(2)}) collective-permute-start(bf16[128,512]{1,0:T(8,128)(2,1)S(1)} %broadcast_select_fusion), channel_id=1, source_target_pairs={{0,6},{2,0},{4,2},{6,4},{1,7},{3,1},{5,3},{7,5},{8,14},{10,8},{12,... | collective-permute-start | bytes 393224 | tf_op jit(solution)/shard_map/ppermute | solution.py:100
  14.2 10.5 %collective-permute-start.2 = (bf16[128,512]{1,0:T(8,128)(2,1)S(1)}, bf16[128,512]{1,0:T(8,128)(2,1)S(1)}, u32[]{:S(2)}, u32[]{:S(2)}) collective-permute-start(bf16[128,512]{1,0:T(8,128)(2,1)S(1)} %collective-permute-done.1), channel_id=1, source_target_pairs={{0,56},{8,0},{16,8},{24,16},{32,24},{40,32},{48,40},{56,48},{1,57}... | collective-permute-start | bytes 393224 | tf_op jit(solution)/shard_map/ppermute | solution.py:100
  16.9 10.5 %collective-permute-start.5 = (bf16[128,512]{1,0:T(8,128)(2,1)S(1)}, bf16[128,512]{1,0:T(8,128)(2,1)S(1)}, u32[]{:S(2)}, u32[]{:S(2)}) collective-permute-start(bf16[128,512]{1,0:T(8,128)(2,1)S(1)} %collective-permute-done.4), channel_id=1, source_target_pairs={{0,8},{8,16},{16,24},{24,32},{32,40},{40,48},{48,56},{56,0},{1,9},... | collective-permute-start | bytes 393224 | tf_op jit(solution)/shard_map/ppermute | solution.py:99
  17.1 5.0 %collective-permute-start.14 = (bf16[128,512]{1,0:T(8,128)(2,1)S(1)}, bf16[128,512]{1,0:T(8,128)(2,1)S(1)}, u32[]{:S(2)}, u32[]{:S(2)}) collective-permute-start(bf16[128,512]{1,0:T(8,128)(2,1)S(1)} %collective-permute-done.13), channel_id=1, source_target_pairs={{0,2},{2,4},{4,6},{6,0},{1,3},{3,5},{5,7},{7,1},{8,10},{10,12},{12... | collective-permute-start | bytes 393224 | tf_op jit(solution)/shard_map/ppermute | solution.py:104
  22.2 21.8 %collective-permute-start.15 = (bf16[4,128,512]{2,1,0:T(8,128)(2,1)S(1)}, bf16[4,128,512]{2,1,0:T(8,128)(2,1)S(1)}, u32[]{:S(2)}, u32[]{:S(2)}) collective-permute-start(bf16[4,128,512]{2,1,0:T(8,128)(2,1)S(1)} %pad_maximum_fusion.1), channel_id=1, source_target_pairs={{0,56},{8,0},{16,8},{24,16},{32,24},{40,32},{48,40},{56,48},{1,57}... | collective-permute-start | bytes 1572872 | tf_op jit(solution)/shard_map/ppermute | solution.py:100
  24.8 22.2 %collective-permute-start.18 = (bf16[4,128,512]{2,1,0:T(8,128)(2,1)S(1)}, bf16[4,128,512]{2,1,0:T(8,128)(2,1)S(1)}, u32[]{:S(2)}, u32[]{:S(2)}) collective-permute-start(bf16[4,128,512]{2,1,0:T(8,128)(2,1)S(1)} %pad_maximum_fusion.1), channel_id=1, source_target_pairs={{0,8},{8,16},{16,24},{24,32},{32,40},{40,48},{48,56},{56,0},{1,9},... | collective-permute-start | bytes 1572872 | tf_op jit(solution)/shard_map/ppermute | solution.py:99
  24.8 14.2 %collective-permute-start.3 = (bf16[128,512]{1,0:T(8,128)(2,1)S(1)}, bf16[128,512]{1,0:T(8,128)(2,1)S(1)}, u32[]{:S(2)}, u32[]{:S(2)}) collective-permute-start(bf16[128,512]{1,0:T(8,128)(2,1)S(1)} %collective-permute-done.2), channel_id=1, source_target_pairs={{0,56},{8,0},{16,8},{24,16},{32,24},{40,32},{48,40},{56,48},{1,57}... | collective-permute-start | bytes 393224 | tf_op jit(solution)/shard_map/ppermute | solution.py:100
  27.4 11.5 %collective-permute-start.6 = (bf16[128,512]{1,0:T(8,128)(2,1)S(1)}, bf16[128,512]{1,0:T(8,128)(2,1)S(1)}, u32[]{:S(2)}, u32[]{:S(2)}) collective-permute-start(bf16[128,512]{1,0:T(8,128)(2,1)S(1)} %collective-permute-done.5), channel_id=1, source_target_pairs={{0,8},{8,16},{16,24},{24,32},{32,40},{40,48},{48,56},{56,0},{1,9},... | collective-permute-start | bytes 393224 | tf_op jit(solution)/shard_map/ppermute | solution.py:99
  38.9 5.0 %collective-permute-start.7 = (bf16[128,512]{1,0:T(8,128)(2,1)S(1)}, bf16[128,512]{1,0:T(8,128)(2,1)S(1)}, u32[]{:S(2)}, u32[]{:S(2)}) collective-permute-start(bf16[128,512]{1,0:T(8,128)(2,1)S(1)} %collective-permute-done.6), channel_id=1, source_target_pairs={{0,8},{8,16},{16,24},{24,32},{32,40},{40,48},{48,56},{56,0},{1,9},... | collective-permute-start | bytes 393224 | tf_op jit(solution)/shard_map/ppermute | solution.py:104
  44.0 8.1 %collective-permute-start.16 = (bf16[4,128,512]{2,1,0:T(8,128)(2,1)S(1)}, bf16[4,128,512]{2,1,0:T(8,128)(2,1)S(1)}, u32[]{:S(2)}, u32[]{:S(2)}) collective-permute-start(bf16[4,128,512]{2,1,0:T(8,128)(2,1)S(1)} %collective-permute-done.15), channel_id=1, source_target_pairs={{0,56},{8,0},{16,8},{24,16},{32,24},{40,32},{48,40},{56,48},{1,57}... | collective-permute-start | bytes 1572872 | tf_op jit(solution)/shard_map/ppermute | solution.py:100
  44.1 19.5 %collective-permute-start.8 = (bf16[8,128,512]{2,1,0:T(8,128)(2,1)S(1)}, bf16[8,128,512]{2,1,0:T(8,128)(2,1)S(1)}, u32[]{:S(2)}, u32[]{:S(2)}) collective-permute-start(bf16[8,128,512]{2,1,0:T(8,128)(2,1)S(1)} %bitcast_dynamic-update-slice_fusion.7), channel_id=1, source_target_pairs={{0,6},{2,0},{4,2},{6,4},{1,7},{3,1},{5,3},{7,5},{8,14},{10,8},{12,... | collective-permute-start | bytes 3145736 | tf_op jit(solution)/shard_map/ppermute | solution.py:100
  45.8 20.7 %collective-permute-start.9 = (bf16[8,128,512]{2,1,0:T(8,128)(2,1)S(1)}, bf16[8,128,512]{2,1,0:T(8,128)(2,1)S(1)}, u32[]{:S(2)}, u32[]{:S(2)}) collective-permute-start(bf16[8,128,512]{2,1,0:T(8,128)(2,1)S(1)} %bitcast_dynamic-update-slice_fusion.7), channel_id=1, source_target_pairs={{0,2},{2,4},{4,6},{6,0},{1,3},{3,5},{5,7},{7,1},{8,10},{10,12},{12... | collective-permute-start | bytes 3145736 | tf_op jit(solution)/shard_map/ppermute | solution.py:99
  45.8 23.2 %collective-permute-start.23 = (bf16[2048,256]{1,0:T(8,128)(2,1)S(1)}, bf16[2048,256]{1,0:T(8,128)(2,1)S(1)}, u32[]{:S(2)}, u32[]{:S(2)}) collective-permute-start(bf16[2048,256]{1,0:T(8,128)(2,1)S(1)} %copy-done), channel_id=1, source_target_pairs={{0,64},{64,128},{128,192},{192,0},{1,65},{65,129},{129,193},{193,1... | collective-permute-start | bytes 3145736 | tf_op jit(solution)/shard_map/ppermute | solution.py:122
  47.0 22.9 %collective-permute-start.24 = (bf16[2048,256]{1,0:T(8,128)(2,1)S(1)}, bf16[2048,256]{1,0:T(8,128)(2,1)S(1)}, u32[]{:S(2)}, u32[]{:S(2)}) collective-permute-start(bf16[2048,256]{1,0:T(8,128)(2,1)S(1)} %copy-done), channel_id=1, source_target_pairs={{0,192},{64,0},{128,64},{192,128},{1,193},{65,1},{129,65},{193,129... | collective-permute-start | bytes 3145736 | tf_op jit(solution)/shard_map/ppermute | solution.py:123
  52.1 9.5 %collective-permute-start.19 = (bf16[4,128,512]{2,1,0:T(8,128)(2,1)S(1)}, bf16[4,128,512]{2,1,0:T(8,128)(2,1)S(1)}, u32[]{:S(2)}, u32[]{:S(2)}) collective-permute-start(bf16[4,128,512]{2,1,0:T(8,128)(2,1)S(1)} %collective-permute-done.18), channel_id=1, source_target_pairs={{0,8},{8,16},{16,24},{24,32},{32,40},{40,48},{48,56},{56,0},{1,9},... | collective-permute-start | bytes 1572872 | tf_op jit(solution)/shard_map/ppermute | solution.py:99
  61.7 10.4 %collective-permute-start.17 = (bf16[4,128,512]{2,1,0:T(8,128)(2,1)S(1)}, bf16[4,128,512]{2,1,0:T(8,128)(2,1)S(1)}, u32[]{:S(2)}, u32[]{:S(2)}) collective-permute-start(bf16[4,128,512]{2,1,0:T(8,128)(2,1)S(1)} %collective-permute-done.16), channel_id=1, source_target_pairs={{0,56},{8,0},{16,8},{24,16},{32,24},{40,32},{48,40},{56,48},{1,57}... | collective-permute-start | bytes 1572872 | tf_op jit(solution)/shard_map/ppermute | solution.py:100
  63.6 10.3 %collective-permute-start.20 = (bf16[4,128,512]{2,1,0:T(8,128)(2,1)S(1)}, bf16[4,128,512]{2,1,0:T(8,128)(2,1)S(1)}, u32[]{:S(2)}, u32[]{:S(2)}) collective-permute-start(bf16[4,128,512]{2,1,0:T(8,128)(2,1)S(1)} %collective-permute-done.19), channel_id=1, source_target_pairs={{0,8},{8,16},{16,24},{24,32},{32,40},{40,48},{48,56},{56,0},{1,9},... | collective-permute-start | bytes 1572872 | tf_op jit(solution)/shard_map/ppermute | solution.py:99
  66.5 9.5 %collective-permute-start.11 = (bf16[4,128,512]{2,1,0:T(8,128)(2,1)S(1)}, bf16[4,128,512]{2,1,0:T(8,128)(2,1)S(1)}, u32[]{:S(2)}, u32[]{:S(2)}) collective-permute-start(bf16[4,128,512]{2,1,0:T(8,128)(2,1)S(1)} %slice.33), channel_id=1, source_target_pairs={{0,6},{2,0},{4,2},{6,4},{1,7},{3,1},{5,3},{7,5},{8,14},{10,8},{12,... | collective-permute-start | bytes 1572872 | tf_op jit(solution)/shard_map/ppermute | solution.py:109
  69.0 9.6 %collective-permute-start.10 = (bf16[4,128,512]{2,1,0:T(8,128)(2,1)S(1)}, bf16[4,128,512]{2,1,0:T(8,128)(2,1)S(1)}, u32[]{:S(2)}, u32[]{:S(2)}) collective-permute-start(bf16[4,128,512]{2,1,0:T(8,128)(2,1)S(1)} %slice.32), channel_id=1, source_target_pairs={{0,2},{2,4},{4,6},{6,0},{1,3},{3,5},{5,7},{7,1},{8,10},{10,12},{12... | collective-permute-start | bytes 1572872 | tf_op jit(solution)/shard_map/ppermute | solution.py:108
  69.9 20.0 %collective-permute-start.25 = (bf16[1024,256]{1,0:T(8,128)(2,1)S(1)}, bf16[1024,256]{1,0:T(8,128)(2,1)S(1)}, u32[]{:S(2)}, u32[]{:S(2)}) collective-permute-start(bf16[1024,256]{1,0:T(8,128)(2,1)S(1)} %slice.36), channel_id=1, source_target_pairs={{0,64},{64,128},{128,192},{192,0},{1,65},{65,129},{129,193},{193,1... | collective-permute-start | bytes 1572872 | tf_op jit(solution)/shard_map/ppermute | solution.py:132
  72.1 18.7 %collective-permute-start.26 = (bf16[1024,256]{1,0:T(8,128)(2,1)S(1)}, bf16[1024,256]{1,0:T(8,128)(2,1)S(1)}, u32[]{:S(2)}, u32[]{:S(2)}) collective-permute-start(bf16[1024,256]{1,0:T(8,128)(2,1)S(1)} %slice.37), channel_id=1, source_target_pairs={{0,192},{64,0},{128,64},{192,128},{1,193},{65,1},{129,65},{193,129... | collective-permute-start | bytes 1572872 | tf_op jit(solution)/shard_map/ppermute | solution.py:133
  73.9 7.8 %collective-permute-start.22 = (bf16[2,128,512]{2,1,0:T(8,128)(2,1)S(1)}, bf16[2,128,512]{2,1,0:T(8,128)(2,1)S(1)}, u32[]{:S(2)}, u32[]{:S(2)}) collective-permute-start(bf16[2,128,512]{2,1,0:T(8,128)(2,1)S(1)} %slice.35), channel_id=1, source_target_pairs={{0,56},{8,0},{16,8},{24,16},{32,24},{40,32},{48,40},{56,48},{1,57}... | collective-permute-start | bytes 786440 | tf_op jit(solution)/shard_map/ppermute | solution.py:109
  76.0 8.1 %collective-permute-start.21 = (bf16[2,128,512]{2,1,0:T(8,128)(2,1)S(1)}, bf16[2,128,512]{2,1,0:T(8,128)(2,1)S(1)}, u32[]{:S(2)}, u32[]{:S(2)}) collective-permute-start(bf16[2,128,512]{2,1,0:T(8,128)(2,1)S(1)} %slice.34), channel_id=1, source_target_pairs={{0,8},{8,16},{16,24},{24,32},{32,40},{40,48},{48,56},{56,0},{1,9},... | collective-permute-start | bytes 786440 | tf_op jit(solution)/shard_map/ppermute | solution.py:108
  85.9 18.3 %copy-start.5 = (s32[1,1,4]{2,1,0:T(1,128)S(1)}, s32[1,1,4]{2,1,0:T(1,128)}, u32[]{:S(2)}) copy-start(s32[1,1,4]{2,1,0:T(1,128)} %param.7) | copy-start | bytes 52
  85.9 18.3 %copy-start.6 = (s32[1,1,4]{2,1,0:T(1,128)S(1)}, s32[1,1,4]{2,1,0:T(1,128)}, u32[]{:S(2)}) copy-start(s32[1,1,4]{2,1,0:T(1,128)} %param.8) | copy-start | bytes 52
  91.6 18.8 %collective-permute-start.27 = (bf16[32,128,512]{2,1,0:T(8,128)(2,1)}, bf16[32,128,512]{2,1,0:T(8,128)(2,1)}, u32[]{:S(2)}, u32[]{:S(2)}) collective-permute-start(bf16[32,128,512]{2,1,0:T(8,128)(2,1)} %bitcast.22.rest_0_), channel_id=1, source_target_pairs={{0,1},{1,0},{2,3},{3,2},{4,5},{5,4},{6,7},{7,6},{8,9},{9,8},{10,11... | collective-permute-start | bytes 12582920 | tf_op jit(solution)/shard_map/ppermute | solution.py:180
  103.3 13.1 %collective-permute-start.28 = (bf16[32,128,512]{2,1,0:T(8,128)(2,1)}, bf16[32,128,512]{2,1,0:T(8,128)(2,1)}, u32[]{:S(2)}, u32[]{:S(2)}) collective-permute-start(bf16[32,128,512]{2,1,0:T(8,128)(2,1)} %bitcast.35.rest_1_), channel_id=1, source_target_pairs={{0,1},{1,0},{2,3},{3,2},{4,5},{5,4},{6,7},{7,6},{8,9},{9,8},{10,11... | collective-permute-start | bytes 12582920 | tf_op jit(solution)/shard_map/ppermute | solution.py:181
  (4 other events, 3.7 us)

commit v4 on v3

--- a/solution.py
+++ b/solution.py
@@ -167,13 +167,14 @@
     trail = jnp.where(on_first, recv, keep)
 
     lead_z = jnp.stack(relative_gather(lead, "z", nz, split=False), 0)
+    trail_y = jnp.stack(relative_gather(trail, "y", ny, split=False), 0)
+    grad_pieces, starts = ring_gather(out_grad, "in", in_place)
+    lead_z, trail_y, grad_pieces = lax.optimization_barrier((lead_z, trail_y, grad_pieces))
     lead_all = jnp.stack(relative_gather(lead_z, "y", ny), 1)
-    trail_y = jnp.stack(relative_gather(trail, "y", ny, split=False), 0)
     trail_all = jnp.stack(relative_gather(trail_y, "z", nz), 0)
     lead_all = lead_all.reshape(nz * ny, tok, width)
     trail_all = trail_all.reshape(nz * ny, tok, width)
 
-    grad_pieces, starts = ring_gather(out_grad, "in", in_place)
     lead_all, trail_all, grad_pieces = lax.optimization_barrier((lead_all, trail_all, grad_pieces))
     grad_pieces = [g.reshape(g.shape[0] // (2 * tok), 2, tok, g.shape[1]) for g in grad_pieces]
     starts = starts // (2 * tok)

time: 122 us -> 125 us (1.025)
  starting transfers between devices: 43.1 us -> 46.3 us
  Pallas kernels: 5.01 us -> 7.7 us
  waiting for transfers between devices: 54.2 us -> 52.3 us
    ppermute x8, waiting for transfers between devices: 22.5 us -> 5.17 us  [relative_gather(): from_left = lax.ppermute(from_left, axis, right)]
    ppermute x8, waiting for transfers between devices: 5.21 us -> 20 us  [relative_gather(): from_right = lax.ppermute(from_right, axis, left)]
    ppermute x1, waiting for transfers between devices: 0.01 us -> 9.43 us  [ring_gather(): near_a = lax.ppermute(from_left[:half], axis, right)]
    ppermute x8, starting transfers between devices: 15.5 us -> 22.5 us  [relative_gather(): from_right = lax.ppermute(from_right, axis, left)]
    ppermute x1, starting transfers between devices: 11.7 us -> 6.29 us  [on_device(): lead_other = lax.ppermute(lead_all, 'core', swap)]
    ppermute x2, waiting for transfers between devices: 9.55 us -> 5.39 us  [relative_gather(): rel[n // 2] = lax.ppermute(from_left, axis, right)]
    ppermute x1, waiting for transfers between devices: 2.95 us -> 0.25 us  [on_device(): lead_other = lax.ppermute(lead_all, 'core', swap)]
    pallas_call x2, Pallas kernels: 5.01 us -> 7.7 us  [block_products(): pl.pallas_call(functools.partial(block_kernel, n_grad, ny), out_shape=jax...]
  transfers between devices with their start and end apart: 29 -> 29, of which waited for: 15 -> 13; matrix products, arithmetic and copies ran while one was open for 9% -> 6% of each run, Pallas kernels for 1% -> 3%
where the time goes in v4:
time: 125 us
  waiting for transfers between devices  52.3 us (42%)
  starting transfers between devices  46.3 us (37%)
  local copies, waits for them, and re-layouts  12.3 us (10%)
  Pallas kernels  7.7 us (6%)
  other arithmetic  5.44 us (4%)
    ppermute x8, starting transfers between devices, relative_gather(): from_right = lax.ppermute(from_right, axis, left)  22.5 us
    ppermute x8, waiting for transfers between devices, relative_gather(): from_right = lax.ppermute(from_right, axis, left)  20 us
    ppermute x1, waiting for transfers between devices, ring_gather(): near_a = lax.ppermute(from_left[:half], axis, right)  9.43 us
    unnamed x26, local copies, waits for them, and re-layouts  8.73 us
    pallas_call x2, Pallas kernels, block_products(): pl.pallas_call(functools.partial(block_kernel, n_grad, ny), out_shape=jax...  7.7 us
    ppermute x1, starting transfers between devices, on_device(): lead_other = lax.ppermute(lead_all, 'core', swap)  6.29 us
    ppermute x1, waiting for transfers between devices, on_device(): trail_other = lax.ppermute(trail_all, 'core', swap)  6 us
    ppermute x2, starting transfers between devices, relative_gather(): near_b = lax.ppermute(from_right[half:], axis, left)  5.82 us
  transfers between devices with their start and end apart: 29, of which 13 were waited for; matrix products, arithmetic and copies ran while one was open for 6% of the time, Pallas kernels for 3%

profile of v4, /device:TPU:1, one launch (start us, length us, event | category | flops | bytes accessed | tf_op | source)
XLA Modules:
  0.0 124.9 jit_solution(15438978472242340594)
XLA Ops:
  1.0 3.3 %collective-permute-start = (bf16[128,512]{1,0:T(8,128)(2,1)S(1)}, bf16[128,512]{1,0:T(8,128)(2,1)S(1)}, u32[]{:S(2)}, u32[]{:S(2)}) collective-permute-start(bf16[128,512]{1,0:T(8,128)(2,1)S(1)} %broadcast_select_fusion.2), channel_id=1, source_target_pairs={{0,1},{1,0},{2,3},{3,2},{4,5},{5,4},{6,7},{7,6},{8,9},{9,8},{10,11... | collective-permute-start | bytes 393224 | tf_op jit(solution)/shard_map/ppermute | solution.py:165
  5.3 1.0 bitcast_dynamic-update-slice_fusion.14
  6.3 3.9 %collective-permute-start.1 = (bf16[128,512]{1,0:T(8,128)(2,1)S(1)}, bf16[128,512]{1,0:T(8,128)(2,1)S(1)}, u32[]{:S(2)}, u32[]{:S(2)}) collective-permute-start(bf16[128,512]{1,0:T(8,128)(2,1)S(1)} %get-tuple-element.37), channel_id=1, source_target_pairs={{0,56},{8,0},{16,8},{24,16},{32,24},{40,32},{48,40},{56,48},{1,57}... | collective-permute-start | bytes 393224 | tf_op jit(solution)/shard_map/ppermute | solution.py:100
  11.2 1.4 %collective-permute-start.9 = (bf16[128,512]{1,0:T(8,128)(2,1)S(1)}, bf16[128,512]{1,0:T(8,128)(2,1)S(1)}, u32[]{:S(2)}, u32[]{:S(2)}) collective-permute-start(bf16[128,512]{1,0:T(8,128)(2,1)S(1)} %broadcast_select_fusion), channel_id=1, source_target_pairs={{0,2},{2,4},{4,6},{6,0},{1,3},{3,5},{5,7},{7,1},{8,10},{10,12},{12... | collective-permute-start | bytes 393224 | tf_op jit(solution)/shard_map/ppermute | solution.py:99
  12.6 1.2 collective-permute-start.11
  13.8 1.5 %collective-permute-start.12 = (bf16[2048,256]{1,0:T(8,128)(2,1)}, bf16[2048,256]{1,0:T(8,128)(2,1)S(1)}, u32[]{:S(2)}, u32[]{:S(2)}) collective-permute-start(bf16[2048,256]{1,0:T(8,128)(2,1)} %param.6), channel_id=1, source_target_pairs={{0,192},{64,0},{128,64},{192,128},{1,193},{65,1},{129,65},{193,129... | collective-permute-start | bytes 3145736 | tf_op jit(solution)/shard_map/ppermute | solution.py:123
  15.3 1.5 %collective-permute-start.8 = (bf16[128,512]{1,0:T(8,128)(2,1)S(1)}, bf16[128,512]{1,0:T(8,128)(2,1)S(1)}, u32[]{:S(2)}, u32[]{:S(2)}) collective-permute-start(bf16[128,512]{1,0:T(8,128)(2,1)S(1)} %broadcast_select_fusion), channel_id=1, source_target_pairs={{0,6},{2,0},{4,2},{6,4},{1,7},{3,1},{5,3},{7,5},{8,14},{10,8},{12,... | collective-permute-start | bytes 393224 | tf_op jit(solution)/shard_map/ppermute | solution.py:100
  16.8 2.7 %collective-permute-start.2 = (bf16[128,512]{1,0:T(8,128)(2,1)S(1)}, bf16[128,512]{1,0:T(8,128)(2,1)S(1)}, u32[]{:S(2)}, u32[]{:S(2)}) collective-permute-start(bf16[128,512]{1,0:T(8,128)(2,1)S(1)} %collective-permute-done.1), channel_id=1, source_target_pairs={{0,56},{8,0},{16,8},{24,16},{32,24},{40,32},{48,40},{56,48},{1,57}... | collective-permute-start | bytes 393224 | tf_op jit(solution)/shard_map/ppermute | solution.py:100
  19.5 1.2 collective-permute-start.10
  21.4 3.4 %collective-permute-start.3 = (bf16[128,512]{1,0:T(8,128)(2,1)S(1)}, bf16[128,512]{1,0:T(8,128)(2,1)S(1)}, u32[]{:S(2)}, u32[]{:S(2)}) collective-permute-start(bf16[128,512]{1,0:T(8,128)(2,1)S(1)} %collective-permute-done.2), channel_id=1, source_target_pairs={{0,56},{8,0},{16,8},{24,16},{32,24},{40,32},{48,40},{56,48},{1,57}... | collective-permute-start | bytes 393224 | tf_op jit(solution)/shard_map/ppermute | solution.py:100
  25.0 5.1 %collective-permute-done.6 = bf16[128,512]{1,0:T(8,128)(2,1)S(1)} collective-permute-done((bf16[128,512]{1,0:T(8,128)(2,1)S(1)}, bf16[128,512]{1,0:T(8,128)(2,1)S(1)}, u32[]{:S(2)}, u32[]{:S(2)}) %collective-permute-start.6) | collective-permute-done | bytes 131104 | tf_op jit(solution)/shard_map/ppermute | solution.py:99
  30.2 5.3 %collective-permute-done.7 = bf16[128,512]{1,0:T(8,128)(2,1)S(1)} collective-permute-done((bf16[128,512]{1,0:T(8,128)(2,1)S(1)}, bf16[128,512]{1,0:T(8,128)(2,1)S(1)}, u32[]{:S(2)}, u32[]{:S(2)}) %collective-permute-start.7) | collective-permute-done | bytes 131104 | tf_op jit(solution)/shard_map/ppermute | solution.py:104
  35.5 2.3 %collective-permute-done.11 = bf16[2048,256]{1,0:T(8,128)(2,1)S(1)} collective-permute-done((bf16[2048,256]{1,0:T(8,128)(2,1)}, bf16[2048,256]{1,0:T(8,128)(2,1)S(1)}, u32[]{:S(2)}, u32[]{:S(2)}) %collective-permute-start.11) | collective-permute-done | bytes 1048608 | tf_op jit(solution)/shard_map/ppermute | solution.py:122
  38.0 2.7 %collective-permute-start.14 = (bf16[1024,256]{1,0:T(8,128)(2,1)S(1)}, bf16[1024,256]{1,0:T(8,128)(2,1)S(1)}, u32[]{:S(2)}, u32[]{:S(2)}) collective-permute-start(bf16[1024,256]{1,0:T(8,128)(2,1)S(1)} %slice.33), channel_id=1, source_target_pairs={{0,192},{64,0},{128,64},{192,128},{1,193},{65,1},{129,65},{193,129... | collective-permute-start | bytes 1572872 | tf_op jit(solution)/shard_map/ppermute | solution.py:133
  40.8 9.4 %collective-permute-done.13 = bf16[1024,256]{1,0:T(8,128)(2,1)S(1)} collective-permute-done((bf16[1024,256]{1,0:T(8,128)(2,1)S(1)}, bf16[1024,256]{1,0:T(8,128)(2,1)S(1)}, u32[]{:S(2)}, u32[]{:S(2)}) %collective-permute-start.13) | collective-permute-done | bytes 524320 | tf_op jit(solution)/shard_map/ppermute | solution.py:132
  51.8 1.8 %collective-permute-start.15 = (bf16[8,128,512]{2,1,0:T(8,128)(2,1)S(1)}, bf16[8,128,512]{2,1,0:T(8,128)(2,1)S(1)}, u32[]{:S(2)}, u32[]{:S(2)}) collective-permute-start(bf16[8,128,512]{2,1,0:T(8,128)(2,1)S(1)} %bitcast_dynamic-update-slice_fusion.7), channel_id=1, source_target_pairs={{0,6},{2,0},{4,2},{6,4},{1,7},{3,1},{5,3},{7,5},{8,14},{10,8},{12,... | collective-permute-start | bytes 3145736 | tf_op jit(solution)/shard_map/ppermute | solution.py:100
  53.8 2.6 %collective-permute-start.19 = (bf16[4,128,512]{2,1,0:T(8,128)(2,1)S(1)}, bf16[4,128,512]{2,1,0:T(8,128)(2,1)S(1)}, u32[]{:S(2)}, u32[]{:S(2)}) collective-permute-start(bf16[4,128,512]{2,1,0:T(8,128)(2,1)S(1)} %pad_maximum_fusion.1), channel_id=1, source_target_pairs={{0,56},{8,0},{16,8},{24,16},{32,24},{40,32},{48,40},{56,48},{1,57}... | collective-permute-start | bytes 1572872 | tf_op jit(solution)/shard_map/ppermute | solution.py:100
  56.4 8.2 %collective-permute-done.19 = bf16[4,128,512]{2,1,0:T(8,128)(2,1)S(1)} collective-permute-done((bf16[4,128,512]{2,1,0:T(8,128)(2,1)S(1)}, bf16[4,128,512]{2,1,0:T(8,128)(2,1)S(1)}, u32[]{:S(2)}, u32[]{:S(2)}) %collective-permute-start.19) | collective-permute-done | bytes 524320 | tf_op jit(solution)/shard_map/ppermute | solution.py:100
  64.5 3.4 %collective-permute-start.20 = (bf16[4,128,512]{2,1,0:T(8,128)(2,1)S(1)}, bf16[4,128,512]{2,1,0:T(8,128)(2,1)S(1)}, u32[]{:S(2)}, u32[]{:S(2)}) collective-permute-start(bf16[4,128,512]{2,1,0:T(8,128)(2,1)S(1)} %collective-permute-done.19), channel_id=1, source_target_pairs={{0,56},{8,0},{16,8},{24,16},{32,24},{40,32},{48,40},{56,48},{1,57}... | collective-permute-start | bytes 1572872 | tf_op jit(solution)/shard_map/ppermute | solution.py:100
  68.0 6.2 %collective-permute-done.15 = bf16[8,128,512]{2,1,0:T(8,128)(2,1)S(1)} collective-permute-done((bf16[8,128,512]{2,1,0:T(8,128)(2,1)S(1)}, bf16[8,128,512]{2,1,0:T(8,128)(2,1)S(1)}, u32[]{:S(2)}, u32[]{:S(2)}) %collective-permute-start.15) | collective-permute-done | bytes 1048608 | tf_op jit(solution)/shard_map/ppermute | solution.py:100
  74.2 2.3 %collective-permute-start.18 = (bf16[4,128,512]{2,1,0:T(8,128)(2,1)S(1)}, bf16[4,128,512]{2,1,0:T(8,128)(2,1)S(1)}, u32[]{:S(2)}, u32[]{:S(2)}) collective-permute-start(bf16[4,128,512]{2,1,0:T(8,128)(2,1)S(1)} %slice.35), channel_id=1, source_target_pairs={{0,6},{2,0},{4,2},{6,4},{1,7},{3,1},{5,3},{7,5},{8,14},{10,8},{12,... | collective-permute-start | bytes 1572872 | tf_op jit(solution)/shard_map/ppermute | solution.py:109
  76.7 3.2 %collective-permute-start.21 = (bf16[4,128,512]{2,1,0:T(8,128)(2,1)S(1)}, bf16[4,128,512]{2,1,0:T(8,128)(2,1)S(1)}, u32[]{:S(2)}, u32[]{:S(2)}) collective-permute-start(bf16[4,128,512]{2,1,0:T(8,128)(2,1)S(1)} %collective-permute-done.20), channel_id=1, source_target_pairs={{0,56},{8,0},{16,8},{24,16},{32,24},{40,32},{48,40},{56,48},{1,57}... | collective-permute-start | bytes 1572872 | tf_op jit(solution)/shard_map/ppermute | solution.py:100
  82.4 4.9 %collective-permute-done.21 = bf16[4,128,512]{2,1,0:T(8,128)(2,1)S(1)} collective-permute-done((bf16[4,128,512]{2,1,0:T(8,128)(2,1)S(1)}, bf16[4,128,512]{2,1,0:T(8,128)(2,1)S(1)}, u32[]{:S(2)}, u32[]{:S(2)}) %collective-permute-start.21) | collective-permute-done | bytes 524320 | tf_op jit(solution)/shard_map/ppermute | solution.py:100
  87.3 3.5 %collective-permute-start.26 = (bf16[2,128,512]{2,1,0:T(8,128)(2,1)S(1)}, bf16[2,128,512]{2,1,0:T(8,128)(2,1)S(1)}, u32[]{:S(2)}, u32[]{:S(2)}) collective-permute-start(bf16[2,128,512]{2,1,0:T(8,128)(2,1)S(1)} %slice.37), channel_id=1, source_target_pairs={{0,56},{8,0},{16,8},{24,16},{32,24},{40,32},{48,40},{56,48},{1,57}... | collective-permute-start | bytes 786440 | tf_op jit(solution)/shard_map/ppermute | solution.py:109
  91.6 2.4 %copy.6 = bf16[8,4,128,512]{3,2,1,0:T(8,128)(2,1)} copy(bf16[8,4,128,512]{3,2,0,1:T(8,128)(2,1)S(1)} %pad_maximum_fusion) | data formatting | bytes 8388608 | tf_op jit(solution)/shard_map/stack | solution.py:173
  94.9 2.7 %collective-permute-done.25 = bf16[2,128,512]{2,1,0:T(8,128)(2,1)S(1)} collective-permute-done((bf16[2,128,512]{2,1,0:T(8,128)(2,1)S(1)}, bf16[2,128,512]{2,1,0:T(8,128)(2,1)S(1)}, u32[]{:S(2)}, u32[]{:S(2)}) %collective-permute-start.25) | collective-permute-done | bytes 262176 | tf_op jit(solution)/shard_map/ppermute | solution.py:108
  100.9 6.3 %collective-permute-start.27 = (bf16[32,128,512]{2,1,0:T(8,128)(2,1)}, bf16[32,128,512]{2,1,0:T(8,128)(2,1)}, u32[]{:S(2)}, u32[]{:S(2)}) collective-permute-start(bf16[32,128,512]{2,1,0:T(8,128)(2,1)} %bitcast.26.rest_0_), channel_id=1, source_target_pairs={{0,1},{1,0},{2,3},{3,2},{4,5},{5,4},{6,7},{7,6},{8,9},{9,8},{10,11... | collective-permute-start | bytes 12582920 | tf_op jit(solution)/shard_map/ppermute | solution.py:181
  108.1 1.0 copy-done.2
  109.2 1.0 copy-done.4
  110.2 3.8 %shard_map.55 = f32[4,128,128]{2,1,0:T(8,128)S(1)} custom-call(s32[4]{0:T(128)S(1)} %and_select_fusion.2.rows_ref, s32[4]{0:T(128)S(1)} %clamp_bitcast_fusion.cols_ref, s32[4]{0:T(128)S(1)} %and_convert_fusion.1.use_ref, s32[5]{0:T(128)S(1)} %and_select_fusion.starts_ref, s32[2]{0:T(128)S(1)} %pad_add_fusion.place_ref, ...), custom_call_target="tpu_custom_call" | custom-call | flops 1073741824 | bytes 17039360 | tf_op jit(solution)/shard_map/pallas_call | solution.py:78
  114.3 6.0 %collective-permute-done.28.rest_1_ = bf16[32,128,512]{2,1,0:T(8,128)(2,1)} collective-permute-done((bf16[32,128,512]{2,1,0:T(8,128)(2,1)}, bf16[32,128,512]{2,1,0:T(8,128)(2,1)}, u32[]{:S(2)}, u32[]{:S(2)}) %collective-permute-start.28) | collective-permute-done | bytes 4194336 | tf_op jit(solution)/shard_map/ppermute | solution.py:182
  120.3 3.9 %shard_map.56 = f32[4,128,128]{2,1,0:T(8,128)S(1)} custom-call(s32[4]{0:T(128)S(1)} %and_select_fusion.2.rows_ref, s32[4]{0:T(128)S(1)} %clamp_bitcast_fusion.cols_ref, s32[4]{0:T(128)S(1)} %get-tuple-element.33.use_ref, s32[5]{0:T(128)S(1)} %and_select_fusion.starts_ref, s32[2]{0:T(128)S(1)} %pad_add_fusion.place_ref, ...), custom_call_target="tpu_custom_call" | custom-call | flops 1073741824 | bytes 17039360 | tf_op jit(solution)/shard_map/pallas_call | solution.py:78
  (78 shorter events, 14.7 us)
Async XLA Ops:
  1.0 4.3 %collective-permute-start = (bf16[128,512]{1,0:T(8,128)(2,1)S(1)}, bf16[128,512]{1,0:T(8,128)(2,1)S(1)}, u32[]{:S(2)}, u32[]{:S(2)}) collective-permute-start(bf16[128,512]{1,0:T(8,128)(2,1)S(1)} %broadcast_select_fusion.2), channel_id=1, source_target_pairs={{0,1},{1,0},{2,3},{3,2},{4,5},{5,4},{6,7},{7,6},{8,9},{9,8},{10,11... | collective-permute-start | bytes 393224 | tf_op jit(solution)/shard_map/ppermute | solution.py:165
  6.3 9.0 %collective-permute-start.1 = (bf16[128,512]{1,0:T(8,128)(2,1)S(1)}, bf16[128,512]{1,0:T(8,128)(2,1)S(1)}, u32[]{:S(2)}, u32[]{:S(2)}) collective-permute-start(bf16[128,512]{1,0:T(8,128)(2,1)S(1)} %get-tuple-element.37), channel_id=1, source_target_pairs={{0,56},{8,0},{16,8},{24,16},{32,24},{40,32},{48,40},{56,48},{1,57}... | collective-permute-start | bytes 393224 | tf_op jit(solution)/shard_map/ppermute | solution.py:100
  10.2 6.6 %collective-permute-start.4 = (bf16[128,512]{1,0:T(8,128)(2,1)S(1)}, bf16[128,512]{1,0:T(8,128)(2,1)S(1)}, u32[]{:S(2)}, u32[]{:S(2)}) collective-permute-start(bf16[128,512]{1,0:T(8,128)(2,1)S(1)} %get-tuple-element.37), channel_id=1, source_target_pairs={{0,8},{8,16},{16,24},{24,32},{32,40},{40,48},{48,56},{56,0},{1,9},... | collective-permute-start | bytes 393224 | tf_op jit(solution)/shard_map/ppermute | solution.py:99
  11.2 8.3 %collective-permute-start.9 = (bf16[128,512]{1,0:T(8,128)(2,1)S(1)}, bf16[128,512]{1,0:T(8,128)(2,1)S(1)}, u32[]{:S(2)}, u32[]{:S(2)}) collective-permute-start(bf16[128,512]{1,0:T(8,128)(2,1)S(1)} %broadcast_select_fusion), channel_id=1, source_target_pairs={{0,2},{2,4},{4,6},{6,0},{1,3},{3,5},{5,7},{7,1},{8,10},{10,12},{12... | collective-permute-start | bytes 393224 | tf_op jit(solution)/shard_map/ppermute | solution.py:99
  12.6 25.2 %collective-permute-start.11 = (bf16[2048,256]{1,0:T(8,128)(2,1)}, bf16[2048,256]{1,0:T(8,128)(2,1)S(1)}, u32[]{:S(2)}, u32[]{:S(2)}) collective-permute-start(bf16[2048,256]{1,0:T(8,128)(2,1)} %param.6), channel_id=1, source_target_pairs={{0,64},{64,128},{128,192},{192,0},{1,65},{65,129},{129,193},{193,1... | collective-permute-start | bytes 3145736 | tf_op jit(solution)/shard_map/ppermute | solution.py:122
  13.8 24.1 %collective-permute-start.12 = (bf16[2048,256]{1,0:T(8,128)(2,1)}, bf16[2048,256]{1,0:T(8,128)(2,1)S(1)}, u32[]{:S(2)}, u32[]{:S(2)}) collective-permute-start(bf16[2048,256]{1,0:T(8,128)(2,1)} %param.6), channel_id=1, source_target_pairs={{0,192},{64,0},{128,64},{192,128},{1,193},{65,1},{129,65},{193,129... | collective-permute-start | bytes 3145736 | tf_op jit(solution)/shard_map/ppermute | solution.py:123
  15.3 4.2 %collective-permute-start.8 = (bf16[128,512]{1,0:T(8,128)(2,1)S(1)}, bf16[128,512]{1,0:T(8,128)(2,1)S(1)}, u32[]{:S(2)}, u32[]{:S(2)}) collective-permute-start(bf16[128,512]{1,0:T(8,128)(2,1)S(1)} %broadcast_select_fusion), channel_id=1, source_target_pairs={{0,6},{2,0},{4,2},{6,4},{1,7},{3,1},{5,3},{7,5},{8,14},{10,8},{12,... | collective-permute-start | bytes 393224 | tf_op jit(solution)/shard_map/ppermute | solution.py:100
  16.8 4.6 %collective-permute-start.2 = (bf16[128,512]{1,0:T(8,128)(2,1)S(1)}, bf16[128,512]{1,0:T(8,128)(2,1)S(1)}, u32[]{:S(2)}, u32[]{:S(2)}) collective-permute-start(bf16[128,512]{1,0:T(8,128)(2,1)S(1)} %collective-permute-done.1), channel_id=1, source_target_pairs={{0,56},{8,0},{16,8},{24,16},{32,24},{40,32},{48,40},{56,48},{1,57}... | collective-permute-start | bytes 393224 | tf_op jit(solution)/shard_map/ppermute | solution.py:100
  19.5 5.3 %collective-permute-start.5 = (bf16[128,512]{1,0:T(8,128)(2,1)S(1)}, bf16[128,512]{1,0:T(8,128)(2,1)S(1)}, u32[]{:S(2)}, u32[]{:S(2)}) collective-permute-start(bf16[128,512]{1,0:T(8,128)(2,1)S(1)} %collective-permute-done.4), channel_id=1, source_target_pairs={{0,8},{8,16},{16,24},{24,32},{32,40},{40,48},{48,56},{56,0},{1,9},... | collective-permute-start | bytes 393224 | tf_op jit(solution)/shard_map/ppermute | solution.py:99
  19.5 5.4 %collective-permute-start.10 = (bf16[128,512]{1,0:T(8,128)(2,1)S(1)}, bf16[128,512]{1,0:T(8,128)(2,1)S(1)}, u32[]{:S(2)}, u32[]{:S(2)}) collective-permute-start(bf16[128,512]{1,0:T(8,128)(2,1)S(1)} %collective-permute-done.9), channel_id=1, source_target_pairs={{0,2},{2,4},{4,6},{6,0},{1,3},{3,5},{5,7},{7,1},{8,10},{10,12},{12... | collective-permute-start | bytes 393224 | tf_op jit(solution)/shard_map/ppermute | solution.py:104
  21.4 8.7 %collective-permute-start.3 = (bf16[128,512]{1,0:T(8,128)(2,1)S(1)}, bf16[128,512]{1,0:T(8,128)(2,1)S(1)}, u32[]{:S(2)}, u32[]{:S(2)}) collective-permute-start(bf16[128,512]{1,0:T(8,128)(2,1)S(1)} %collective-permute-done.2), channel_id=1, source_target_pairs={{0,56},{8,0},{16,8},{24,16},{32,24},{40,32},{48,40},{56,48},{1,57}... | collective-permute-start | bytes 393224 | tf_op jit(solution)/shard_map/ppermute | solution.py:100
  24.8 5.3 %collective-permute-start.6 = (bf16[128,512]{1,0:T(8,128)(2,1)S(1)}, bf16[128,512]{1,0:T(8,128)(2,1)S(1)}, u32[]{:S(2)}, u32[]{:S(2)}) collective-permute-start(bf16[128,512]{1,0:T(8,128)(2,1)S(1)} %collective-permute-done.5), channel_id=1, source_target_pairs={{0,8},{8,16},{16,24},{24,32},{32,40},{40,48},{48,56},{56,0},{1,9},... | collective-permute-start | bytes 393224 | tf_op jit(solution)/shard_map/ppermute | solution.py:99
  30.1 5.3 %collective-permute-start.7 = (bf16[128,512]{1,0:T(8,128)(2,1)S(1)}, bf16[128,512]{1,0:T(8,128)(2,1)S(1)}, u32[]{:S(2)}, u32[]{:S(2)}) collective-permute-start(bf16[128,512]{1,0:T(8,128)(2,1)S(1)} %collective-permute-done.6), channel_id=1, source_target_pairs={{0,8},{8,16},{16,24},{24,32},{32,40},{40,48},{48,56},{56,0},{1,9},... | collective-permute-start | bytes 393224 | tf_op jit(solution)/shard_map/ppermute | solution.py:104
  37.9 12.4 %collective-permute-start.13 = (bf16[1024,256]{1,0:T(8,128)(2,1)S(1)}, bf16[1024,256]{1,0:T(8,128)(2,1)S(1)}, u32[]{:S(2)}, u32[]{:S(2)}) collective-permute-start(bf16[1024,256]{1,0:T(8,128)(2,1)S(1)} %slice.32), channel_id=1, source_target_pairs={{0,64},{64,128},{128,192},{192,0},{1,65},{65,129},{129,193},{193,1... | collective-permute-start | bytes 1572872 | tf_op jit(solution)/shard_map/ppermute | solution.py:132
  38.0 13.0 %collective-permute-start.14 = (bf16[1024,256]{1,0:T(8,128)(2,1)S(1)}, bf16[1024,256]{1,0:T(8,128)(2,1)S(1)}, u32[]{:S(2)}, u32[]{:S(2)}) collective-permute-start(bf16[1024,256]{1,0:T(8,128)(2,1)S(1)} %slice.33), channel_id=1, source_target_pairs={{0,192},{64,0},{128,64},{192,128},{1,193},{65,1},{129,65},{193,129... | collective-permute-start | bytes 1572872 | tf_op jit(solution)/shard_map/ppermute | solution.py:133
  51.8 22.4 %collective-permute-start.15 = (bf16[8,128,512]{2,1,0:T(8,128)(2,1)S(1)}, bf16[8,128,512]{2,1,0:T(8,128)(2,1)S(1)}, u32[]{:S(2)}, u32[]{:S(2)}) collective-permute-start(bf16[8,128,512]{2,1,0:T(8,128)(2,1)S(1)} %bitcast_dynamic-update-slice_fusion.7), channel_id=1, source_target_pairs={{0,6},{2,0},{4,2},{6,4},{1,7},{3,1},{5,3},{7,5},{8,14},{10,8},{12,... | collective-permute-start | bytes 3145736 | tf_op jit(solution)/shard_map/ppermute | solution.py:100
  53.6 22.9 %collective-permute-start.16 = (bf16[8,128,512]{2,1,0:T(8,128)(2,1)S(1)}, bf16[8,128,512]{2,1,0:T(8,128)(2,1)S(1)}, u32[]{:S(2)}, u32[]{:S(2)}) collective-permute-start(bf16[8,128,512]{2,1,0:T(8,128)(2,1)S(1)} %bitcast_dynamic-update-slice_fusion.7), channel_id=1, source_target_pairs={{0,2},{2,4},{4,6},{6,0},{1,3},{3,5},{5,7},{7,1},{8,10},{10,12},{12... | collective-permute-start | bytes 3145736 | tf_op jit(solution)/shard_map/ppermute | solution.py:99
  53.8 10.8 %collective-permute-start.19 = (bf16[4,128,512]{2,1,0:T(8,128)(2,1)S(1)}, bf16[4,128,512]{2,1,0:T(8,128)(2,1)S(1)}, u32[]{:S(2)}, u32[]{:S(2)}) collective-permute-start(bf16[4,128,512]{2,1,0:T(8,128)(2,1)S(1)} %pad_maximum_fusion.1), channel_id=1, source_target_pairs={{0,56},{8,0},{16,8},{24,16},{32,24},{40,32},{48,40},{56,48},{1,57}... | collective-permute-start | bytes 1572872 | tf_op jit(solution)/shard_map/ppermute | solution.py:100
  56.4 11.6 %collective-permute-start.22 = (bf16[4,128,512]{2,1,0:T(8,128)(2,1)S(1)}, bf16[4,128,512]{2,1,0:T(8,128)(2,1)S(1)}, u32[]{:S(2)}, u32[]{:S(2)}) collective-permute-start(bf16[4,128,512]{2,1,0:T(8,128)(2,1)S(1)} %pad_maximum_fusion.1), channel_id=1, source_target_pairs={{0,8},{8,16},{16,24},{24,32},{32,40},{40,48},{48,56},{56,0},{1,9},... | collective-permute-start | bytes 1572872 | tf_op jit(solution)/shard_map/ppermute | solution.py:99
  64.5 12.2 %collective-permute-start.20 = (bf16[4,128,512]{2,1,0:T(8,128)(2,1)S(1)}, bf16[4,128,512]{2,1,0:T(8,128)(2,1)S(1)}, u32[]{:S(2)}, u32[]{:S(2)}) collective-permute-start(bf16[4,128,512]{2,1,0:T(8,128)(2,1)S(1)} %collective-permute-done.19), channel_id=1, source_target_pairs={{0,56},{8,0},{16,8},{24,16},{32,24},{40,32},{48,40},{56,48},{1,57}... | collective-permute-start | bytes 1572872 | tf_op jit(solution)/shard_map/ppermute | solution.py:100
  68.0 11.9 %collective-permute-start.23 = (bf16[4,128,512]{2,1,0:T(8,128)(2,1)S(1)}, bf16[4,128,512]{2,1,0:T(8,128)(2,1)S(1)}, u32[]{:S(2)}, u32[]{:S(2)}) collective-permute-start(bf16[4,128,512]{2,1,0:T(8,128)(2,1)S(1)} %collective-permute-done.22), channel_id=1, source_target_pairs={{0,8},{8,16},{16,24},{24,32},{32,40},{40,48},{48,56},{56,0},{1,9},... | collective-permute-start | bytes 1572872 | tf_op jit(solution)/shard_map/ppermute | solution.py:99
  74.2 16.6 %collective-permute-start.18 = (bf16[4,128,512]{2,1,0:T(8,128)(2,1)S(1)}, bf16[4,128,512]{2,1,0:T(8,128)(2,1)S(1)}, u32[]{:S(2)}, u32[]{:S(2)}) collective-permute-start(bf16[4,128,512]{2,1,0:T(8,128)(2,1)S(1)} %slice.35), channel_id=1, source_target_pairs={{0,6},{2,0},{4,2},{6,4},{1,7},{3,1},{5,3},{7,5},{8,14},{10,8},{12,... | collective-permute-start | bytes 1572872 | tf_op jit(solution)/shard_map/ppermute | solution.py:109
  76.6 14.3 %collective-permute-start.17 = (bf16[4,128,512]{2,1,0:T(8,128)(2,1)S(1)}, bf16[4,128,512]{2,1,0:T(8,128)(2,1)S(1)}, u32[]{:S(2)}, u32[]{:S(2)}) collective-permute-start(bf16[4,128,512]{2,1,0:T(8,128)(2,1)S(1)} %slice.34), channel_id=1, source_target_pairs={{0,2},{2,4},{4,6},{6,0},{1,3},{3,5},{5,7},{7,1},{8,10},{10,12},{12... | collective-permute-start | bytes 1572872 | tf_op jit(solution)/shard_map/ppermute | solution.py:108
  76.7 10.5 %collective-permute-start.21 = (bf16[4,128,512]{2,1,0:T(8,128)(2,1)S(1)}, bf16[4,128,512]{2,1,0:T(8,128)(2,1)S(1)}, u32[]{:S(2)}, u32[]{:S(2)}) collective-permute-start(bf16[4,128,512]{2,1,0:T(8,128)(2,1)S(1)} %collective-permute-done.20), channel_id=1, source_target_pairs={{0,56},{8,0},{16,8},{24,16},{32,24},{40,32},{48,40},{56,48},{1,57}... | collective-permute-start | bytes 1572872 | tf_op jit(solution)/shard_map/ppermute | solution.py:100
  79.9 10.9 %collective-permute-start.24 = (bf16[4,128,512]{2,1,0:T(8,128)(2,1)S(1)}, bf16[4,128,512]{2,1,0:T(8,128)(2,1)S(1)}, u32[]{:S(2)}, u32[]{:S(2)}) collective-permute-start(bf16[4,128,512]{2,1,0:T(8,128)(2,1)S(1)} %collective-permute-done.23), channel_id=1, source_target_pairs={{0,8},{8,16},{16,24},{24,32},{32,40},{40,48},{48,56},{56,0},{1,9},... | collective-permute-start | bytes 1572872 | tf_op jit(solution)/shard_map/ppermute | solution.py:99
  87.3 7.6 %collective-permute-start.26 = (bf16[2,128,512]{2,1,0:T(8,128)(2,1)S(1)}, bf16[2,128,512]{2,1,0:T(8,128)(2,1)S(1)}, u32[]{:S(2)}, u32[]{:S(2)}) collective-permute-start(bf16[2,128,512]{2,1,0:T(8,128)(2,1)S(1)} %slice.37), channel_id=1, source_target_pairs={{0,56},{8,0},{16,8},{24,16},{32,24},{40,32},{48,40},{56,48},{1,57}... | collective-permute-start | bytes 786440 | tf_op jit(solution)/shard_map/ppermute | solution.py:109
  90.8 6.8 %collective-permute-start.25 = (bf16[2,128,512]{2,1,0:T(8,128)(2,1)S(1)}, bf16[2,128,512]{2,1,0:T(8,128)(2,1)S(1)}, u32[]{:S(2)}, u32[]{:S(2)}) collective-permute-start(bf16[2,128,512]{2,1,0:T(8,128)(2,1)S(1)} %slice.36), channel_id=1, source_target_pairs={{0,8},{8,16},{16,24},{24,32},{32,40},{40,48},{48,56},{56,0},{1,9},... | collective-permute-start | bytes 786440 | tf_op jit(solution)/shard_map/ppermute | solution.py:108
  94.0 14.0 %copy-start.5 = (s32[1,1,4]{2,1,0:T(1,128)S(1)}, s32[1,1,4]{2,1,0:T(1,128)}, u32[]{:S(2)}) copy-start(s32[1,1,4]{2,1,0:T(1,128)} %param.7) | copy-start | bytes 52
  94.0 14.0 %copy-start.6 = (s32[1,1,4]{2,1,0:T(1,128)S(1)}, s32[1,1,4]{2,1,0:T(1,128)}, u32[]{:S(2)}) copy-start(s32[1,1,4]{2,1,0:T(1,128)} %param.8) | copy-start | bytes 52
  94.0 14.1 %copy-start = (bf16[2048,256]{1,0:T(8,128)(2,1)S(1)}, bf16[2048,256]{1,0:T(8,128)(2,1)}, u32[]{:S(2)}) copy-start(bf16[2048,256]{1,0:T(8,128)(2,1)} %param.6) | copy-start | bytes 3145732
  100.9 13.4 %collective-permute-start.27 = (bf16[32,128,512]{2,1,0:T(8,128)(2,1)}, bf16[32,128,512]{2,1,0:T(8,128)(2,1)}, u32[]{:S(2)}, u32[]{:S(2)}) collective-permute-start(bf16[32,128,512]{2,1,0:T(8,128)(2,1)} %bitcast.26.rest_0_), channel_id=1, source_target_pairs={{0,1},{1,0},{2,3},{3,2},{4,5},{5,4},{6,7},{7,6},{8,9},{9,8},{10,11... | collective-permute-start | bytes 12582920 | tf_op jit(solution)/shard_map/ppermute | solution.py:181
  107.2 13.1 %collective-permute-start.28 = (bf16[32,128,512]{2,1,0:T(8,128)(2,1)}, bf16[32,128,512]{2,1,0:T(8,128)(2,1)}, u32[]{:S(2)}, u32[]{:S(2)}) collective-permute-start(bf16[32,128,512]{2,1,0:T(8,128)(2,1)} %bitcast.35.rest_1_), channel_id=1, source_target_pairs={{0,1},{1,0},{2,3},{3,2},{4,5},{5,4},{6,7},{7,6},{8,9},{9,8},{10,11... | collective-permute-start | bytes 12582920 | tf_op jit(solution)/shard_map/ppermute | solution.py:182
  (4 other events, 3.7 us)

commit v5 on v3

--- a/solution.py
+++ b/solution.py
@@ -63,7 +63,7 @@
                 )
 
             out_ref[s] = lax.fori_loop(
-                0, chunks, body, jnp.zeros((BLK, BLK), jnp.float32), unroll=8
+                0, chunks, body, jnp.zeros((BLK, BLK), jnp.float32), unroll=True
             )
 
 

time: 122 us -> 121 us (level)
  waiting for transfers between devices: 54.2 us -> 52.2 us
  Pallas kernels: 5.01 us -> 6.44 us
    ppermute x1, waiting for transfers between devices: 2.95 us -> 0.89 us  [on_device(): lead_other = lax.ppermute(lead_all, 'core', swap)]
    pallas_call x2, Pallas kernels: 5.01 us -> 6.44 us  [block_products(): pl.pallas_call(functools.partial(block_kernel, n_grad, ny), out_shape=jax...]
  transfers between devices with their start and end apart: 29 -> 29, of which waited for: 15 -> 15; matrix products, arithmetic and copies ran while one was open for 9% -> 9% of each run, Pallas kernels for 1% -> 3%
where the time goes in v5:
time: 121 us; the launch traced here: 120 us
  waiting for transfers between devices  52.2 us (43%)
  starting transfers between devices  43.1 us (36%)
  local copies, waits for them, and re-layouts  11.4 us (9%)
  Pallas kernels  6.44 us (5%)
  other arithmetic  6.38 us (5%)
    ppermute x8, waiting for transfers between devices, relative_gather(): from_left = lax.ppermute(from_left, axis, right)  22.5 us
    ppermute x8, starting transfers between devices, relative_gather(): from_right = lax.ppermute(from_right, axis, left)  15.5 us
    ppermute x1, starting transfers between devices, on_device(): lead_other = lax.ppermute(lead_all, 'core', swap)  11.7 us
    ppermute x2, waiting for transfers between devices, relative_gather(): rel[n // 2] = lax.ppermute(from_left, axis, right)  9.55 us
    unnamed x25, local copies, waits for them, and re-layouts  7.89 us
    pallas_call x2, Pallas kernels, block_products(): pl.pallas_call(functools.partial(block_kernel, n_grad, ny), out_shape=jax...  6.44 us
    ppermute x1, waiting for transfers between devices, on_device(): trail_other = lax.ppermute(trail_all, 'core', swap)  6 us
    ppermute x8, waiting for transfers between devices, relative_gather(): from_right = lax.ppermute(from_right, axis, left)  5.21 us
  transfers between devices with their start and end apart: 29, of which 15 were waited for; matrix products, arithmetic and copies ran while one was open for 9% of the time, Pallas kernels for 3%

profile of v5, /device:TPU:1, one launch (start us, length us, event | category | flops | bytes accessed | tf_op | source)
XLA Modules:
  0.0 120.4 jit_solution(15286570796829250951)
XLA Ops:
  0.0 1.1 broadcast_select_fusion.2
  1.1 3.3 %collective-permute-start = (bf16[128,512]{1,0:T(8,128)(2,1)S(1)}, bf16[128,512]{1,0:T(8,128)(2,1)S(1)}, u32[]{:S(2)}, u32[]{:S(2)}) collective-permute-start(bf16[128,512]{1,0:T(8,128)(2,1)S(1)} %broadcast_select_fusion.2), channel_id=1, source_target_pairs={{0,1},{1,0},{2,3},{3,2},{4,5},{5,4},{6,7},{7,6},{8,9},{9,8},{10,11... | collective-permute-start | bytes 393224 | tf_op jit(solution)/shard_map/ppermute | solution.py:165
  6.4 3.9 %collective-permute-start.1 = (bf16[128,512]{1,0:T(8,128)(2,1)S(1)}, bf16[128,512]{1,0:T(8,128)(2,1)S(1)}, u32[]{:S(2)}, u32[]{:S(2)}) collective-permute-start(bf16[128,512]{1,0:T(8,128)(2,1)S(1)} %get-tuple-element.23), channel_id=1, source_target_pairs={{0,56},{8,0},{16,8},{24,16},{32,24},{40,32},{48,40},{56,48},{1,57}... | collective-permute-start | bytes 393224 | tf_op jit(solution)/shard_map/ppermute | solution.py:100
  11.3 1.4 %collective-permute-start.13 = (bf16[128,512]{1,0:T(8,128)(2,1)S(1)}, bf16[128,512]{1,0:T(8,128)(2,1)S(1)}, u32[]{:S(2)}, u32[]{:S(2)}) collective-permute-start(bf16[128,512]{1,0:T(8,128)(2,1)S(1)} %broadcast_select_fusion), channel_id=1, source_target_pairs={{0,2},{2,4},{4,6},{6,0},{1,3},{3,5},{5,7},{7,1},{8,10},{10,12},{12... | collective-permute-start | bytes 393224 | tf_op jit(solution)/shard_map/ppermute | solution.py:99
  12.7 1.5 %collective-permute-start.12 = (bf16[128,512]{1,0:T(8,128)(2,1)S(1)}, bf16[128,512]{1,0:T(8,128)(2,1)S(1)}, u32[]{:S(2)}, u32[]{:S(2)}) collective-permute-start(bf16[128,512]{1,0:T(8,128)(2,1)S(1)} %broadcast_select_fusion), channel_id=1, source_target_pairs={{0,6},{2,0},{4,2},{6,4},{1,7},{3,1},{5,3},{7,5},{8,14},{10,8},{12,... | collective-permute-start | bytes 393224 | tf_op jit(solution)/shard_map/ppermute | solution.py:100
  14.2 2.7 %collective-permute-start.2 = (bf16[128,512]{1,0:T(8,128)(2,1)S(1)}, bf16[128,512]{1,0:T(8,128)(2,1)S(1)}, u32[]{:S(2)}, u32[]{:S(2)}) collective-permute-start(bf16[128,512]{1,0:T(8,128)(2,1)S(1)} %collective-permute-done.1), channel_id=1, source_target_pairs={{0,56},{8,0},{16,8},{24,16},{32,24},{40,32},{48,40},{56,48},{1,57}... | collective-permute-start | bytes 393224 | tf_op jit(solution)/shard_map/ppermute | solution.py:100
  17.6 4.5 %collective-permute-done.14 = bf16[128,512]{1,0:T(8,128)(2,1)S(1)} collective-permute-done((bf16[128,512]{1,0:T(8,128)(2,1)S(1)}, bf16[128,512]{1,0:T(8,128)(2,1)S(1)}, u32[]{:S(2)}, u32[]{:S(2)}) %collective-permute-start.14) | collective-permute-done | bytes 131104 | tf_op jit(solution)/shard_map/ppermute | solution.py:104
  22.2 2.5 %collective-permute-start.15 = (bf16[4,128,512]{2,1,0:T(8,128)(2,1)S(1)}, bf16[4,128,512]{2,1,0:T(8,128)(2,1)S(1)}, u32[]{:S(2)}, u32[]{:S(2)}) collective-permute-start(bf16[4,128,512]{2,1,0:T(8,128)(2,1)S(1)} %pad_maximum_fusion.1), channel_id=1, source_target_pairs={{0,56},{8,0},{16,8},{24,16},{32,24},{40,32},{48,40},{56,48},{1,57}... | collective-permute-start | bytes 1572872 | tf_op jit(solution)/shard_map/ppermute | solution.py:100
  24.8 2.7 %collective-permute-start.3 = (bf16[128,512]{1,0:T(8,128)(2,1)S(1)}, bf16[128,512]{1,0:T(8,128)(2,1)S(1)}, u32[]{:S(2)}, u32[]{:S(2)}) collective-permute-start(bf16[128,512]{1,0:T(8,128)(2,1)S(1)} %collective-permute-done.2), channel_id=1, source_target_pairs={{0,56},{8,0},{16,8},{24,16},{32,24},{40,32},{48,40},{56,48},{1,57}... | collective-permute-start | bytes 393224 | tf_op jit(solution)/shard_map/ppermute | solution.py:100
  27.5 11.5 %collective-permute-done.6 = bf16[128,512]{1,0:T(8,128)(2,1)S(1)} collective-permute-done((bf16[128,512]{1,0:T(8,128)(2,1)S(1)}, bf16[128,512]{1,0:T(8,128)(2,1)S(1)}, u32[]{:S(2)}, u32[]{:S(2)}) %collective-permute-start.6) | collective-permute-done | bytes 131104 | tf_op jit(solution)/shard_map/ppermute | solution.py:99
  39.0 5.0 %collective-permute-done.7 = bf16[128,512]{1,0:T(8,128)(2,1)S(1)} collective-permute-done((bf16[128,512]{1,0:T(8,128)(2,1)S(1)}, bf16[128,512]{1,0:T(8,128)(2,1)S(1)}, u32[]{:S(2)}, u32[]{:S(2)}) %collective-permute-start.7) | collective-permute-done | bytes 131104 | tf_op jit(solution)/shard_map/ppermute | solution.py:104
  44.1 1.6 %collective-permute-start.8 = (bf16[8,128,512]{2,1,0:T(8,128)(2,1)S(1)}, bf16[8,128,512]{2,1,0:T(8,128)(2,1)S(1)}, u32[]{:S(2)}, u32[]{:S(2)}) collective-permute-start(bf16[8,128,512]{2,1,0:T(8,128)(2,1)S(1)} %bitcast_dynamic-update-slice_fusion.7), channel_id=1, source_target_pairs={{0,6},{2,0},{4,2},{6,4},{1,7},{3,1},{5,3},{7,5},{8,14},{10,8},{12,... | collective-permute-start | bytes 3145736 | tf_op jit(solution)/shard_map/ppermute | solution.py:100
  45.8 1.2 %collective-permute-start.23 = (bf16[2048,256]{1,0:T(8,128)(2,1)S(1)}, bf16[2048,256]{1,0:T(8,128)(2,1)S(1)}, u32[]{:S(2)}, u32[]{:S(2)}) collective-permute-start(bf16[2048,256]{1,0:T(8,128)(2,1)S(1)} %copy-done), channel_id=1, source_target_pairs={{0,64},{64,128},{128,192},{192,0},{1,65},{65,129},{129,193},{193,1... | collective-permute-start | bytes 3145736 | tf_op jit(solution)/shard_map/ppermute | solution.py:122
  47.0 1.5 %collective-permute-start.24 = (bf16[2048,256]{1,0:T(8,128)(2,1)S(1)}, bf16[2048,256]{1,0:T(8,128)(2,1)S(1)}, u32[]{:S(2)}, u32[]{:S(2)}) collective-permute-start(bf16[2048,256]{1,0:T(8,128)(2,1)S(1)} %copy-done), channel_id=1, source_target_pairs={{0,192},{64,0},{128,64},{192,128},{1,193},{65,1},{129,65},{193,129... | collective-permute-start | bytes 3145736 | tf_op jit(solution)/shard_map/ppermute | solution.py:123
  48.5 3.7 %collective-permute-done.16 = bf16[4,128,512]{2,1,0:T(8,128)(2,1)S(1)} collective-permute-done((bf16[4,128,512]{2,1,0:T(8,128)(2,1)S(1)}, bf16[4,128,512]{2,1,0:T(8,128)(2,1)S(1)}, u32[]{:S(2)}, u32[]{:S(2)}) %collective-permute-start.16) | collective-permute-done | bytes 524320 | tf_op jit(solution)/shard_map/ppermute | solution.py:100
  52.1 9.5 %collective-permute-done.19 = bf16[4,128,512]{2,1,0:T(8,128)(2,1)S(1)} collective-permute-done((bf16[4,128,512]{2,1,0:T(8,128)(2,1)S(1)}, bf16[4,128,512]{2,1,0:T(8,128)(2,1)S(1)}, u32[]{:S(2)}, u32[]{:S(2)}) %collective-permute-start.19) | collective-permute-done | bytes 524320 | tf_op jit(solution)/shard_map/ppermute | solution.py:99
  62.1 1.5 %collective-permute-done.8 = bf16[8,128,512]{2,1,0:T(8,128)(2,1)S(1)} collective-permute-done((bf16[8,128,512]{2,1,0:T(8,128)(2,1)S(1)}, bf16[8,128,512]{2,1,0:T(8,128)(2,1)S(1)}, u32[]{:S(2)}, u32[]{:S(2)}) %collective-permute-start.8) | collective-permute-done | bytes 1048608 | tf_op jit(solution)/shard_map/ppermute | solution.py:100
  63.6 1.2 collective-permute-start.20
  66.5 2.4 %collective-permute-start.11 = (bf16[4,128,512]{2,1,0:T(8,128)(2,1)S(1)}, bf16[4,128,512]{2,1,0:T(8,128)(2,1)S(1)}, u32[]{:S(2)}, u32[]{:S(2)}) collective-permute-start(bf16[4,128,512]{2,1,0:T(8,128)(2,1)S(1)} %slice.33), channel_id=1, source_target_pairs={{0,6},{2,0},{4,2},{6,4},{1,7},{3,1},{5,3},{7,5},{8,14},{10,8},{12,... | collective-permute-start | bytes 1572872 | tf_op jit(solution)/shard_map/ppermute | solution.py:109
  69.9 1.3 %collective-permute-start.25 = (bf16[1024,256]{1,0:T(8,128)(2,1)S(1)}, bf16[1024,256]{1,0:T(8,128)(2,1)S(1)}, u32[]{:S(2)}, u32[]{:S(2)}) collective-permute-start(bf16[1024,256]{1,0:T(8,128)(2,1)S(1)} %slice.36), channel_id=1, source_target_pairs={{0,64},{64,128},{128,192},{192,0},{1,65},{65,129},{129,193},{193,1... | collective-permute-start | bytes 1572872 | tf_op jit(solution)/shard_map/ppermute | solution.py:132
  72.1 1.5 %collective-permute-start.26 = (bf16[1024,256]{1,0:T(8,128)(2,1)S(1)}, bf16[1024,256]{1,0:T(8,128)(2,1)S(1)}, u32[]{:S(2)}, u32[]{:S(2)}) collective-permute-start(bf16[1024,256]{1,0:T(8,128)(2,1)S(1)} %slice.37), channel_id=1, source_target_pairs={{0,192},{64,0},{128,64},{192,128},{1,193},{65,1},{129,65},{193,129... | collective-permute-start | bytes 1572872 | tf_op jit(solution)/shard_map/ppermute | solution.py:133
  73.9 1.2 %collective-permute-start.22 = (bf16[2,128,512]{2,1,0:T(8,128)(2,1)S(1)}, bf16[2,128,512]{2,1,0:T(8,128)(2,1)S(1)}, u32[]{:S(2)}, u32[]{:S(2)}) collective-permute-start(bf16[2,128,512]{2,1,0:T(8,128)(2,1)S(1)} %slice.35), channel_id=1, source_target_pairs={{0,56},{8,0},{16,8},{24,16},{32,24},{40,32},{48,40},{56,48},{1,57}... | collective-permute-start | bytes 786440 | tf_op jit(solution)/shard_map/ppermute | solution.py:109
  76.5 2.1 %collective-permute-done.10 = bf16[4,128,512]{2,1,0:T(8,128)(2,1)S(1)} collective-permute-done((bf16[4,128,512]{2,1,0:T(8,128)(2,1)S(1)}, bf16[4,128,512]{2,1,0:T(8,128)(2,1)S(1)}, u32[]{:S(2)}, u32[]{:S(2)}) %collective-permute-start.10) | collective-permute-done | bytes 524320 | tf_op jit(solution)/shard_map/ppermute | solution.py:108
  79.3 2.4 %collective-permute-done.22 = bf16[2,128,512]{2,1,0:T(8,128)(2,1)S(1)} collective-permute-done((bf16[2,128,512]{2,1,0:T(8,128)(2,1)S(1)}, bf16[2,128,512]{2,1,0:T(8,128)(2,1)S(1)}, u32[]{:S(2)}, u32[]{:S(2)}) %collective-permute-start.22) | collective-permute-done | bytes 262176 | tf_op jit(solution)/shard_map/ppermute | solution.py:109
  81.7 2.5 %collective-permute-done.21 = bf16[2,128,512]{2,1,0:T(8,128)(2,1)S(1)} collective-permute-done((bf16[2,128,512]{2,1,0:T(8,128)(2,1)S(1)}, bf16[2,128,512]{2,1,0:T(8,128)(2,1)S(1)}, u32[]{:S(2)}, u32[]{:S(2)}) %collective-permute-start.21) | collective-permute-done | bytes 262176 | tf_op jit(solution)/shard_map/ppermute | solution.py:108
  85.9 2.4 %copy.6 = bf16[8,4,128,512]{3,2,1,0:T(8,128)(2,1)} copy(bf16[8,4,128,512]{3,2,0,1:T(8,128)(2,1)S(1)} %pad_maximum_fusion) | data formatting | bytes 8388608 | tf_op jit(solution)/shard_map/stack | solution.py:170
  91.6 11.7 %collective-permute-start.27 = (bf16[32,128,512]{2,1,0:T(8,128)(2,1)}, bf16[32,128,512]{2,1,0:T(8,128)(2,1)}, u32[]{:S(2)}, u32[]{:S(2)}) collective-permute-start(bf16[32,128,512]{2,1,0:T(8,128)(2,1)} %bitcast.22.rest_0_), channel_id=1, source_target_pairs={{0,1},{1,0},{2,3},{3,2},{4,5},{5,4},{6,7},{7,6},{8,9},{9,8},{10,11... | collective-permute-start | bytes 12582920 | tf_op jit(solution)/shard_map/ppermute | solution.py:180
  104.2 1.0 copy-done.2
  105.3 1.0 copy-done.4
  106.3 3.2 %shard_map.55 = f32[4,128,128]{2,1,0:T(8,128)S(1)} custom-call(s32[4]{0:T(128)S(1)} %and_select_fusion.2.rows_ref, s32[4]{0:T(128)S(1)} %clamp_bitcast_fusion.cols_ref, s32[4]{0:T(128)S(1)} %and_convert_fusion.1.use_ref, s32[5]{0:T(128)S(1)} %and_select_fusion.starts_ref, s32[2]{0:T(128)S(1)} %pad_add_fusion.place_ref, ...), custom_call_target="tpu_custom_call" | custom-call | flops 1073741824 | bytes 17039360 | tf_op jit(solution)/shard_map/pallas_call | solution.py:78
  110.4 6.0 %collective-permute-done.28.rest_1_ = bf16[32,128,512]{2,1,0:T(8,128)(2,1)} collective-permute-done((bf16[32,128,512]{2,1,0:T(8,128)(2,1)}, bf16[32,128,512]{2,1,0:T(8,128)(2,1)}, u32[]{:S(2)}, u32[]{:S(2)}) %collective-permute-start.28) | collective-permute-done | bytes 4194336 | tf_op jit(solution)/shard_map/ppermute | solution.py:181
  116.4 3.2 %shard_map.56 = f32[4,128,128]{2,1,0:T(8,128)S(1)} custom-call(s32[4]{0:T(128)S(1)} %and_select_fusion.2.rows_ref, s32[4]{0:T(128)S(1)} %clamp_bitcast_fusion.cols_ref, s32[4]{0:T(128)S(1)} %get-tuple-element.19.use_ref, s32[5]{0:T(128)S(1)} %and_select_fusion.starts_ref, s32[2]{0:T(128)S(1)} %pad_add_fusion.place_ref, ...), custom_call_target="tpu_custom_call" | custom-call | flops 1073741824 | bytes 17039360 | tf_op jit(solution)/shard_map/pallas_call | solution.py:78
  (78 shorter events, 17.1 us)
Async XLA Ops:
  0.0 45.8 %copy-start = (bf16[2048,256]{1,0:T(8,128)(2,1)S(1)}, bf16[2048,256]{1,0:T(8,128)(2,1)}, u32[]{:S(2)}) copy-start(bf16[2048,256]{1,0:T(8,128)(2,1)} %param.6) | copy-start | bytes 3145732
  1.1 4.3 %collective-permute-start = (bf16[128,512]{1,0:T(8,128)(2,1)S(1)}, bf16[128,512]{1,0:T(8,128)(2,1)S(1)}, u32[]{:S(2)}, u32[]{:S(2)}) collective-permute-start(bf16[128,512]{1,0:T(8,128)(2,1)S(1)} %broadcast_select_fusion.2), channel_id=1, source_target_pairs={{0,1},{1,0},{2,3},{3,2},{4,5},{5,4},{6,7},{7,6},{8,9},{9,8},{10,11... | collective-permute-start | bytes 393224 | tf_op jit(solution)/shard_map/ppermute | solution.py:165
  6.4 7.9 %collective-permute-start.1 = (bf16[128,512]{1,0:T(8,128)(2,1)S(1)}, bf16[128,512]{1,0:T(8,128)(2,1)S(1)}, u32[]{:S(2)}, u32[]{:S(2)}) collective-permute-start(bf16[128,512]{1,0:T(8,128)(2,1)S(1)} %get-tuple-element.23), channel_id=1, source_target_pairs={{0,56},{8,0},{16,8},{24,16},{32,24},{40,32},{48,40},{56,48},{1,57}... | collective-permute-start | bytes 393224 | tf_op jit(solution)/shard_map/ppermute | solution.py:100
  10.3 6.6 %collective-permute-start.4 = (bf16[128,512]{1,0:T(8,128)(2,1)S(1)}, bf16[128,512]{1,0:T(8,128)(2,1)S(1)}, u32[]{:S(2)}, u32[]{:S(2)}) collective-permute-start(bf16[128,512]{1,0:T(8,128)(2,1)S(1)} %get-tuple-element.23), channel_id=1, source_target_pairs={{0,8},{8,16},{16,24},{24,32},{32,40},{40,48},{48,56},{56,0},{1,9},... | collective-permute-start | bytes 393224 | tf_op jit(solution)/shard_map/ppermute | solution.py:99
  11.3 5.8 %collective-permute-start.13 = (bf16[128,512]{1,0:T(8,128)(2,1)S(1)}, bf16[128,512]{1,0:T(8,128)(2,1)S(1)}, u32[]{:S(2)}, u32[]{:S(2)}) collective-permute-start(bf16[128,512]{1,0:T(8,128)(2,1)S(1)} %broadcast_select_fusion), channel_id=1, source_target_pairs={{0,2},{2,4},{4,6},{6,0},{1,3},{3,5},{5,7},{7,1},{8,10},{10,12},{12... | collective-permute-start | bytes 393224 | tf_op jit(solution)/shard_map/ppermute | solution.py:99
  12.7 4.9 %collective-permute-start.12 = (bf16[128,512]{1,0:T(8,128)(2,1)S(1)}, bf16[128,512]{1,0:T(8,128)(2,1)S(1)}, u32[]{:S(2)}, u32[]{:S(2)}) collective-permute-start(bf16[128,512]{1,0:T(8,128)(2,1)S(1)} %broadcast_select_fusion), channel_id=1, source_target_pairs={{0,6},{2,0},{4,2},{6,4},{1,7},{3,1},{5,3},{7,5},{8,14},{10,8},{12,... | collective-permute-start | bytes 393224 | tf_op jit(solution)/shard_map/ppermute | solution.py:100
  14.2 10.5 %collective-permute-start.2 = (bf16[128,512]{1,0:T(8,128)(2,1)S(1)}, bf16[128,512]{1,0:T(8,128)(2,1)S(1)}, u32[]{:S(2)}, u32[]{:S(2)}) collective-permute-start(bf16[128,512]{1,0:T(8,128)(2,1)S(1)} %collective-permute-done.1), channel_id=1, source_target_pairs={{0,56},{8,0},{16,8},{24,16},{32,24},{40,32},{48,40},{56,48},{1,57}... | collective-permute-start | bytes 393224 | tf_op jit(solution)/shard_map/ppermute | solution.py:100
  16.9 10.5 %collective-permute-start.5 = (bf16[128,512]{1,0:T(8,128)(2,1)S(1)}, bf16[128,512]{1,0:T(8,128)(2,1)S(1)}, u32[]{:S(2)}, u32[]{:S(2)}) collective-permute-start(bf16[128,512]{1,0:T(8,128)(2,1)S(1)} %collective-permute-done.4), channel_id=1, source_target_pairs={{0,8},{8,16},{16,24},{24,32},{32,40},{40,48},{48,56},{56,0},{1,9},... | collective-permute-start | bytes 393224 | tf_op jit(solution)/shard_map/ppermute | solution.py:99
  17.1 5.0 %collective-permute-start.14 = (bf16[128,512]{1,0:T(8,128)(2,1)S(1)}, bf16[128,512]{1,0:T(8,128)(2,1)S(1)}, u32[]{:S(2)}, u32[]{:S(2)}) collective-permute-start(bf16[128,512]{1,0:T(8,128)(2,1)S(1)} %collective-permute-done.13), channel_id=1, source_target_pairs={{0,2},{2,4},{4,6},{6,0},{1,3},{3,5},{5,7},{7,1},{8,10},{10,12},{12... | collective-permute-start | bytes 393224 | tf_op jit(solution)/shard_map/ppermute | solution.py:104
  22.2 21.8 %collective-permute-start.15 = (bf16[4,128,512]{2,1,0:T(8,128)(2,1)S(1)}, bf16[4,128,512]{2,1,0:T(8,128)(2,1)S(1)}, u32[]{:S(2)}, u32[]{:S(2)}) collective-permute-start(bf16[4,128,512]{2,1,0:T(8,128)(2,1)S(1)} %pad_maximum_fusion.1), channel_id=1, source_target_pairs={{0,56},{8,0},{16,8},{24,16},{32,24},{40,32},{48,40},{56,48},{1,57}... | collective-permute-start | bytes 1572872 | tf_op jit(solution)/shard_map/ppermute | solution.py:100
  24.8 22.2 %collective-permute-start.18 = (bf16[4,128,512]{2,1,0:T(8,128)(2,1)S(1)}, bf16[4,128,512]{2,1,0:T(8,128)(2,1)S(1)}, u32[]{:S(2)}, u32[]{:S(2)}) collective-permute-start(bf16[4,128,512]{2,1,0:T(8,128)(2,1)S(1)} %pad_maximum_fusion.1), channel_id=1, source_target_pairs={{0,8},{8,16},{16,24},{24,32},{32,40},{40,48},{48,56},{56,0},{1,9},... | collective-permute-start | bytes 1572872 | tf_op jit(solution)/shard_map/ppermute | solution.py:99
  24.8 14.2 %collective-permute-start.3 = (bf16[128,512]{1,0:T(8,128)(2,1)S(1)}, bf16[128,512]{1,0:T(8,128)(2,1)S(1)}, u32[]{:S(2)}, u32[]{:S(2)}) collective-permute-start(bf16[128,512]{1,0:T(8,128)(2,1)S(1)} %collective-permute-done.2), channel_id=1, source_target_pairs={{0,56},{8,0},{16,8},{24,16},{32,24},{40,32},{48,40},{56,48},{1,57}... | collective-permute-start | bytes 393224 | tf_op jit(solution)/shard_map/ppermute | solution.py:100
  27.4 11.5 %collective-permute-start.6 = (bf16[128,512]{1,0:T(8,128)(2,1)S(1)}, bf16[128,512]{1,0:T(8,128)(2,1)S(1)}, u32[]{:S(2)}, u32[]{:S(2)}) collective-permute-start(bf16[128,512]{1,0:T(8,128)(2,1)S(1)} %collective-permute-done.5), channel_id=1, source_target_pairs={{0,8},{8,16},{16,24},{24,32},{32,40},{40,48},{48,56},{56,0},{1,9},... | collective-permute-start | bytes 393224 | tf_op jit(solution)/shard_map/ppermute | solution.py:99
  38.9 5.0 %collective-permute-start.7 = (bf16[128,512]{1,0:T(8,128)(2,1)S(1)}, bf16[128,512]{1,0:T(8,128)(2,1)S(1)}, u32[]{:S(2)}, u32[]{:S(2)}) collective-permute-start(bf16[128,512]{1,0:T(8,128)(2,1)S(1)} %collective-permute-done.6), channel_id=1, source_target_pairs={{0,8},{8,16},{16,24},{24,32},{32,40},{40,48},{48,56},{56,0},{1,9},... | collective-permute-start | bytes 393224 | tf_op jit(solution)/shard_map/ppermute | solution.py:104
  44.0 8.1 %collective-permute-start.16 = (bf16[4,128,512]{2,1,0:T(8,128)(2,1)S(1)}, bf16[4,128,512]{2,1,0:T(8,128)(2,1)S(1)}, u32[]{:S(2)}, u32[]{:S(2)}) collective-permute-start(bf16[4,128,512]{2,1,0:T(8,128)(2,1)S(1)} %collective-permute-done.15), channel_id=1, source_target_pairs={{0,56},{8,0},{16,8},{24,16},{32,24},{40,32},{48,40},{56,48},{1,57}... | collective-permute-start | bytes 1572872 | tf_op jit(solution)/shard_map/ppermute | solution.py:100
  44.1 19.5 %collective-permute-start.8 = (bf16[8,128,512]{2,1,0:T(8,128)(2,1)S(1)}, bf16[8,128,512]{2,1,0:T(8,128)(2,1)S(1)}, u32[]{:S(2)}, u32[]{:S(2)}) collective-permute-start(bf16[8,128,512]{2,1,0:T(8,128)(2,1)S(1)} %bitcast_dynamic-update-slice_fusion.7), channel_id=1, source_target_pairs={{0,6},{2,0},{4,2},{6,4},{1,7},{3,1},{5,3},{7,5},{8,14},{10,8},{12,... | collective-permute-start | bytes 3145736 | tf_op jit(solution)/shard_map/ppermute | solution.py:100
  45.8 20.7 %collective-permute-start.9 = (bf16[8,128,512]{2,1,0:T(8,128)(2,1)S(1)}, bf16[8,128,512]{2,1,0:T(8,128)(2,1)S(1)}, u32[]{:S(2)}, u32[]{:S(2)}) collective-permute-start(bf16[8,128,512]{2,1,0:T(8,128)(2,1)S(1)} %bitcast_dynamic-update-slice_fusion.7), channel_id=1, source_target_pairs={{0,2},{2,4},{4,6},{6,0},{1,3},{3,5},{5,7},{7,1},{8,10},{10,12},{12... | collective-permute-start | bytes 3145736 | tf_op jit(solution)/shard_map/ppermute | solution.py:99
  45.8 23.2 %collective-permute-start.23 = (bf16[2048,256]{1,0:T(8,128)(2,1)S(1)}, bf16[2048,256]{1,0:T(8,128)(2,1)S(1)}, u32[]{:S(2)}, u32[]{:S(2)}) collective-permute-start(bf16[2048,256]{1,0:T(8,128)(2,1)S(1)} %copy-done), channel_id=1, source_target_pairs={{0,64},{64,128},{128,192},{192,0},{1,65},{65,129},{129,193},{193,1... | collective-permute-start | bytes 3145736 | tf_op jit(solution)/shard_map/ppermute | solution.py:122
  47.0 22.9 %collective-permute-start.24 = (bf16[2048,256]{1,0:T(8,128)(2,1)S(1)}, bf16[2048,256]{1,0:T(8,128)(2,1)S(1)}, u32[]{:S(2)}, u32[]{:S(2)}) collective-permute-start(bf16[2048,256]{1,0:T(8,128)(2,1)S(1)} %copy-done), channel_id=1, source_target_pairs={{0,192},{64,0},{128,64},{192,128},{1,193},{65,1},{129,65},{193,129... | collective-permute-start | bytes 3145736 | tf_op jit(solution)/shard_map/ppermute | solution.py:123
  52.1 9.5 %collective-permute-start.19 = (bf16[4,128,512]{2,1,0:T(8,128)(2,1)S(1)}, bf16[4,128,512]{2,1,0:T(8,128)(2,1)S(1)}, u32[]{:S(2)}, u32[]{:S(2)}) collective-permute-start(bf16[4,128,512]{2,1,0:T(8,128)(2,1)S(1)} %collective-permute-done.18), channel_id=1, source_target_pairs={{0,8},{8,16},{16,24},{24,32},{32,40},{40,48},{48,56},{56,0},{1,9},... | collective-permute-start | bytes 1572872 | tf_op jit(solution)/shard_map/ppermute | solution.py:99
  61.7 10.4 %collective-permute-start.17 = (bf16[4,128,512]{2,1,0:T(8,128)(2,1)S(1)}, bf16[4,128,512]{2,1,0:T(8,128)(2,1)S(1)}, u32[]{:S(2)}, u32[]{:S(2)}) collective-permute-start(bf16[4,128,512]{2,1,0:T(8,128)(2,1)S(1)} %collective-permute-done.16), channel_id=1, source_target_pairs={{0,56},{8,0},{16,8},{24,16},{32,24},{40,32},{48,40},{56,48},{1,57}... | collective-permute-start | bytes 1572872 | tf_op jit(solution)/shard_map/ppermute | solution.py:100
  63.6 10.3 %collective-permute-start.20 = (bf16[4,128,512]{2,1,0:T(8,128)(2,1)S(1)}, bf16[4,128,512]{2,1,0:T(8,128)(2,1)S(1)}, u32[]{:S(2)}, u32[]{:S(2)}) collective-permute-start(bf16[4,128,512]{2,1,0:T(8,128)(2,1)S(1)} %collective-permute-done.19), channel_id=1, source_target_pairs={{0,8},{8,16},{16,24},{24,32},{32,40},{40,48},{48,56},{56,0},{1,9},... | collective-permute-start | bytes 1572872 | tf_op jit(solution)/shard_map/ppermute | solution.py:99
  66.5 9.5 %collective-permute-start.11 = (bf16[4,128,512]{2,1,0:T(8,128)(2,1)S(1)}, bf16[4,128,512]{2,1,0:T(8,128)(2,1)S(1)}, u32[]{:S(2)}, u32[]{:S(2)}) collective-permute-start(bf16[4,128,512]{2,1,0:T(8,128)(2,1)S(1)} %slice.33), channel_id=1, source_target_pairs={{0,6},{2,0},{4,2},{6,4},{1,7},{3,1},{5,3},{7,5},{8,14},{10,8},{12,... | collective-permute-start | bytes 1572872 | tf_op jit(solution)/shard_map/ppermute | solution.py:109
  69.0 9.6 %collective-permute-start.10 = (bf16[4,128,512]{2,1,0:T(8,128)(2,1)S(1)}, bf16[4,128,512]{2,1,0:T(8,128)(2,1)S(1)}, u32[]{:S(2)}, u32[]{:S(2)}) collective-permute-start(bf16[4,128,512]{2,1,0:T(8,128)(2,1)S(1)} %slice.32), channel_id=1, source_target_pairs={{0,2},{2,4},{4,6},{6,0},{1,3},{3,5},{5,7},{7,1},{8,10},{10,12},{12... | collective-permute-start | bytes 1572872 | tf_op jit(solution)/shard_map/ppermute | solution.py:108
  69.9 20.0 %collective-permute-start.25 = (bf16[1024,256]{1,0:T(8,128)(2,1)S(1)}, bf16[1024,256]{1,0:T(8,128)(2,1)S(1)}, u32[]{:S(2)}, u32[]{:S(2)}) collective-permute-start(bf16[1024,256]{1,0:T(8,128)(2,1)S(1)} %slice.36), channel_id=1, source_target_pairs={{0,64},{64,128},{128,192},{192,0},{1,65},{65,129},{129,193},{193,1... | collective-permute-start | bytes 1572872 | tf_op jit(solution)/shard_map/ppermute | solution.py:132
  72.1 18.7 %collective-permute-start.26 = (bf16[1024,256]{1,0:T(8,128)(2,1)S(1)}, bf16[1024,256]{1,0:T(8,128)(2,1)S(1)}, u32[]{:S(2)}, u32[]{:S(2)}) collective-permute-start(bf16[1024,256]{1,0:T(8,128)(2,1)S(1)} %slice.37), channel_id=1, source_target_pairs={{0,192},{64,0},{128,64},{192,128},{1,193},{65,1},{129,65},{193,129... | collective-permute-start | bytes 1572872 | tf_op jit(solution)/shard_map/ppermute | solution.py:133
  73.9 7.8 %collective-permute-start.22 = (bf16[2,128,512]{2,1,0:T(8,128)(2,1)S(1)}, bf16[2,128,512]{2,1,0:T(8,128)(2,1)S(1)}, u32[]{:S(2)}, u32[]{:S(2)}) collective-permute-start(bf16[2,128,512]{2,1,0:T(8,128)(2,1)S(1)} %slice.35), channel_id=1, source_target_pairs={{0,56},{8,0},{16,8},{24,16},{32,24},{40,32},{48,40},{56,48},{1,57}... | collective-permute-start | bytes 786440 | tf_op jit(solution)/shard_map/ppermute | solution.py:109
  76.0 8.1 %collective-permute-start.21 = (bf16[2,128,512]{2,1,0:T(8,128)(2,1)S(1)}, bf16[2,128,512]{2,1,0:T(8,128)(2,1)S(1)}, u32[]{:S(2)}, u32[]{:S(2)}) collective-permute-start(bf16[2,128,512]{2,1,0:T(8,128)(2,1)S(1)} %slice.34), channel_id=1, source_target_pairs={{0,8},{8,16},{16,24},{24,32},{32,40},{40,48},{48,56},{56,0},{1,9},... | collective-permute-start | bytes 786440 | tf_op jit(solution)/shard_map/ppermute | solution.py:108
  85.9 18.3 %copy-start.5 = (s32[1,1,4]{2,1,0:T(1,128)S(1)}, s32[1,1,4]{2,1,0:T(1,128)}, u32[]{:S(2)}) copy-start(s32[1,1,4]{2,1,0:T(1,128)} %param.7) | copy-start | bytes 52
  85.9 18.3 %copy-start.6 = (s32[1,1,4]{2,1,0:T(1,128)S(1)}, s32[1,1,4]{2,1,0:T(1,128)}, u32[]{:S(2)}) copy-start(s32[1,1,4]{2,1,0:T(1,128)} %param.8) | copy-start | bytes 52
  91.6 18.8 %collective-permute-start.27 = (bf16[32,128,512]{2,1,0:T(8,128)(2,1)}, bf16[32,128,512]{2,1,0:T(8,128)(2,1)}, u32[]{:S(2)}, u32[]{:S(2)}) collective-permute-start(bf16[32,128,512]{2,1,0:T(8,128)(2,1)} %bitcast.22.rest_0_), channel_id=1, source_target_pairs={{0,1},{1,0},{2,3},{3,2},{4,5},{5,4},{6,7},{7,6},{8,9},{9,8},{10,11... | collective-permute-start | bytes 12582920 | tf_op jit(solution)/shard_map/ppermute | solution.py:180
  103.3 13.1 %collective-permute-start.28 = (bf16[32,128,512]{2,1,0:T(8,128)(2,1)}, bf16[32,128,512]{2,1,0:T(8,128)(2,1)}, u32[]{:S(2)}, u32[]{:S(2)}) collective-permute-start(bf16[32,128,512]{2,1,0:T(8,128)(2,1)} %bitcast.35.rest_1_), channel_id=1, source_target_pairs={{0,1},{1,0},{2,3},{3,2},{4,5},{5,4},{6,7},{7,6},{8,9},{9,8},{10,11... | collective-permute-start | bytes 12582920 | tf_op jit(solution)/shard_map/ppermute | solution.py:181
  (4 other events, 3.7 us)

commit v6 on v4

--- a/solution.py
+++ b/solution.py
@@ -168,8 +168,26 @@
 
     lead_z = jnp.stack(relative_gather(lead, "z", nz, split=False), 0)
     trail_y = jnp.stack(relative_gather(trail, "y", ny, split=False), 0)
-    grad_pieces, starts = ring_gather(out_grad, "in", in_place)
-    lead_z, trail_y, grad_pieces = lax.optimization_barrier((lead_z, trail_y, grad_pieces))
+    n_in = lax.axis_size("in")
+    length = out_grad.shape[0]
+    right = [(k, (k + 1) % n_in) for k in range(n_in)]
+    left = [(k, (k - 1) % n_in) for k in range(n_in)]
+    from_left = lax.ppermute(out_grad, "in", right)
+    from_right = lax.ppermute(out_grad, "in", left)
+    lead_z, trail_y, from_left, from_right = lax.optimization_barrier(
+        (lead_z, trail_y, from_left, from_right)
+    )
+    grad_pieces = [out_grad, from_left, from_right]
+    offsets = [0, -1, 1]
+    for d in range(2, n_in // 2 + 1):
+        from_left = lax.ppermute(from_left, "in", right)
+        grad_pieces.append(from_left)
+        offsets.append(-d)
+        if 2 * d < n_in:
+            from_right = lax.ppermute(from_right, "in", left)
+            grad_pieces.append(from_right)
+            offsets.append(d)
+    starts = jnp.stack([((in_place + o) % n_in) * length for o in offsets]).astype(jnp.int32)
     lead_all = jnp.stack(relative_gather(lead_z, "y", ny), 1)
     trail_all = jnp.stack(relative_gather(trail_y, "z", nz), 0)
     lead_all = lead_all.reshape(nz * ny, tok, width)

time: 125 us -> 121 us (0.968)
  the two profiles are of different devices: /device:TPU:1 before, /device:TPU:3 now
where the time goes in v6:
time: 121 us; the launch traced here: 122 us
  waiting for transfers between devices  52.2 us (43%)
  starting transfers between devices  41.9 us (35%)
  local copies, waits for them, and re-layouts  10.7 us (9%)
  Pallas kernels  10.4 us (9%)
  other arithmetic  5.52 us (5%)
    ppermute x8, starting transfers between devices, relative_gather(): from_right = lax.ppermute(from_right, axis, left)  22.6 us
    ppermute x8, waiting for transfers between devices, relative_gather(): from_right = lax.ppermute(from_right, axis, left)  18.2 us
    pallas_call x2, Pallas kernels, block_products(): pl.pallas_call(functools.partial(block_kernel, n_grad, ny), out_shape=jax...  10.4 us
    ppermute x1, waiting for transfers between devices, on_device(): from_right = lax.ppermute(out_grad, 'in', left)  8.43 us
    ppermute x1, starting transfers between devices, on_device(): lead_other = lax.ppermute(lead_all, 'core', swap)  7.69 us
    unnamed x22, local copies, waits for them, and re-layouts  7.28 us
    ppermute x2, starting transfers between devices, relative_gather(): near_b = lax.ppermute(from_right[half:], axis, left)  6.45 us
    ppermute x1, waiting for transfers between devices, on_device(): trail_other = lax.ppermute(trail_all, 'core', swap)  6 us
  transfers between devices with their start and end apart: 28, of which 14 were waited for; matrix products, arithmetic and copies ran while one was open for 9% of the time, Pallas kernels for 3%

profile of v6, /device:TPU:3, one launch (start us, length us, event | category | flops | bytes accessed | tf_op | source)
XLA Modules:
  0.0 121.6 jit_solution(3921146041632746797)
XLA Ops:
  0.0 1.0 broadcast_select_fusion.2
  1.7 1.0 collective-permute-done
  2.7 1.0 bitcast_dynamic-update-slice_fusion.14
  3.8 5.7 %collective-permute-start.1 = (bf16[128,512]{1,0:T(8,128)(2,1)S(1)}, bf16[128,512]{1,0:T(8,128)(2,1)S(1)}, u32[]{:S(2)}, u32[]{:S(2)}) collective-permute-start(bf16[128,512]{1,0:T(8,128)(2,1)S(1)} %get-tuple-element.29), channel_id=1, source_target_pairs={{0,56},{8,0},{16,8},{24,16},{32,24},{40,32},{48,40},{56,48},{1,57}... | collective-permute-start | bytes 393224 | tf_op jit(solution)/shard_map/ppermute | solution.py:100
  9.4 1.0 broadcast_select_fusion
  10.4 1.4 %collective-permute-start.9 = (bf16[128,512]{1,0:T(8,128)(2,1)S(1)}, bf16[128,512]{1,0:T(8,128)(2,1)S(1)}, u32[]{:S(2)}, u32[]{:S(2)}) collective-permute-start(bf16[128,512]{1,0:T(8,128)(2,1)S(1)} %broadcast_select_fusion), channel_id=1, source_target_pairs={{0,2},{2,4},{4,6},{6,0},{1,3},{3,5},{5,7},{7,1},{8,10},{10,12},{12... | collective-permute-start | bytes 393224 | tf_op jit(solution)/shard_map/ppermute | solution.py:99
  11.8 1.2 collective-permute-start.11
  13.0 1.5 %collective-permute-start.8 = (bf16[128,512]{1,0:T(8,128)(2,1)S(1)}, bf16[128,512]{1,0:T(8,128)(2,1)S(1)}, u32[]{:S(2)}, u32[]{:S(2)}) collective-permute-start(bf16[128,512]{1,0:T(8,128)(2,1)S(1)} %broadcast_select_fusion), channel_id=1, source_target_pairs={{0,6},{2,0},{4,2},{6,4},{1,7},{3,1},{5,3},{7,5},{8,14},{10,8},{12,... | collective-permute-start | bytes 393224 | tf_op jit(solution)/shard_map/ppermute | solution.py:100
  14.5 2.7 %collective-permute-start.2 = (bf16[128,512]{1,0:T(8,128)(2,1)S(1)}, bf16[128,512]{1,0:T(8,128)(2,1)S(1)}, u32[]{:S(2)}, u32[]{:S(2)}) collective-permute-start(bf16[128,512]{1,0:T(8,128)(2,1)S(1)} %collective-permute-done.1), channel_id=1, source_target_pairs={{0,56},{8,0},{16,8},{24,16},{32,24},{40,32},{48,40},{56,48},{1,57}... | collective-permute-start | bytes 393224 | tf_op jit(solution)/shard_map/ppermute | solution.py:100
  17.3 1.8 %collective-permute-done.2 = bf16[128,512]{1,0:T(8,128)(2,1)S(1)} collective-permute-done((bf16[128,512]{1,0:T(8,128)(2,1)S(1)}, bf16[128,512]{1,0:T(8,128)(2,1)S(1)}, u32[]{:S(2)}, u32[]{:S(2)}) %collective-permute-start.2) | collective-permute-done | bytes 131104 | tf_op jit(solution)/shard_map/ppermute | solution.py:100
  19.2 3.1 %collective-permute-start.3 = (bf16[128,512]{1,0:T(8,128)(2,1)S(1)}, bf16[128,512]{1,0:T(8,128)(2,1)S(1)}, u32[]{:S(2)}, u32[]{:S(2)}) collective-permute-start(bf16[128,512]{1,0:T(8,128)(2,1)S(1)} %collective-permute-done.2), channel_id=1, source_target_pairs={{0,56},{8,0},{16,8},{24,16},{32,24},{40,32},{48,40},{56,48},{1,57}... | collective-permute-start | bytes 393224 | tf_op jit(solution)/shard_map/ppermute | solution.py:100
  23.0 4.3 %collective-permute-done.6 = bf16[128,512]{1,0:T(8,128)(2,1)S(1)} collective-permute-done((bf16[128,512]{1,0:T(8,128)(2,1)S(1)}, bf16[128,512]{1,0:T(8,128)(2,1)S(1)}, u32[]{:S(2)}, u32[]{:S(2)}) %collective-permute-start.6) | collective-permute-done | bytes 131104 | tf_op jit(solution)/shard_map/ppermute | solution.py:99
  27.3 5.0 %collective-permute-done.7 = bf16[128,512]{1,0:T(8,128)(2,1)S(1)} collective-permute-done((bf16[128,512]{1,0:T(8,128)(2,1)S(1)}, bf16[128,512]{1,0:T(8,128)(2,1)S(1)}, u32[]{:S(2)}, u32[]{:S(2)}) %collective-permute-start.7) | collective-permute-done | bytes 131104 | tf_op jit(solution)/shard_map/ppermute | solution.py:104
  32.4 3.4 %collective-permute-done.11 = bf16[2048,256]{1,0:T(8,128)(2,1)S(1)} collective-permute-done((bf16[2048,256]{1,0:T(8,128)(2,1)}, bf16[2048,256]{1,0:T(8,128)(2,1)S(1)}, u32[]{:S(2)}, u32[]{:S(2)}) %collective-permute-start.11) | collective-permute-done | bytes 1048608 | tf_op jit(solution)/shard_map/ppermute | solution.py:175
  35.8 8.4 %collective-permute-done.12 = bf16[2048,256]{1,0:T(8,128)(2,1)S(1)} collective-permute-done((bf16[2048,256]{1,0:T(8,128)(2,1)}, bf16[2048,256]{1,0:T(8,128)(2,1)S(1)}, u32[]{:S(2)}, u32[]{:S(2)}) %collective-permute-start.12) | collective-permute-done | bytes 1048608 | tf_op jit(solution)/shard_map/ppermute | solution.py:176
  44.2 1.8 %collective-permute-start.13 = (bf16[8,128,512]{2,1,0:T(8,128)(2,1)S(1)}, bf16[8,128,512]{2,1,0:T(8,128)(2,1)S(1)}, u32[]{:S(2)}, u32[]{:S(2)}) collective-permute-start(bf16[8,128,512]{2,1,0:T(8,128)(2,1)S(1)} %bitcast_dynamic-update-slice_fusion.7), channel_id=1, source_target_pairs={{0,6},{2,0},{4,2},{6,4},{1,7},{3,1},{5,3},{7,5},{8,14},{10,8},{12,... | collective-permute-start | bytes 3145736 | tf_op jit(solution)/shard_map/ppermute | solution.py:100
  46.0 2.4 %collective-permute-start.17 = (bf16[4,128,512]{2,1,0:T(8,128)(2,1)S(1)}, bf16[4,128,512]{2,1,0:T(8,128)(2,1)S(1)}, u32[]{:S(2)}, u32[]{:S(2)}) collective-permute-start(bf16[4,128,512]{2,1,0:T(8,128)(2,1)S(1)} %pad_maximum_fusion.1), channel_id=1, source_target_pairs={{0,56},{8,0},{16,8},{24,16},{32,24},{40,32},{48,40},{56,48},{1,57}... | collective-permute-start | bytes 1572872 | tf_op jit(solution)/shard_map/ppermute | solution.py:100
  48.4 7.0 %collective-permute-done.17 = bf16[4,128,512]{2,1,0:T(8,128)(2,1)S(1)} collective-permute-done((bf16[4,128,512]{2,1,0:T(8,128)(2,1)S(1)}, bf16[4,128,512]{2,1,0:T(8,128)(2,1)S(1)}, u32[]{:S(2)}, u32[]{:S(2)}) %collective-permute-start.17) | collective-permute-done | bytes 524320 | tf_op jit(solution)/shard_map/ppermute | solution.py:100
  55.4 3.3 %collective-permute-start.18 = (bf16[4,128,512]{2,1,0:T(8,128)(2,1)S(1)}, bf16[4,128,512]{2,1,0:T(8,128)(2,1)S(1)}, u32[]{:S(2)}, u32[]{:S(2)}) collective-permute-start(bf16[4,128,512]{2,1,0:T(8,128)(2,1)S(1)} %collective-permute-done.17), channel_id=1, source_target_pairs={{0,56},{8,0},{16,8},{24,16},{32,24},{40,32},{48,40},{56,48},{1,57}... | collective-permute-start | bytes 1572872 | tf_op jit(solution)/shard_map/ppermute | solution.py:100
  58.8 6.3 %collective-permute-done.13 = bf16[8,128,512]{2,1,0:T(8,128)(2,1)S(1)} collective-permute-done((bf16[8,128,512]{2,1,0:T(8,128)(2,1)S(1)}, bf16[8,128,512]{2,1,0:T(8,128)(2,1)S(1)}, u32[]{:S(2)}, u32[]{:S(2)}) %collective-permute-start.13) | collective-permute-done | bytes 1048608 | tf_op jit(solution)/shard_map/ppermute | solution.py:100
  65.1 3.3 %collective-permute-start.16 = (bf16[4,128,512]{2,1,0:T(8,128)(2,1)S(1)}, bf16[4,128,512]{2,1,0:T(8,128)(2,1)S(1)}, u32[]{:S(2)}, u32[]{:S(2)}) collective-permute-start(bf16[4,128,512]{2,1,0:T(8,128)(2,1)S(1)} %slice.25), channel_id=1, source_target_pairs={{0,6},{2,0},{4,2},{6,4},{1,7},{3,1},{5,3},{7,5},{8,14},{10,8},{12,... | collective-permute-start | bytes 1572872 | tf_op jit(solution)/shard_map/ppermute | solution.py:109
  68.5 2.2 %collective-permute-start.19 = (bf16[4,128,512]{2,1,0:T(8,128)(2,1)S(1)}, bf16[4,128,512]{2,1,0:T(8,128)(2,1)S(1)}, u32[]{:S(2)}, u32[]{:S(2)}) collective-permute-start(bf16[4,128,512]{2,1,0:T(8,128)(2,1)S(1)} %collective-permute-done.18), channel_id=1, source_target_pairs={{0,56},{8,0},{16,8},{24,16},{32,24},{40,32},{48,40},{56,48},{1,57}... | collective-permute-start | bytes 1572872 | tf_op jit(solution)/shard_map/ppermute | solution.py:100
  74.1 3.0 %collective-permute-done.19 = bf16[4,128,512]{2,1,0:T(8,128)(2,1)S(1)} collective-permute-done((bf16[4,128,512]{2,1,0:T(8,128)(2,1)S(1)}, bf16[4,128,512]{2,1,0:T(8,128)(2,1)S(1)}, u32[]{:S(2)}, u32[]{:S(2)}) %collective-permute-start.19) | collective-permute-done | bytes 524320 | tf_op jit(solution)/shard_map/ppermute | solution.py:100
  77.1 3.2 %collective-permute-start.24 = (bf16[2,128,512]{2,1,0:T(8,128)(2,1)S(1)}, bf16[2,128,512]{2,1,0:T(8,128)(2,1)S(1)}, u32[]{:S(2)}, u32[]{:S(2)}) collective-permute-start(bf16[2,128,512]{2,1,0:T(8,128)(2,1)S(1)} %slice.27), channel_id=1, source_target_pairs={{0,56},{8,0},{16,8},{24,16},{32,24},{40,32},{48,40},{56,48},{1,57}... | collective-permute-start | bytes 786440 | tf_op jit(solution)/shard_map/ppermute | solution.py:109
  81.6 2.4 %copy.6 = bf16[8,4,128,512]{3,2,1,0:T(8,128)(2,1)} copy(bf16[8,4,128,512]{3,2,0,1:T(8,128)(2,1)S(1)} %pad_maximum_fusion) | data formatting | bytes 8388608 | tf_op jit(solution)/shard_map/stack | solution.py:191
  85.7 3.4 %collective-permute-done.23 = bf16[2,128,512]{2,1,0:T(8,128)(2,1)S(1)} collective-permute-done((bf16[2,128,512]{2,1,0:T(8,128)(2,1)S(1)}, bf16[2,128,512]{2,1,0:T(8,128)(2,1)S(1)}, u32[]{:S(2)}, u32[]{:S(2)}) %collective-permute-start.23) | collective-permute-done | bytes 262176 | tf_op jit(solution)/shard_map/ppermute | solution.py:108
  93.4 7.7 %collective-permute-start.26 = (bf16[32,128,512]{2,1,0:T(8,128)(2,1)}, bf16[32,128,512]{2,1,0:T(8,128)(2,1)}, u32[]{:S(2)}, u32[]{:S(2)}) collective-permute-start(bf16[32,128,512]{2,1,0:T(8,128)(2,1)} %bitcast.25.rest_0_), channel_id=1, source_target_pairs={{0,1},{1,0},{2,3},{3,2},{4,5},{5,4},{6,7},{7,6},{8,9},{9,8},{10,11... | collective-permute-start | bytes 12582920 | tf_op jit(solution)/shard_map/ppermute | solution.py:199
  102.0 1.2 copy-done.2
  103.2 3.8 %shard_map.55 = f32[4,128,128]{2,1,0:T(8,128)S(1)} custom-call(s32[4]{0:T(128)S(1)} %get-tuple-element.31.rows_ref, s32[4]{0:T(128)S(1)} %clamp_bitcast_fusion.cols_ref, s32[4]{0:T(128)S(1)} %and_convert_fusion.1.use_ref, s32[4]{0:T(128)S(1)} %get-tuple-element.30.starts_ref, s32[2]{0:T(128)S(1)} %pad_add_fusion.1.place_ref, ...), custom_call_target="tpu_custom_call" | custom-call | flops 1073741824 | bytes 17039360 | tf_op jit(solution)/shard_map/pallas_call | solution.py:78
  107.1 1.2 collective-permute-done.26.rest_0_
  108.2 6.0 %collective-permute-done.27.rest_1_ = bf16[32,128,512]{2,1,0:T(8,128)(2,1)} collective-permute-done((bf16[32,128,512]{2,1,0:T(8,128)(2,1)}, bf16[32,128,512]{2,1,0:T(8,128)(2,1)}, u32[]{:S(2)}, u32[]{:S(2)}) %collective-permute-start.27) | collective-permute-done | bytes 4194336 | tf_op jit(solution)/shard_map/ppermute | solution.py:200
  114.2 6.6 %shard_map.56 = f32[4,128,128]{2,1,0:T(8,128)S(1)} custom-call(s32[4]{0:T(128)S(1)} %get-tuple-element.31.rows_ref, s32[4]{0:T(128)S(1)} %clamp_bitcast_fusion.cols_ref, s32[4]{0:T(128)S(1)} %get-tuple-element.25.use_ref, s32[4]{0:T(128)S(1)} %get-tuple-element.30.starts_ref, s32[2]{0:T(128)S(1)} %pad_add_fusion.1.place_ref, ...), custom_call_target="tpu_custom_call" | custom-call | flops 1073741824 | bytes 17039360 | tf_op jit(solution)/shard_map/pallas_call | solution.py:78
  (68 shorter events, 13.4 us)
Async XLA Ops:
  1.0 1.7 %collective-permute-start = (bf16[128,512]{1,0:T(8,128)(2,1)S(1)}, bf16[128,512]{1,0:T(8,128)(2,1)S(1)}, u32[]{:S(2)}, u32[]{:S(2)}) collective-permute-start(bf16[128,512]{1,0:T(8,128)(2,1)S(1)} %broadcast_select_fusion.2), channel_id=1, source_target_pairs={{0,1},{1,0},{2,3},{3,2},{4,5},{5,4},{6,7},{7,6},{8,9},{9,8},{10,11... | collective-permute-start | bytes 393224 | tf_op jit(solution)/shard_map/ppermute | solution.py:165
  3.8 10.8 %collective-permute-start.1 = (bf16[128,512]{1,0:T(8,128)(2,1)S(1)}, bf16[128,512]{1,0:T(8,128)(2,1)S(1)}, u32[]{:S(2)}, u32[]{:S(2)}) collective-permute-start(bf16[128,512]{1,0:T(8,128)(2,1)S(1)} %get-tuple-element.29), channel_id=1, source_target_pairs={{0,56},{8,0},{16,8},{24,16},{32,24},{40,32},{48,40},{56,48},{1,57}... | collective-permute-start | bytes 393224 | tf_op jit(solution)/shard_map/ppermute | solution.py:100
  9.4 7.8 %collective-permute-start.4 = (bf16[128,512]{1,0:T(8,128)(2,1)S(1)}, bf16[128,512]{1,0:T(8,128)(2,1)S(1)}, u32[]{:S(2)}, u32[]{:S(2)}) collective-permute-start(bf16[128,512]{1,0:T(8,128)(2,1)S(1)} %get-tuple-element.29), channel_id=1, source_target_pairs={{0,8},{8,16},{16,24},{24,32},{32,40},{40,48},{48,56},{56,0},{1,9},... | collective-permute-start | bytes 393224 | tf_op jit(solution)/shard_map/ppermute | solution.py:99
  10.4 6.8 %collective-permute-start.9 = (bf16[128,512]{1,0:T(8,128)(2,1)S(1)}, bf16[128,512]{1,0:T(8,128)(2,1)S(1)}, u32[]{:S(2)}, u32[]{:S(2)}) collective-permute-start(bf16[128,512]{1,0:T(8,128)(2,1)S(1)} %broadcast_select_fusion), channel_id=1, source_target_pairs={{0,2},{2,4},{4,6},{6,0},{1,3},{3,5},{5,7},{7,1},{8,10},{10,12},{12... | collective-permute-start | bytes 393224 | tf_op jit(solution)/shard_map/ppermute | solution.py:99
  11.8 24.0 %collective-permute-start.11 = (bf16[2048,256]{1,0:T(8,128)(2,1)}, bf16[2048,256]{1,0:T(8,128)(2,1)S(1)}, u32[]{:S(2)}, u32[]{:S(2)}) collective-permute-start(bf16[2048,256]{1,0:T(8,128)(2,1)} %param.6), channel_id=1, source_target_pairs={{0,64},{64,128},{128,192},{192,0},{1,65},{65,129},{129,193},{193,1... | collective-permute-start | bytes 3145736 | tf_op jit(solution)/shard_map/ppermute | solution.py:175
  13.0 9.3 %collective-permute-start.8 = (bf16[128,512]{1,0:T(8,128)(2,1)S(1)}, bf16[128,512]{1,0:T(8,128)(2,1)S(1)}, u32[]{:S(2)}, u32[]{:S(2)}) collective-permute-start(bf16[128,512]{1,0:T(8,128)(2,1)S(1)} %broadcast_select_fusion), channel_id=1, source_target_pairs={{0,6},{2,0},{4,2},{6,4},{1,7},{3,1},{5,3},{7,5},{8,14},{10,8},{12,... | collective-permute-start | bytes 393224 | tf_op jit(solution)/shard_map/ppermute | solution.py:100
  14.5 4.6 %collective-permute-start.2 = (bf16[128,512]{1,0:T(8,128)(2,1)S(1)}, bf16[128,512]{1,0:T(8,128)(2,1)S(1)}, u32[]{:S(2)}, u32[]{:S(2)}) collective-permute-start(bf16[128,512]{1,0:T(8,128)(2,1)S(1)} %collective-permute-done.1), channel_id=1, source_target_pairs={{0,56},{8,0},{16,8},{24,16},{32,24},{40,32},{48,40},{56,48},{1,57}... | collective-permute-start | bytes 393224 | tf_op jit(solution)/shard_map/ppermute | solution.py:100
  17.2 5.0 %collective-permute-start.5 = (bf16[128,512]{1,0:T(8,128)(2,1)S(1)}, bf16[128,512]{1,0:T(8,128)(2,1)S(1)}, u32[]{:S(2)}, u32[]{:S(2)}) collective-permute-start(bf16[128,512]{1,0:T(8,128)(2,1)S(1)} %collective-permute-done.4), channel_id=1, source_target_pairs={{0,8},{8,16},{16,24},{24,32},{32,40},{40,48},{48,56},{56,0},{1,9},... | collective-permute-start | bytes 393224 | tf_op jit(solution)/shard_map/ppermute | solution.py:99
  17.2 5.7 %collective-permute-start.10 = (bf16[128,512]{1,0:T(8,128)(2,1)S(1)}, bf16[128,512]{1,0:T(8,128)(2,1)S(1)}, u32[]{:S(2)}, u32[]{:S(2)}) collective-permute-start(bf16[128,512]{1,0:T(8,128)(2,1)S(1)} %collective-permute-done.9), channel_id=1, source_target_pairs={{0,2},{2,4},{4,6},{6,0},{1,3},{3,5},{5,7},{7,1},{8,10},{10,12},{12... | collective-permute-start | bytes 393224 | tf_op jit(solution)/shard_map/ppermute | solution.py:104
  19.2 8.1 %collective-permute-start.3 = (bf16[128,512]{1,0:T(8,128)(2,1)S(1)}, bf16[128,512]{1,0:T(8,128)(2,1)S(1)}, u32[]{:S(2)}, u32[]{:S(2)}) collective-permute-start(bf16[128,512]{1,0:T(8,128)(2,1)S(1)} %collective-permute-done.2), channel_id=1, source_target_pairs={{0,56},{8,0},{16,8},{24,16},{32,24},{40,32},{48,40},{56,48},{1,57}... | collective-permute-start | bytes 393224 | tf_op jit(solution)/shard_map/ppermute | solution.py:100
  22.2 5.0 %collective-permute-start.6 = (bf16[128,512]{1,0:T(8,128)(2,1)S(1)}, bf16[128,512]{1,0:T(8,128)(2,1)S(1)}, u32[]{:S(2)}, u32[]{:S(2)}) collective-permute-start(bf16[128,512]{1,0:T(8,128)(2,1)S(1)} %collective-permute-done.5), channel_id=1, source_target_pairs={{0,8},{8,16},{16,24},{24,32},{32,40},{40,48},{48,56},{56,0},{1,9},... | collective-permute-start | bytes 393224 | tf_op jit(solution)/shard_map/ppermute | solution.py:99
  22.3 22.0 %collective-permute-start.12 = (bf16[2048,256]{1,0:T(8,128)(2,1)}, bf16[2048,256]{1,0:T(8,128)(2,1)S(1)}, u32[]{:S(2)}, u32[]{:S(2)}) collective-permute-start(bf16[2048,256]{1,0:T(8,128)(2,1)} %param.6), channel_id=1, source_target_pairs={{0,192},{64,0},{128,64},{192,128},{1,193},{65,1},{129,65},{193,129... | collective-permute-start | bytes 3145736 | tf_op jit(solution)/shard_map/ppermute | solution.py:176
  27.3 5.0 %collective-permute-start.7 = (bf16[128,512]{1,0:T(8,128)(2,1)S(1)}, bf16[128,512]{1,0:T(8,128)(2,1)S(1)}, u32[]{:S(2)}, u32[]{:S(2)}) collective-permute-start(bf16[128,512]{1,0:T(8,128)(2,1)S(1)} %collective-permute-done.6), channel_id=1, source_target_pairs={{0,8},{8,16},{16,24},{24,32},{32,40},{40,48},{48,56},{56,0},{1,9},... | collective-permute-start | bytes 393224 | tf_op jit(solution)/shard_map/ppermute | solution.py:104
  44.2 20.8 %collective-permute-start.13 = (bf16[8,128,512]{2,1,0:T(8,128)(2,1)S(1)}, bf16[8,128,512]{2,1,0:T(8,128)(2,1)S(1)}, u32[]{:S(2)}, u32[]{:S(2)}) collective-permute-start(bf16[8,128,512]{2,1,0:T(8,128)(2,1)S(1)} %bitcast_dynamic-update-slice_fusion.7), channel_id=1, source_target_pairs={{0,6},{2,0},{4,2},{6,4},{1,7},{3,1},{5,3},{7,5},{8,14},{10,8},{12,... | collective-permute-start | bytes 3145736 | tf_op jit(solution)/shard_map/ppermute | solution.py:100
  46.0 22.3 %collective-permute-start.14 = (bf16[8,128,512]{2,1,0:T(8,128)(2,1)S(1)}, bf16[8,128,512]{2,1,0:T(8,128)(2,1)S(1)}, u32[]{:S(2)}, u32[]{:S(2)}) collective-permute-start(bf16[8,128,512]{2,1,0:T(8,128)(2,1)S(1)} %bitcast_dynamic-update-slice_fusion.7), channel_id=1, source_target_pairs={{0,2},{2,4},{4,6},{6,0},{1,3},{3,5},{5,7},{7,1},{8,10},{10,12},{12... | collective-permute-start | bytes 3145736 | tf_op jit(solution)/shard_map/ppermute | solution.py:99
  46.0 9.4 %collective-permute-start.17 = (bf16[4,128,512]{2,1,0:T(8,128)(2,1)S(1)}, bf16[4,128,512]{2,1,0:T(8,128)(2,1)S(1)}, u32[]{:S(2)}, u32[]{:S(2)}) collective-permute-start(bf16[4,128,512]{2,1,0:T(8,128)(2,1)S(1)} %pad_maximum_fusion.1), channel_id=1, source_target_pairs={{0,56},{8,0},{16,8},{24,16},{32,24},{40,32},{48,40},{56,48},{1,57}... | collective-permute-start | bytes 1572872 | tf_op jit(solution)/shard_map/ppermute | solution.py:100
  48.4 10.3 %collective-permute-start.20 = (bf16[4,128,512]{2,1,0:T(8,128)(2,1)S(1)}, bf16[4,128,512]{2,1,0:T(8,128)(2,1)S(1)}, u32[]{:S(2)}, u32[]{:S(2)}) collective-permute-start(bf16[4,128,512]{2,1,0:T(8,128)(2,1)S(1)} %pad_maximum_fusion.1), channel_id=1, source_target_pairs={{0,8},{8,16},{16,24},{24,32},{32,40},{40,48},{48,56},{56,0},{1,9},... | collective-permute-start | bytes 1572872 | tf_op jit(solution)/shard_map/ppermute | solution.py:99
  55.4 13.0 %collective-permute-start.18 = (bf16[4,128,512]{2,1,0:T(8,128)(2,1)S(1)}, bf16[4,128,512]{2,1,0:T(8,128)(2,1)S(1)}, u32[]{:S(2)}, u32[]{:S(2)}) collective-permute-start(bf16[4,128,512]{2,1,0:T(8,128)(2,1)S(1)} %collective-permute-done.17), channel_id=1, source_target_pairs={{0,56},{8,0},{16,8},{24,16},{32,24},{40,32},{48,40},{56,48},{1,57}... | collective-permute-start | bytes 1572872 | tf_op jit(solution)/shard_map/ppermute | solution.py:100
  58.7 11.9 %collective-permute-start.21 = (bf16[4,128,512]{2,1,0:T(8,128)(2,1)S(1)}, bf16[4,128,512]{2,1,0:T(8,128)(2,1)S(1)}, u32[]{:S(2)}, u32[]{:S(2)}) collective-permute-start(bf16[4,128,512]{2,1,0:T(8,128)(2,1)S(1)} %collective-permute-done.20), channel_id=1, source_target_pairs={{0,8},{8,16},{16,24},{24,32},{32,40},{40,48},{48,56},{56,0},{1,9},... | collective-permute-start | bytes 1572872 | tf_op jit(solution)/shard_map/ppermute | solution.py:99
  65.1 15.9 %collective-permute-start.16 = (bf16[4,128,512]{2,1,0:T(8,128)(2,1)S(1)}, bf16[4,128,512]{2,1,0:T(8,128)(2,1)S(1)}, u32[]{:S(2)}, u32[]{:S(2)}) collective-permute-start(bf16[4,128,512]{2,1,0:T(8,128)(2,1)S(1)} %slice.25), channel_id=1, source_target_pairs={{0,6},{2,0},{4,2},{6,4},{1,7},{3,1},{5,3},{7,5},{8,14},{10,8},{12,... | collective-permute-start | bytes 1572872 | tf_op jit(solution)/shard_map/ppermute | solution.py:109
  68.4 12.6 %collective-permute-start.15 = (bf16[4,128,512]{2,1,0:T(8,128)(2,1)S(1)}, bf16[4,128,512]{2,1,0:T(8,128)(2,1)S(1)}, u32[]{:S(2)}, u32[]{:S(2)}) collective-permute-start(bf16[4,128,512]{2,1,0:T(8,128)(2,1)S(1)} %slice.24), channel_id=1, source_target_pairs={{0,2},{2,4},{4,6},{6,0},{1,3},{3,5},{5,7},{7,1},{8,10},{10,12},{12... | collective-permute-start | bytes 1572872 | tf_op jit(solution)/shard_map/ppermute | solution.py:108
  68.5 8.6 %collective-permute-start.19 = (bf16[4,128,512]{2,1,0:T(8,128)(2,1)S(1)}, bf16[4,128,512]{2,1,0:T(8,128)(2,1)S(1)}, u32[]{:S(2)}, u32[]{:S(2)}) collective-permute-start(bf16[4,128,512]{2,1,0:T(8,128)(2,1)S(1)} %collective-permute-done.18), channel_id=1, source_target_pairs={{0,56},{8,0},{16,8},{24,16},{32,24},{40,32},{48,40},{56,48},{1,57}... | collective-permute-start | bytes 1572872 | tf_op jit(solution)/shard_map/ppermute | solution.py:100
  70.7 10.1 %collective-permute-start.22 = (bf16[4,128,512]{2,1,0:T(8,128)(2,1)S(1)}, bf16[4,128,512]{2,1,0:T(8,128)(2,1)S(1)}, u32[]{:S(2)}, u32[]{:S(2)}) collective-permute-start(bf16[4,128,512]{2,1,0:T(8,128)(2,1)S(1)} %collective-permute-done.21), channel_id=1, source_target_pairs={{0,8},{8,16},{16,24},{24,32},{32,40},{40,48},{48,56},{56,0},{1,9},... | collective-permute-start | bytes 1572872 | tf_op jit(solution)/shard_map/ppermute | solution.py:99
  71.5 20.9 %collective-permute-start.25 = (bf16[2048,256]{1,0:T(8,128)(2,1)S(1)}, bf16[2048,256]{1,0:T(8,128)(2,1)S(1)}, u32[]{:S(2)}, u32[]{:S(2)}) collective-permute-start(bf16[2048,256]{1,0:T(8,128)(2,1)S(1)} %collective-permute-done.11), channel_id=1, source_target_pairs={{0,64},{64,128},{128,192},{192,0},{1,65},{65,129},{129,193},{193,1... | collective-permute-start | bytes 3145736 | tf_op jit(solution)/shard_map/ppermute | solution.py:183
  77.1 8.5 %collective-permute-start.24 = (bf16[2,128,512]{2,1,0:T(8,128)(2,1)S(1)}, bf16[2,128,512]{2,1,0:T(8,128)(2,1)S(1)}, u32[]{:S(2)}, u32[]{:S(2)}) collective-permute-start(bf16[2,128,512]{2,1,0:T(8,128)(2,1)S(1)} %slice.27), channel_id=1, source_target_pairs={{0,56},{8,0},{16,8},{24,16},{32,24},{40,32},{48,40},{56,48},{1,57}... | collective-permute-start | bytes 786440 | tf_op jit(solution)/shard_map/ppermute | solution.py:109
  80.8 8.2 %collective-permute-start.23 = (bf16[2,128,512]{2,1,0:T(8,128)(2,1)S(1)}, bf16[2,128,512]{2,1,0:T(8,128)(2,1)S(1)}, u32[]{:S(2)}, u32[]{:S(2)}) collective-permute-start(bf16[2,128,512]{2,1,0:T(8,128)(2,1)S(1)} %slice.26), channel_id=1, source_target_pairs={{0,8},{8,16},{16,24},{24,32},{32,40},{40,48},{48,56},{56,0},{1,9},... | collective-permute-start | bytes 786440 | tf_op jit(solution)/shard_map/ppermute | solution.py:108
  84.1 17.8 %copy-start.4 = (s32[1,1,4]{2,1,0:T(1,128)S(1)}, s32[1,1,4]{2,1,0:T(1,128)}, u32[]{:S(2)}) copy-start(s32[1,1,4]{2,1,0:T(1,128)} %param.8) | copy-start | bytes 52
  84.1 17.8 %copy-start.3 = (s32[1,1,4]{2,1,0:T(1,128)S(1)}, s32[1,1,4]{2,1,0:T(1,128)}, u32[]{:S(2)}) copy-start(s32[1,1,4]{2,1,0:T(1,128)} %param.7) | copy-start | bytes 52
  84.1 17.9 %copy-start = (bf16[2048,256]{1,0:T(8,128)(2,1)S(1)}, bf16[2048,256]{1,0:T(8,128)(2,1)}, u32[]{:S(2)}) copy-start(bf16[2048,256]{1,0:T(8,128)(2,1)} %param.6) | copy-start | bytes 3145732
  93.4 14.8 %collective-permute-start.26 = (bf16[32,128,512]{2,1,0:T(8,128)(2,1)}, bf16[32,128,512]{2,1,0:T(8,128)(2,1)}, u32[]{:S(2)}, u32[]{:S(2)}) collective-permute-start(bf16[32,128,512]{2,1,0:T(8,128)(2,1)} %bitcast.25.rest_0_), channel_id=1, source_target_pairs={{0,1},{1,0},{2,3},{3,2},{4,5},{5,4},{6,7},{7,6},{8,9},{9,8},{10,11... | collective-permute-start | bytes 12582920 | tf_op jit(solution)/shard_map/ppermute | solution.py:199
  101.1 13.1 %collective-permute-start.27 = (bf16[32,128,512]{2,1,0:T(8,128)(2,1)}, bf16[32,128,512]{2,1,0:T(8,128)(2,1)}, u32[]{:S(2)}, u32[]{:S(2)}) collective-permute-start(bf16[32,128,512]{2,1,0:T(8,128)(2,1)} %bitcast.34.rest_1_), channel_id=1, source_target_pairs={{0,1},{1,0},{2,3},{3,2},{4,5},{5,4},{6,7},{7,6},{8,9},{9,8},{10,11... | collective-permute-start | bytes 12582920 | tf_op jit(solution)/shard_map/ppermute | solution.py:200
  102.0 1.2 %copy-start.2 = (bf16[2048,256]{1,0:T(8,128)(2,1)S(1)}, bf16[2048,256]{1,0:T(8,128)(2,1)}, u32[]{:S(2)}) copy-start(bf16[2048,256]{1,0:T(8,128)(2,1)} %copy-done.1) | copy-start | bytes 3145732
  (1 other events, 1.0 us)

commit v7 on v3

--- a/solution.py
+++ b/solution.py
@@ -174,7 +174,7 @@
     trail_all = trail_all.reshape(nz * ny, tok, width)
 
     grad_pieces, starts = ring_gather(out_grad, "in", in_place)
-    lead_all, trail_all, grad_pieces = lax.optimization_barrier((lead_all, trail_all, grad_pieces))
+    lead_all, grad_pieces = lax.optimization_barrier((lead_all, grad_pieces))
     grad_pieces = [g.reshape(g.shape[0] // (2 * tok), 2, tok, g.shape[1]) for g in grad_pieces]
     starts = starts // (2 * tok)
     lead_other = lax.ppermute(lead_all, "core", swap)

time: 122 us -> 111 us (0.910)
  waiting for transfers between devices: 54.2 us -> 39.8 us
  Pallas kernels: 5.01 us -> 7.72 us
  starting transfers between devices: 43.1 us -> 44.8 us
    ppermute x1, waiting for transfers between devices: 6 us -> 0.25 us  [on_device(): trail_other = lax.ppermute(trail_all, 'core', swap)]
    ppermute x2, waiting for transfers between devices: 4.61 us -> 1.32 us  [relative_gather(): near_a = lax.ppermute(from_left[:half], axis, right)]
    ppermute x1, waiting for transfers between devices: 2.95 us -> 0.01 us  [on_device(): lead_other = lax.ppermute(lead_all, 'core', swap)]
    ppermute x1, starting transfers between devices: 0.01 us -> 2.82 us  [on_device(): trail_other = lax.ppermute(trail_all, 'core', swap)]
    pallas_call x2, Pallas kernels: 5.01 us -> 7.72 us  [block_products(): pl.pallas_call(functools.partial(block_kernel, n_grad, ny), out_shape=jax...]
    ppermute x2, waiting for transfers between devices: 2.43 us -> 0.01 us  [relative_gather(): near_b = lax.ppermute(from_right[half:], axis, left)]
  transfers between devices with their start and end apart: 29 -> 29, of which waited for: 15 -> 12; matrix products, arithmetic and copies ran while one was open for 9% -> 10% of each run, Pallas kernels for 1% -> 3%
where the time goes in v7:
time: 111 us
  starting transfers between devices  44.8 us (40%)
  waiting for transfers between devices  39.8 us (36%)
  local copies, waits for them, and re-layouts  11.4 us (10%)
  Pallas kernels  7.72 us (7%)
  other arithmetic  6.38 us (6%)
    ppermute x8, waiting for transfers between devices, relative_gather(): from_left = lax.ppermute(from_left, axis, right)  23.3 us
    ppermute x8, starting transfers between devices, relative_gather(): from_right = lax.ppermute(from_right, axis, left)  15.5 us
    ppermute x1, starting transfers between devices, on_device(): lead_other = lax.ppermute(lead_all, 'core', swap)  10.6 us
    ppermute x2, waiting for transfers between devices, relative_gather(): rel[n // 2] = lax.ppermute(from_left, axis, right)  9.55 us
    unnamed x25, local copies, waits for them, and re-layouts  7.88 us
    pallas_call x2, Pallas kernels, block_products(): pl.pallas_call(functools.partial(block_kernel, n_grad, ny), out_shape=jax...  7.72 us
    ppermute x8, waiting for transfers between devices, relative_gather(): from_right = lax.ppermute(from_right, axis, left)  4.36 us
    ppermute x1, starting transfers between devices, on_device(): recv = lax.ppermute(send, 'core', swap)  3.29 us
  transfers between devices with their start and end apart: 29, of which 12 were waited for; matrix products, arithmetic and copies ran while one was open for 10% of the time, Pallas kernels for 3%

profile of v7, /device:TPU:1, one launch (start us, length us, event | category | flops | bytes accessed | tf_op | source)
XLA Modules:
  0.0 111.1 jit_solution(9541733810023623046)
XLA Ops:
  0.0 1.1 broadcast_select_fusion.2
  1.1 3.3 %collective-permute-start = (bf16[128,512]{1,0:T(8,128)(2,1)S(1)}, bf16[128,512]{1,0:T(8,128)(2,1)S(1)}, u32[]{:S(2)}, u32[]{:S(2)}) collective-permute-start(bf16[128,512]{1,0:T(8,128)(2,1)S(1)} %broadcast_select_fusion.2), channel_id=1, source_target_pairs={{0,1},{1,0},{2,3},{3,2},{4,5},{5,4},{6,7},{7,6},{8,9},{9,8},{10,11... | collective-permute-start | bytes 393224 | tf_op jit(solution)/shard_map/ppermute | solution.py:165
  5.4 1.0 bitcast_dynamic-update-slice_fusion.14
  6.4 3.9 %collective-permute-start.1 = (bf16[128,512]{1,0:T(8,128)(2,1)S(1)}, bf16[128,512]{1,0:T(8,128)(2,1)S(1)}, u32[]{:S(2)}, u32[]{:S(2)}) collective-permute-start(bf16[128,512]{1,0:T(8,128)(2,1)S(1)} %get-tuple-element.21), channel_id=1, source_target_pairs={{0,56},{8,0},{16,8},{24,16},{32,24},{40,32},{48,40},{56,48},{1,57}... | collective-permute-start | bytes 393224 | tf_op jit(solution)/shard_map/ppermute | solution.py:100
  11.3 1.4 %collective-permute-start.17 = (bf16[128,512]{1,0:T(8,128)(2,1)S(1)}, bf16[128,512]{1,0:T(8,128)(2,1)S(1)}, u32[]{:S(2)}, u32[]{:S(2)}) collective-permute-start(bf16[128,512]{1,0:T(8,128)(2,1)S(1)} %broadcast_select_fusion), channel_id=1, source_target_pairs={{0,2},{2,4},{4,6},{6,0},{1,3},{3,5},{5,7},{7,1},{8,10},{10,12},{12... | collective-permute-start | bytes 393224 | tf_op jit(solution)/shard_map/ppermute | solution.py:99
  12.7 1.5 %collective-permute-start.16 = (bf16[128,512]{1,0:T(8,128)(2,1)S(1)}, bf16[128,512]{1,0:T(8,128)(2,1)S(1)}, u32[]{:S(2)}, u32[]{:S(2)}) collective-permute-start(bf16[128,512]{1,0:T(8,128)(2,1)S(1)} %broadcast_select_fusion), channel_id=1, source_target_pairs={{0,6},{2,0},{4,2},{6,4},{1,7},{3,1},{5,3},{7,5},{8,14},{10,8},{12,... | collective-permute-start | bytes 393224 | tf_op jit(solution)/shard_map/ppermute | solution.py:100
  14.2 2.7 %collective-permute-start.2 = (bf16[128,512]{1,0:T(8,128)(2,1)S(1)}, bf16[128,512]{1,0:T(8,128)(2,1)S(1)}, u32[]{:S(2)}, u32[]{:S(2)}) collective-permute-start(bf16[128,512]{1,0:T(8,128)(2,1)S(1)} %collective-permute-done.1), channel_id=1, source_target_pairs={{0,56},{8,0},{16,8},{24,16},{32,24},{40,32},{48,40},{56,48},{1,57}... | collective-permute-start | bytes 393224 | tf_op jit(solution)/shard_map/ppermute | solution.py:100
  17.6 4.5 %collective-permute-done.18 = bf16[128,512]{1,0:T(8,128)(2,1)S(1)} collective-permute-done((bf16[128,512]{1,0:T(8,128)(2,1)S(1)}, bf16[128,512]{1,0:T(8,128)(2,1)S(1)}, u32[]{:S(2)}, u32[]{:S(2)}) %collective-permute-start.18) | collective-permute-done | bytes 131104 | tf_op jit(solution)/shard_map/ppermute | solution.py:104
  22.2 2.5 %collective-permute-start.19 = (bf16[4,128,512]{2,1,0:T(8,128)(2,1)S(1)}, bf16[4,128,512]{2,1,0:T(8,128)(2,1)S(1)}, u32[]{:S(2)}, u32[]{:S(2)}) collective-permute-start(bf16[4,128,512]{2,1,0:T(8,128)(2,1)S(1)} %pad_maximum_fusion.1), channel_id=1, source_target_pairs={{0,56},{8,0},{16,8},{24,16},{32,24},{40,32},{48,40},{56,48},{1,57}... | collective-permute-start | bytes 1572872 | tf_op jit(solution)/shard_map/ppermute | solution.py:100
  24.8 2.7 %collective-permute-start.3 = (bf16[128,512]{1,0:T(8,128)(2,1)S(1)}, bf16[128,512]{1,0:T(8,128)(2,1)S(1)}, u32[]{:S(2)}, u32[]{:S(2)}) collective-permute-start(bf16[128,512]{1,0:T(8,128)(2,1)S(1)} %collective-permute-done.2), channel_id=1, source_target_pairs={{0,56},{8,0},{16,8},{24,16},{32,24},{40,32},{48,40},{56,48},{1,57}... | collective-permute-start | bytes 393224 | tf_op jit(solution)/shard_map/ppermute | solution.py:100
  27.5 11.5 %collective-permute-done.6 = bf16[128,512]{1,0:T(8,128)(2,1)S(1)} collective-permute-done((bf16[128,512]{1,0:T(8,128)(2,1)S(1)}, bf16[128,512]{1,0:T(8,128)(2,1)S(1)}, u32[]{:S(2)}, u32[]{:S(2)}) %collective-permute-start.6) | collective-permute-done | bytes 131104 | tf_op jit(solution)/shard_map/ppermute | solution.py:99
  39.0 5.0 %collective-permute-done.7 = bf16[128,512]{1,0:T(8,128)(2,1)S(1)} collective-permute-done((bf16[128,512]{1,0:T(8,128)(2,1)S(1)}, bf16[128,512]{1,0:T(8,128)(2,1)S(1)}, u32[]{:S(2)}, u32[]{:S(2)}) %collective-permute-start.7) | collective-permute-done | bytes 131104 | tf_op jit(solution)/shard_map/ppermute | solution.py:104
  44.1 1.6 %collective-permute-start.8 = (bf16[8,128,512]{2,1,0:T(8,128)(2,1)S(1)}, bf16[8,128,512]{2,1,0:T(8,128)(2,1)S(1)}, u32[]{:S(2)}, u32[]{:S(2)}) collective-permute-start(bf16[8,128,512]{2,1,0:T(8,128)(2,1)S(1)} %bitcast_dynamic-update-slice_fusion.7), channel_id=1, source_target_pairs={{0,6},{2,0},{4,2},{6,4},{1,7},{3,1},{5,3},{7,5},{8,14},{10,8},{12,... | collective-permute-start | bytes 3145736 | tf_op jit(solution)/shard_map/ppermute | solution.py:100
  45.8 1.2 %collective-permute-start.12 = (bf16[2048,256]{1,0:T(8,128)(2,1)S(1)}, bf16[2048,256]{1,0:T(8,128)(2,1)S(1)}, u32[]{:S(2)}, u32[]{:S(2)}) collective-permute-start(bf16[2048,256]{1,0:T(8,128)(2,1)S(1)} %copy-done), channel_id=1, source_target_pairs={{0,64},{64,128},{128,192},{192,0},{1,65},{65,129},{129,193},{193,1... | collective-permute-start | bytes 3145736 | tf_op jit(solution)/shard_map/ppermute | solution.py:122
  47.0 1.5 %collective-permute-start.13 = (bf16[2048,256]{1,0:T(8,128)(2,1)S(1)}, bf16[2048,256]{1,0:T(8,128)(2,1)S(1)}, u32[]{:S(2)}, u32[]{:S(2)}) collective-permute-start(bf16[2048,256]{1,0:T(8,128)(2,1)S(1)} %copy-done), channel_id=1, source_target_pairs={{0,192},{64,0},{128,64},{192,128},{1,193},{65,1},{129,65},{193,129... | collective-permute-start | bytes 3145736 | tf_op jit(solution)/shard_map/ppermute | solution.py:123
  48.5 3.7 %collective-permute-done.20 = bf16[4,128,512]{2,1,0:T(8,128)(2,1)S(1)} collective-permute-done((bf16[4,128,512]{2,1,0:T(8,128)(2,1)S(1)}, bf16[4,128,512]{2,1,0:T(8,128)(2,1)S(1)}, u32[]{:S(2)}, u32[]{:S(2)}) %collective-permute-start.20) | collective-permute-done | bytes 524320 | tf_op jit(solution)/shard_map/ppermute | solution.py:100
  52.1 9.5 %collective-permute-done.23 = bf16[4,128,512]{2,1,0:T(8,128)(2,1)S(1)} collective-permute-done((bf16[4,128,512]{2,1,0:T(8,128)(2,1)S(1)}, bf16[4,128,512]{2,1,0:T(8,128)(2,1)S(1)}, u32[]{:S(2)}, u32[]{:S(2)}) %collective-permute-start.23) | collective-permute-done | bytes 524320 | tf_op jit(solution)/shard_map/ppermute | solution.py:99
  63.6 1.2 %collective-permute-start.24 = (bf16[4,128,512]{2,1,0:T(8,128)(2,1)S(1)}, bf16[4,128,512]{2,1,0:T(8,128)(2,1)S(1)}, u32[]{:S(2)}, u32[]{:S(2)}) collective-permute-start(bf16[4,128,512]{2,1,0:T(8,128)(2,1)S(1)} %collective-permute-done.23), channel_id=1, source_target_pairs={{0,8},{8,16},{16,24},{24,32},{32,40},{40,48},{48,56},{56,0},{1,9},... | collective-permute-start | bytes 1572872 | tf_op jit(solution)/shard_map/ppermute | solution.py:99
  64.8 1.7 %collective-permute-done.9 = bf16[8,128,512]{2,1,0:T(8,128)(2,1)S(1)} collective-permute-done((bf16[8,128,512]{2,1,0:T(8,128)(2,1)S(1)}, bf16[8,128,512]{2,1,0:T(8,128)(2,1)S(1)}, u32[]{:S(2)}, u32[]{:S(2)}) %collective-permute-start.9) | collective-permute-done | bytes 1048608 | tf_op jit(solution)/shard_map/ppermute | solution.py:99
  66.5 1.6 %collective-permute-start.11 = (bf16[4,128,512]{2,1,0:T(8,128)(2,1)S(1)}, bf16[4,128,512]{2,1,0:T(8,128)(2,1)S(1)}, u32[]{:S(2)}, u32[]{:S(2)}) collective-permute-start(bf16[4,128,512]{2,1,0:T(8,128)(2,1)S(1)} %slice.33), channel_id=1, source_target_pairs={{0,6},{2,0},{4,2},{6,4},{1,7},{3,1},{5,3},{7,5},{8,14},{10,8},{12,... | collective-permute-start | bytes 1572872 | tf_op jit(solution)/shard_map/ppermute | solution.py:109
  69.1 1.3 %collective-permute-start.14 = (bf16[1024,256]{1,0:T(8,128)(2,1)S(1)}, bf16[1024,256]{1,0:T(8,128)(2,1)S(1)}, u32[]{:S(2)}, u32[]{:S(2)}) collective-permute-start(bf16[1024,256]{1,0:T(8,128)(2,1)S(1)} %slice.34), channel_id=1, source_target_pairs={{0,64},{64,128},{128,192},{192,0},{1,65},{65,129},{129,193},{193,1... | collective-permute-start | bytes 1572872 | tf_op jit(solution)/shard_map/ppermute | solution.py:132
  71.2 1.5 %collective-permute-start.15 = (bf16[1024,256]{1,0:T(8,128)(2,1)S(1)}, bf16[1024,256]{1,0:T(8,128)(2,1)S(1)}, u32[]{:S(2)}, u32[]{:S(2)}) collective-permute-start(bf16[1024,256]{1,0:T(8,128)(2,1)S(1)} %slice.35), channel_id=1, source_target_pairs={{0,192},{64,0},{128,64},{192,128},{1,193},{65,1},{129,65},{193,129... | collective-permute-start | bytes 1572872 | tf_op jit(solution)/shard_map/ppermute | solution.py:133
  73.9 1.2 %collective-permute-start.26 = (bf16[2,128,512]{2,1,0:T(8,128)(2,1)S(1)}, bf16[2,128,512]{2,1,0:T(8,128)(2,1)S(1)}, u32[]{:S(2)}, u32[]{:S(2)}) collective-permute-start(bf16[2,128,512]{2,1,0:T(8,128)(2,1)S(1)} %slice.37), channel_id=1, source_target_pairs={{0,56},{8,0},{16,8},{24,16},{32,24},{40,32},{48,40},{56,48},{1,57}... | collective-permute-start | bytes 786440 | tf_op jit(solution)/shard_map/ppermute | solution.py:109
  75.2 1.3 %collective-permute-start.25 = (bf16[2,128,512]{2,1,0:T(8,128)(2,1)S(1)}, bf16[2,128,512]{2,1,0:T(8,128)(2,1)S(1)}, u32[]{:S(2)}, u32[]{:S(2)}) collective-permute-start(bf16[2,128,512]{2,1,0:T(8,128)(2,1)S(1)} %slice.36), channel_id=1, source_target_pairs={{0,8},{8,16},{16,24},{24,32},{32,40},{40,48},{48,56},{56,0},{1,9},... | collective-permute-start | bytes 786440 | tf_op jit(solution)/shard_map/ppermute | solution.py:108
  76.5 1.3 %collective-permute-done.10 = bf16[4,128,512]{2,1,0:T(8,128)(2,1)S(1)} collective-permute-done((bf16[4,128,512]{2,1,0:T(8,128)(2,1)S(1)}, bf16[4,128,512]{2,1,0:T(8,128)(2,1)S(1)}, u32[]{:S(2)}, u32[]{:S(2)}) %collective-permute-start.10) | collective-permute-done | bytes 524320 | tf_op jit(solution)/shard_map/ppermute | solution.py:108
  78.5 2.4 %copy.6 = bf16[8,4,128,512]{3,2,1,0:T(8,128)(2,1)} copy(bf16[8,4,128,512]{3,2,0,1:T(8,128)(2,1)S(1)} %pad_maximum_fusion) | data formatting | bytes 8388608 | tf_op jit(solution)/shard_map/stack | solution.py:170
  82.5 10.6 %collective-permute-start.27 = (bf16[32,128,512]{2,1,0:T(8,128)(2,1)}, bf16[32,128,512]{2,1,0:T(8,128)(2,1)}, u32[]{:S(2)}, u32[]{:S(2)}) collective-permute-start(bf16[32,128,512]{2,1,0:T(8,128)(2,1)} %bitcast.22.rest_0_), channel_id=1, source_target_pairs={{0,1},{1,0},{2,3},{3,2},{4,5},{5,4},{6,7},{7,6},{8,9},{9,8},{10,11... | collective-permute-start | bytes 12582920 | tf_op jit(solution)/shard_map/ppermute | solution.py:180
  96.5 2.8 %collective-permute-start.28 = (bf16[32,128,512]{2,1,0:T(8,128)(2,1)}, bf16[32,128,512]{2,1,0:T(8,128)(2,1)}, u32[]{:S(2)}, u32[]{:S(2)}) collective-permute-start(bf16[32,128,512]{2,1,0:T(8,128)(2,1)} %bitcast.35.rest_1_), channel_id=1, source_target_pairs={{0,1},{1,0},{2,3},{3,2},{4,5},{5,4},{6,7},{7,6},{8,9},{9,8},{10,11... | collective-permute-start | bytes 12582920 | tf_op jit(solution)/shard_map/ppermute | solution.py:181
  100.3 1.0 copy-done.2
  101.3 1.0 copy-done.4
  102.3 3.9 %shard_map.55 = f32[4,128,128]{2,1,0:T(8,128)S(1)} custom-call(s32[4]{0:T(128)S(1)} %and_select_fusion.2.rows_ref, s32[4]{0:T(128)S(1)} %clamp_bitcast_fusion.cols_ref, s32[4]{0:T(128)S(1)} %and_convert_fusion.1.use_ref, s32[5]{0:T(128)S(1)} %and_select_fusion.starts_ref, s32[2]{0:T(128)S(1)} %pad_add_fusion.place_ref, ...), custom_call_target="tpu_custom_call" | custom-call | flops 1073741824 | bytes 17039360 | tf_op jit(solution)/shard_map/pallas_call | solution.py:78
  106.5 3.9 %shard_map.56 = f32[4,128,128]{2,1,0:T(8,128)S(1)} custom-call(s32[4]{0:T(128)S(1)} %and_select_fusion.2.rows_ref, s32[4]{0:T(128)S(1)} %clamp_bitcast_fusion.cols_ref, s32[4]{0:T(128)S(1)} %get-tuple-element.17.use_ref, s32[5]{0:T(128)S(1)} %and_select_fusion.starts_ref, s32[2]{0:T(128)S(1)} %pad_add_fusion.place_ref, ...), custom_call_target="tpu_custom_call" | custom-call | flops 1073741824 | bytes 17039360 | tf_op jit(solution)/shard_map/pallas_call | solution.py:78
  (78 shorter events, 14.8 us)
Async XLA Ops:
  0.0 45.8 %copy-start = (bf16[2048,256]{1,0:T(8,128)(2,1)S(1)}, bf16[2048,256]{1,0:T(8,128)(2,1)}, u32[]{:S(2)}) copy-start(bf16[2048,256]{1,0:T(8,128)(2,1)} %param.6) | copy-start | bytes 3145732
  1.1 4.3 %collective-permute-start = (bf16[128,512]{1,0:T(8,128)(2,1)S(1)}, bf16[128,512]{1,0:T(8,128)(2,1)S(1)}, u32[]{:S(2)}, u32[]{:S(2)}) collective-permute-start(bf16[128,512]{1,0:T(8,128)(2,1)S(1)} %broadcast_select_fusion.2), channel_id=1, source_target_pairs={{0,1},{1,0},{2,3},{3,2},{4,5},{5,4},{6,7},{7,6},{8,9},{9,8},{10,11... | collective-permute-start | bytes 393224 | tf_op jit(solution)/shard_map/ppermute | solution.py:165
  6.4 7.9 %collective-permute-start.1 = (bf16[128,512]{1,0:T(8,128)(2,1)S(1)}, bf16[128,512]{1,0:T(8,128)(2,1)S(1)}, u32[]{:S(2)}, u32[]{:S(2)}) collective-permute-start(bf16[128,512]{1,0:T(8,128)(2,1)S(1)} %get-tuple-element.21), channel_id=1, source_target_pairs={{0,56},{8,0},{16,8},{24,16},{32,24},{40,32},{48,40},{56,48},{1,57}... | collective-permute-start | bytes 393224 | tf_op jit(solution)/shard_map/ppermute | solution.py:100
  10.3 6.6 %collective-permute-start.4 = (bf16[128,512]{1,0:T(8,128)(2,1)S(1)}, bf16[128,512]{1,0:T(8,128)(2,1)S(1)}, u32[]{:S(2)}, u32[]{:S(2)}) collective-permute-start(bf16[128,512]{1,0:T(8,128)(2,1)S(1)} %get-tuple-element.21), channel_id=1, source_target_pairs={{0,8},{8,16},{16,24},{24,32},{32,40},{40,48},{48,56},{56,0},{1,9},... | collective-permute-start | bytes 393224 | tf_op jit(solution)/shard_map/ppermute | solution.py:99
  11.3 5.8 %collective-permute-start.17 = (bf16[128,512]{1,0:T(8,128)(2,1)S(1)}, bf16[128,512]{1,0:T(8,128)(2,1)S(1)}, u32[]{:S(2)}, u32[]{:S(2)}) collective-permute-start(bf16[128,512]{1,0:T(8,128)(2,1)S(1)} %broadcast_select_fusion), channel_id=1, source_target_pairs={{0,2},{2,4},{4,6},{6,0},{1,3},{3,5},{5,7},{7,1},{8,10},{10,12},{12... | collective-permute-start | bytes 393224 | tf_op jit(solution)/shard_map/ppermute | solution.py:99
  12.7 4.9 %collective-permute-start.16 = (bf16[128,512]{1,0:T(8,128)(2,1)S(1)}, bf16[128,512]{1,0:T(8,128)(2,1)S(1)}, u32[]{:S(2)}, u32[]{:S(2)}) collective-permute-start(bf16[128,512]{1,0:T(8,128)(2,1)S(1)} %broadcast_select_fusion), channel_id=1, source_target_pairs={{0,6},{2,0},{4,2},{6,4},{1,7},{3,1},{5,3},{7,5},{8,14},{10,8},{12,... | collective-permute-start | bytes 393224 | tf_op jit(solution)/shard_map/ppermute | solution.py:100
  14.2 10.5 %collective-permute-start.2 = (bf16[128,512]{1,0:T(8,128)(2,1)S(1)}, bf16[128,512]{1,0:T(8,128)(2,1)S(1)}, u32[]{:S(2)}, u32[]{:S(2)}) collective-permute-start(bf16[128,512]{1,0:T(8,128)(2,1)S(1)} %collective-permute-done.1), channel_id=1, source_target_pairs={{0,56},{8,0},{16,8},{24,16},{32,24},{40,32},{48,40},{56,48},{1,57}... | collective-permute-start | bytes 393224 | tf_op jit(solution)/shard_map/ppermute | solution.py:100
  16.9 10.5 %collective-permute-start.5 = (bf16[128,512]{1,0:T(8,128)(2,1)S(1)}, bf16[128,512]{1,0:T(8,128)(2,1)S(1)}, u32[]{:S(2)}, u32[]{:S(2)}) collective-permute-start(bf16[128,512]{1,0:T(8,128)(2,1)S(1)} %collective-permute-done.4), channel_id=1, source_target_pairs={{0,8},{8,16},{16,24},{24,32},{32,40},{40,48},{48,56},{56,0},{1,9},... | collective-permute-start | bytes 393224 | tf_op jit(solution)/shard_map/ppermute | solution.py:99
  17.1 5.0 %collective-permute-start.18 = (bf16[128,512]{1,0:T(8,128)(2,1)S(1)}, bf16[128,512]{1,0:T(8,128)(2,1)S(1)}, u32[]{:S(2)}, u32[]{:S(2)}) collective-permute-start(bf16[128,512]{1,0:T(8,128)(2,1)S(1)} %collective-permute-done.17), channel_id=1, source_target_pairs={{0,2},{2,4},{4,6},{6,0},{1,3},{3,5},{5,7},{7,1},{8,10},{10,12},{12... | collective-permute-start | bytes 393224 | tf_op jit(solution)/shard_map/ppermute | solution.py:104
  22.2 21.8 %collective-permute-start.19 = (bf16[4,128,512]{2,1,0:T(8,128)(2,1)S(1)}, bf16[4,128,512]{2,1,0:T(8,128)(2,1)S(1)}, u32[]{:S(2)}, u32[]{:S(2)}) collective-permute-start(bf16[4,128,512]{2,1,0:T(8,128)(2,1)S(1)} %pad_maximum_fusion.1), channel_id=1, source_target_pairs={{0,56},{8,0},{16,8},{24,16},{32,24},{40,32},{48,40},{56,48},{1,57}... | collective-permute-start | bytes 1572872 | tf_op jit(solution)/shard_map/ppermute | solution.py:100
  24.8 22.2 %collective-permute-start.22 = (bf16[4,128,512]{2,1,0:T(8,128)(2,1)S(1)}, bf16[4,128,512]{2,1,0:T(8,128)(2,1)S(1)}, u32[]{:S(2)}, u32[]{:S(2)}) collective-permute-start(bf16[4,128,512]{2,1,0:T(8,128)(2,1)S(1)} %pad_maximum_fusion.1), channel_id=1, source_target_pairs={{0,8},{8,16},{16,24},{24,32},{32,40},{40,48},{48,56},{56,0},{1,9},... | collective-permute-start | bytes 1572872 | tf_op jit(solution)/shard_map/ppermute | solution.py:99
  24.8 14.2 %collective-permute-start.3 = (bf16[128,512]{1,0:T(8,128)(2,1)S(1)}, bf16[128,512]{1,0:T(8,128)(2,1)S(1)}, u32[]{:S(2)}, u32[]{:S(2)}) collective-permute-start(bf16[128,512]{1,0:T(8,128)(2,1)S(1)} %collective-permute-done.2), channel_id=1, source_target_pairs={{0,56},{8,0},{16,8},{24,16},{32,24},{40,32},{48,40},{56,48},{1,57}... | collective-permute-start | bytes 393224 | tf_op jit(solution)/shard_map/ppermute | solution.py:100
  27.4 11.5 %collective-permute-start.6 = (bf16[128,512]{1,0:T(8,128)(2,1)S(1)}, bf16[128,512]{1,0:T(8,128)(2,1)S(1)}, u32[]{:S(2)}, u32[]{:S(2)}) collective-permute-start(bf16[128,512]{1,0:T(8,128)(2,1)S(1)} %collective-permute-done.5), channel_id=1, source_target_pairs={{0,8},{8,16},{16,24},{24,32},{32,40},{40,48},{48,56},{56,0},{1,9},... | collective-permute-start | bytes 393224 | tf_op jit(solution)/shard_map/ppermute | solution.py:99
  38.9 5.0 %collective-permute-start.7 = (bf16[128,512]{1,0:T(8,128)(2,1)S(1)}, bf16[128,512]{1,0:T(8,128)(2,1)S(1)}, u32[]{:S(2)}, u32[]{:S(2)}) collective-permute-start(bf16[128,512]{1,0:T(8,128)(2,1)S(1)} %collective-permute-done.6), channel_id=1, source_target_pairs={{0,8},{8,16},{16,24},{24,32},{32,40},{40,48},{48,56},{56,0},{1,9},... | collective-permute-start | bytes 393224 | tf_op jit(solution)/shard_map/ppermute | solution.py:104
  44.0 8.1 %collective-permute-start.20 = (bf16[4,128,512]{2,1,0:T(8,128)(2,1)S(1)}, bf16[4,128,512]{2,1,0:T(8,128)(2,1)S(1)}, u32[]{:S(2)}, u32[]{:S(2)}) collective-permute-start(bf16[4,128,512]{2,1,0:T(8,128)(2,1)S(1)} %collective-permute-done.19), channel_id=1, source_target_pairs={{0,56},{8,0},{16,8},{24,16},{32,24},{40,32},{48,40},{56,48},{1,57}... | collective-permute-start | bytes 1572872 | tf_op jit(solution)/shard_map/ppermute | solution.py:100
  44.1 19.5 %collective-permute-start.8 = (bf16[8,128,512]{2,1,0:T(8,128)(2,1)S(1)}, bf16[8,128,512]{2,1,0:T(8,128)(2,1)S(1)}, u32[]{:S(2)}, u32[]{:S(2)}) collective-permute-start(bf16[8,128,512]{2,1,0:T(8,128)(2,1)S(1)} %bitcast_dynamic-update-slice_fusion.7), channel_id=1, source_target_pairs={{0,6},{2,0},{4,2},{6,4},{1,7},{3,1},{5,3},{7,5},{8,14},{10,8},{12,... | collective-permute-start | bytes 3145736 | tf_op jit(solution)/shard_map/ppermute | solution.py:100
  45.8 20.7 %collective-permute-start.9 = (bf16[8,128,512]{2,1,0:T(8,128)(2,1)S(1)}, bf16[8,128,512]{2,1,0:T(8,128)(2,1)S(1)}, u32[]{:S(2)}, u32[]{:S(2)}) collective-permute-start(bf16[8,128,512]{2,1,0:T(8,128)(2,1)S(1)} %bitcast_dynamic-update-slice_fusion.7), channel_id=1, source_target_pairs={{0,2},{2,4},{4,6},{6,0},{1,3},{3,5},{5,7},{7,1},{8,10},{10,12},{12... | collective-permute-start | bytes 3145736 | tf_op jit(solution)/shard_map/ppermute | solution.py:99
  45.8 22.3 %collective-permute-start.12 = (bf16[2048,256]{1,0:T(8,128)(2,1)S(1)}, bf16[2048,256]{1,0:T(8,128)(2,1)S(1)}, u32[]{:S(2)}, u32[]{:S(2)}) collective-permute-start(bf16[2048,256]{1,0:T(8,128)(2,1)S(1)} %copy-done), channel_id=1, source_target_pairs={{0,64},{64,128},{128,192},{192,0},{1,65},{65,129},{129,193},{193,1... | collective-permute-start | bytes 3145736 | tf_op jit(solution)/shard_map/ppermute | solution.py:122
  47.0 22.1 %collective-permute-start.13 = (bf16[2048,256]{1,0:T(8,128)(2,1)S(1)}, bf16[2048,256]{1,0:T(8,128)(2,1)S(1)}, u32[]{:S(2)}, u32[]{:S(2)}) collective-permute-start(bf16[2048,256]{1,0:T(8,128)(2,1)S(1)} %copy-done), channel_id=1, source_target_pairs={{0,192},{64,0},{128,64},{192,128},{1,193},{65,1},{129,65},{193,129... | collective-permute-start | bytes 3145736 | tf_op jit(solution)/shard_map/ppermute | solution.py:123
  52.1 9.5 %collective-permute-start.23 = (bf16[4,128,512]{2,1,0:T(8,128)(2,1)S(1)}, bf16[4,128,512]{2,1,0:T(8,128)(2,1)S(1)}, u32[]{:S(2)}, u32[]{:S(2)}) collective-permute-start(bf16[4,128,512]{2,1,0:T(8,128)(2,1)S(1)} %collective-permute-done.22), channel_id=1, source_target_pairs={{0,8},{8,16},{16,24},{24,32},{32,40},{40,48},{48,56},{56,0},{1,9},... | collective-permute-start | bytes 1572872 | tf_op jit(solution)/shard_map/ppermute | solution.py:99
  61.7 9.6 %collective-permute-start.21 = (bf16[4,128,512]{2,1,0:T(8,128)(2,1)S(1)}, bf16[4,128,512]{2,1,0:T(8,128)(2,1)S(1)}, u32[]{:S(2)}, u32[]{:S(2)}) collective-permute-start(bf16[4,128,512]{2,1,0:T(8,128)(2,1)S(1)} %collective-permute-done.20), channel_id=1, source_target_pairs={{0,56},{8,0},{16,8},{24,16},{32,24},{40,32},{48,40},{56,48},{1,57}... | collective-permute-start | bytes 1572872 | tf_op jit(solution)/shard_map/ppermute | solution.py:100
  63.6 10.3 %collective-permute-start.24 = (bf16[4,128,512]{2,1,0:T(8,128)(2,1)S(1)}, bf16[4,128,512]{2,1,0:T(8,128)(2,1)S(1)}, u32[]{:S(2)}, u32[]{:S(2)}) collective-permute-start(bf16[4,128,512]{2,1,0:T(8,128)(2,1)S(1)} %collective-permute-done.23), channel_id=1, source_target_pairs={{0,8},{8,16},{16,24},{24,32},{32,40},{40,48},{48,56},{56,0},{1,9},... | collective-permute-start | bytes 1572872 | tf_op jit(solution)/shard_map/ppermute | solution.py:99
  66.5 8.7 %collective-permute-start.11 = (bf16[4,128,512]{2,1,0:T(8,128)(2,1)S(1)}, bf16[4,128,512]{2,1,0:T(8,128)(2,1)S(1)}, u32[]{:S(2)}, u32[]{:S(2)}) collective-permute-start(bf16[4,128,512]{2,1,0:T(8,128)(2,1)S(1)} %slice.33), channel_id=1, source_target_pairs={{0,6},{2,0},{4,2},{6,4},{1,7},{3,1},{5,3},{7,5},{8,14},{10,8},{12,... | collective-permute-start | bytes 1572872 | tf_op jit(solution)/shard_map/ppermute | solution.py:109
  68.1 9.7 %collective-permute-start.10 = (bf16[4,128,512]{2,1,0:T(8,128)(2,1)S(1)}, bf16[4,128,512]{2,1,0:T(8,128)(2,1)S(1)}, u32[]{:S(2)}, u32[]{:S(2)}) collective-permute-start(bf16[4,128,512]{2,1,0:T(8,128)(2,1)S(1)} %slice.32), channel_id=1, source_target_pairs={{0,2},{2,4},{4,6},{6,0},{1,3},{3,5},{5,7},{7,1},{8,10},{10,12},{12... | collective-permute-start | bytes 1572872 | tf_op jit(solution)/shard_map/ppermute | solution.py:108
  69.1 11.8 %collective-permute-start.14 = (bf16[1024,256]{1,0:T(8,128)(2,1)S(1)}, bf16[1024,256]{1,0:T(8,128)(2,1)S(1)}, u32[]{:S(2)}, u32[]{:S(2)}) collective-permute-start(bf16[1024,256]{1,0:T(8,128)(2,1)S(1)} %slice.34), channel_id=1, source_target_pairs={{0,64},{64,128},{128,192},{192,0},{1,65},{65,129},{129,193},{193,1... | collective-permute-start | bytes 1572872 | tf_op jit(solution)/shard_map/ppermute | solution.py:132
  71.2 10.5 %collective-permute-start.15 = (bf16[1024,256]{1,0:T(8,128)(2,1)S(1)}, bf16[1024,256]{1,0:T(8,128)(2,1)S(1)}, u32[]{:S(2)}, u32[]{:S(2)}) collective-permute-start(bf16[1024,256]{1,0:T(8,128)(2,1)S(1)} %slice.35), channel_id=1, source_target_pairs={{0,192},{64,0},{128,64},{192,128},{1,193},{65,1},{129,65},{193,129... | collective-permute-start | bytes 1572872 | tf_op jit(solution)/shard_map/ppermute | solution.py:133
  73.9 19.2 %collective-permute-start.26 = (bf16[2,128,512]{2,1,0:T(8,128)(2,1)S(1)}, bf16[2,128,512]{2,1,0:T(8,128)(2,1)S(1)}, u32[]{:S(2)}, u32[]{:S(2)}) collective-permute-start(bf16[2,128,512]{2,1,0:T(8,128)(2,1)S(1)} %slice.37), channel_id=1, source_target_pairs={{0,56},{8,0},{16,8},{24,16},{32,24},{40,32},{48,40},{56,48},{1,57}... | collective-permute-start | bytes 786440 | tf_op jit(solution)/shard_map/ppermute | solution.py:109
  75.2 18.0 %collective-permute-start.25 = (bf16[2,128,512]{2,1,0:T(8,128)(2,1)S(1)}, bf16[2,128,512]{2,1,0:T(8,128)(2,1)S(1)}, u32[]{:S(2)}, u32[]{:S(2)}) collective-permute-start(bf16[2,128,512]{2,1,0:T(8,128)(2,1)S(1)} %slice.36), channel_id=1, source_target_pairs={{0,8},{8,16},{16,24},{24,32},{32,40},{40,48},{48,56},{56,0},{1,9},... | collective-permute-start | bytes 786440 | tf_op jit(solution)/shard_map/ppermute | solution.py:108
  80.9 19.3 %copy-start.5 = (s32[1,1,4]{2,1,0:T(1,128)S(1)}, s32[1,1,4]{2,1,0:T(1,128)}, u32[]{:S(2)}) copy-start(s32[1,1,4]{2,1,0:T(1,128)} %param.7) | copy-start | bytes 52
  80.9 19.3 %copy-start.6 = (s32[1,1,4]{2,1,0:T(1,128)S(1)}, s32[1,1,4]{2,1,0:T(1,128)}, u32[]{:S(2)}) copy-start(s32[1,1,4]{2,1,0:T(1,128)} %param.8) | copy-start | bytes 52
  82.5 23.7 %collective-permute-start.27 = (bf16[32,128,512]{2,1,0:T(8,128)(2,1)}, bf16[32,128,512]{2,1,0:T(8,128)(2,1)}, u32[]{:S(2)}, u32[]{:S(2)}) collective-permute-start(bf16[32,128,512]{2,1,0:T(8,128)(2,1)} %bitcast.22.rest_0_), channel_id=1, source_target_pairs={{0,1},{1,0},{2,3},{3,2},{4,5},{5,4},{6,7},{7,6},{8,9},{9,8},{10,11... | collective-permute-start | bytes 12582920 | tf_op jit(solution)/shard_map/ppermute | solution.py:180
  96.5 10.0 %collective-permute-start.28 = (bf16[32,128,512]{2,1,0:T(8,128)(2,1)}, bf16[32,128,512]{2,1,0:T(8,128)(2,1)}, u32[]{:S(2)}, u32[]{:S(2)}) collective-permute-start(bf16[32,128,512]{2,1,0:T(8,128)(2,1)} %bitcast.35.rest_1_), channel_id=1, source_target_pairs={{0,1},{1,0},{2,3},{3,2},{4,5},{5,4},{6,7},{7,6},{8,9},{9,8},{10,11... | collective-permute-start | bytes 12582920 | tf_op jit(solution)/shard_map/ppermute | solution.py:181
  (4 other events, 3.7 us)

commit v8 on v6

--- a/solution.py
+++ b/solution.py
@@ -193,7 +193,7 @@
     lead_all = lead_all.reshape(nz * ny, tok, width)
     trail_all = trail_all.reshape(nz * ny, tok, width)
 
-    lead_all, trail_all, grad_pieces = lax.optimization_barrier((lead_all, trail_all, grad_pieces))
+    lead_all, grad_pieces = lax.optimization_barrier((lead_all, grad_pieces))
     grad_pieces = [g.reshape(g.shape[0] // (2 * tok), 2, tok, g.shape[1]) for g in grad_pieces]
     starts = starts // (2 * tok)
     lead_other = lax.ppermute(lead_all, "core", swap)

time: 121 us -> 115 us (0.950)
  the two profiles are of different devices: /device:TPU:3 before, /device:TPU:1 now
where the time goes in v8:
time: 115 us
  starting transfers between devices  46 us (40%)
  waiting for transfers between devices  44.6 us (39%)
  local copies, waits for them, and re-layouts  10.6 us (9%)
  Pallas kernels  7.7 us (7%)
  other arithmetic  5.52 us (5%)
    ppermute x8, starting transfers between devices, relative_gather(): from_right = lax.ppermute(from_right, axis, left)  20.9 us
    ppermute x8, waiting for transfers between devices, relative_gather(): from_right = lax.ppermute(from_right, axis, left)  18.6 us
    ppermute x1, starting transfers between devices, on_device(): lead_other = lax.ppermute(lead_all, 'core', swap)  7.96 us
    ppermute x1, waiting for transfers between devices, on_device(): from_right = lax.ppermute(out_grad, 'in', left)  7.81 us
    pallas_call x2, Pallas kernels, block_products(): pl.pallas_call(functools.partial(block_kernel, n_grad, ny), out_shape=jax...  7.7 us
    unnamed x22, local copies, waits for them, and re-layouts  7.28 us
    ppermute x2, starting transfers between devices, relative_gather(): near_b = lax.ppermute(from_right[half:], axis, left)  6.18 us
    ppermute x2, waiting for transfers between devices, relative_gather(): rel[n // 2] = lax.ppermute(from_left, axis, right)  5.31 us
  transfers between devices with their start and end apart: 28, of which 11 were waited for; matrix products, arithmetic and copies ran while one was open for 10% of the time, Pallas kernels for 1%

profile of v8, /device:TPU:1, one launch (start us, length us, event | category | flops | bytes accessed | tf_op | source)
XLA Modules:
  0.0 115.4 jit_solution(9702822293286725800)
XLA Ops:
  1.0 3.3 %collective-permute-start = (bf16[128,512]{1,0:T(8,128)(2,1)S(1)}, bf16[128,512]{1,0:T(8,128)(2,1)S(1)}, u32[]{:S(2)}, u32[]{:S(2)}) collective-permute-start(bf16[128,512]{1,0:T(8,128)(2,1)S(1)} %broadcast_select_fusion.2), channel_id=1, source_target_pairs={{0,1},{1,0},{2,3},{3,2},{4,5},{5,4},{6,7},{7,6},{8,9},{9,8},{10,11... | collective-permute-start | bytes 393224 | tf_op jit(solution)/shard_map/ppermute | solution.py:165
  5.3 1.0 bitcast_dynamic-update-slice_fusion.14
  6.3 3.9 %collective-permute-start.1 = (bf16[128,512]{1,0:T(8,128)(2,1)S(1)}, bf16[128,512]{1,0:T(8,128)(2,1)S(1)}, u32[]{:S(2)}, u32[]{:S(2)}) collective-permute-start(bf16[128,512]{1,0:T(8,128)(2,1)S(1)} %get-tuple-element.27), channel_id=1, source_target_pairs={{0,56},{8,0},{16,8},{24,16},{32,24},{40,32},{48,40},{56,48},{1,57}... | collective-permute-start | bytes 393224 | tf_op jit(solution)/shard_map/ppermute | solution.py:100
  10.2 1.0 broadcast_select_fusion
  11.2 1.4 %collective-permute-start.9 = (bf16[128,512]{1,0:T(8,128)(2,1)S(1)}, bf16[128,512]{1,0:T(8,128)(2,1)S(1)}, u32[]{:S(2)}, u32[]{:S(2)}) collective-permute-start(bf16[128,512]{1,0:T(8,128)(2,1)S(1)} %broadcast_select_fusion), channel_id=1, source_target_pairs={{0,2},{2,4},{4,6},{6,0},{1,3},{3,5},{5,7},{7,1},{8,10},{10,12},{12... | collective-permute-start | bytes 393224 | tf_op jit(solution)/shard_map/ppermute | solution.py:99
  12.6 1.2 %collective-permute-start.11 = (bf16[2048,256]{1,0:T(8,128)(2,1)}, bf16[2048,256]{1,0:T(8,128)(2,1)S(1)}, u32[]{:S(2)}, u32[]{:S(2)}) collective-permute-start(bf16[2048,256]{1,0:T(8,128)(2,1)} %param.6), channel_id=1, source_target_pairs={{0,64},{64,128},{128,192},{192,0},{1,65},{65,129},{129,193},{193,1... | collective-permute-start | bytes 3145736 | tf_op jit(solution)/shard_map/ppermute | solution.py:175
  13.8 1.5 %collective-permute-start.8 = (bf16[128,512]{1,0:T(8,128)(2,1)S(1)}, bf16[128,512]{1,0:T(8,128)(2,1)S(1)}, u32[]{:S(2)}, u32[]{:S(2)}) collective-permute-start(bf16[128,512]{1,0:T(8,128)(2,1)S(1)} %broadcast_select_fusion), channel_id=1, source_target_pairs={{0,6},{2,0},{4,2},{6,4},{1,7},{3,1},{5,3},{7,5},{8,14},{10,8},{12,... | collective-permute-start | bytes 393224 | tf_op jit(solution)/shard_map/ppermute | solution.py:100
  15.3 2.7 %collective-permute-start.2 = (bf16[128,512]{1,0:T(8,128)(2,1)S(1)}, bf16[128,512]{1,0:T(8,128)(2,1)S(1)}, u32[]{:S(2)}, u32[]{:S(2)}) collective-permute-start(bf16[128,512]{1,0:T(8,128)(2,1)S(1)} %collective-permute-done.1), channel_id=1, source_target_pairs={{0,56},{8,0},{16,8},{24,16},{32,24},{40,32},{48,40},{56,48},{1,57}... | collective-permute-start | bytes 393224 | tf_op jit(solution)/shard_map/ppermute | solution.py:100
  18.1 1.8 %collective-permute-done.2 = bf16[128,512]{1,0:T(8,128)(2,1)S(1)} collective-permute-done((bf16[128,512]{1,0:T(8,128)(2,1)S(1)}, bf16[128,512]{1,0:T(8,128)(2,1)S(1)}, u32[]{:S(2)}, u32[]{:S(2)}) %collective-permute-start.2) | collective-permute-done | bytes 131104 | tf_op jit(solution)/shard_map/ppermute | solution.py:100
  20.0 3.4 %collective-permute-start.3 = (bf16[128,512]{1,0:T(8,128)(2,1)S(1)}, bf16[128,512]{1,0:T(8,128)(2,1)S(1)}, u32[]{:S(2)}, u32[]{:S(2)}) collective-permute-start(bf16[128,512]{1,0:T(8,128)(2,1)S(1)} %collective-permute-done.2), channel_id=1, source_target_pairs={{0,56},{8,0},{16,8},{24,16},{32,24},{40,32},{48,40},{56,48},{1,57}... | collective-permute-start | bytes 393224 | tf_op jit(solution)/shard_map/ppermute | solution.py:100
  23.4 1.2 %collective-permute-start.12 = (bf16[2048,256]{1,0:T(8,128)(2,1)}, bf16[2048,256]{1,0:T(8,128)(2,1)S(1)}, u32[]{:S(2)}, u32[]{:S(2)}) collective-permute-start(bf16[2048,256]{1,0:T(8,128)(2,1)} %param.6), channel_id=1, source_target_pairs={{0,192},{64,0},{128,64},{192,128},{1,193},{65,1},{129,65},{193,129... | collective-permute-start | bytes 3145736 | tf_op jit(solution)/shard_map/ppermute | solution.py:176
  24.7 4.0 %collective-permute-done.6 = bf16[128,512]{1,0:T(8,128)(2,1)S(1)} collective-permute-done((bf16[128,512]{1,0:T(8,128)(2,1)S(1)}, bf16[128,512]{1,0:T(8,128)(2,1)S(1)}, u32[]{:S(2)}, u32[]{:S(2)}) %collective-permute-start.6) | collective-permute-done | bytes 131104 | tf_op jit(solution)/shard_map/ppermute | solution.py:99
  28.7 5.3 %collective-permute-done.7 = bf16[128,512]{1,0:T(8,128)(2,1)S(1)} collective-permute-done((bf16[128,512]{1,0:T(8,128)(2,1)S(1)}, bf16[128,512]{1,0:T(8,128)(2,1)S(1)}, u32[]{:S(2)}, u32[]{:S(2)}) %collective-permute-start.7) | collective-permute-done | bytes 131104 | tf_op jit(solution)/shard_map/ppermute | solution.py:104
  34.1 3.8 %collective-permute-done.11 = bf16[2048,256]{1,0:T(8,128)(2,1)S(1)} collective-permute-done((bf16[2048,256]{1,0:T(8,128)(2,1)}, bf16[2048,256]{1,0:T(8,128)(2,1)S(1)}, u32[]{:S(2)}, u32[]{:S(2)}) %collective-permute-start.11) | collective-permute-done | bytes 1048608 | tf_op jit(solution)/shard_map/ppermute | solution.py:175
  37.8 7.8 %collective-permute-done.12 = bf16[2048,256]{1,0:T(8,128)(2,1)S(1)} collective-permute-done((bf16[2048,256]{1,0:T(8,128)(2,1)}, bf16[2048,256]{1,0:T(8,128)(2,1)S(1)}, u32[]{:S(2)}, u32[]{:S(2)}) %collective-permute-start.12) | collective-permute-done | bytes 1048608 | tf_op jit(solution)/shard_map/ppermute | solution.py:176
  45.6 1.4 %collective-permute-start.13 = (bf16[8,128,512]{2,1,0:T(8,128)(2,1)S(1)}, bf16[8,128,512]{2,1,0:T(8,128)(2,1)S(1)}, u32[]{:S(2)}, u32[]{:S(2)}) collective-permute-start(bf16[8,128,512]{2,1,0:T(8,128)(2,1)S(1)} %bitcast_dynamic-update-slice_fusion.7), channel_id=1, source_target_pairs={{0,6},{2,0},{4,2},{6,4},{1,7},{3,1},{5,3},{7,5},{8,14},{10,8},{12,... | collective-permute-start | bytes 3145736 | tf_op jit(solution)/shard_map/ppermute | solution.py:100
  47.1 2.4 %collective-permute-start.18 = (bf16[4,128,512]{2,1,0:T(8,128)(2,1)S(1)}, bf16[4,128,512]{2,1,0:T(8,128)(2,1)S(1)}, u32[]{:S(2)}, u32[]{:S(2)}) collective-permute-start(bf16[4,128,512]{2,1,0:T(8,128)(2,1)S(1)} %pad_maximum_fusion.1), channel_id=1, source_target_pairs={{0,56},{8,0},{16,8},{24,16},{32,24},{40,32},{48,40},{56,48},{1,57}... | collective-permute-start | bytes 1572872 | tf_op jit(solution)/shard_map/ppermute | solution.py:100
  49.5 6.9 %collective-permute-done.18 = bf16[4,128,512]{2,1,0:T(8,128)(2,1)S(1)} collective-permute-done((bf16[4,128,512]{2,1,0:T(8,128)(2,1)S(1)}, bf16[4,128,512]{2,1,0:T(8,128)(2,1)S(1)}, u32[]{:S(2)}, u32[]{:S(2)}) %collective-permute-start.18) | collective-permute-done | bytes 524320 | tf_op jit(solution)/shard_map/ppermute | solution.py:100
  56.4 3.3 %collective-permute-start.19 = (bf16[4,128,512]{2,1,0:T(8,128)(2,1)S(1)}, bf16[4,128,512]{2,1,0:T(8,128)(2,1)S(1)}, u32[]{:S(2)}, u32[]{:S(2)}) collective-permute-start(bf16[4,128,512]{2,1,0:T(8,128)(2,1)S(1)} %collective-permute-done.18), channel_id=1, source_target_pairs={{0,56},{8,0},{16,8},{24,16},{32,24},{40,32},{48,40},{56,48},{1,57}... | collective-permute-start | bytes 1572872 | tf_op jit(solution)/shard_map/ppermute | solution.py:100
  59.7 1.0 collective-permute-start.17
  60.8 6.0 %collective-permute-done.13 = bf16[8,128,512]{2,1,0:T(8,128)(2,1)S(1)} collective-permute-done((bf16[8,128,512]{2,1,0:T(8,128)(2,1)S(1)}, bf16[8,128,512]{2,1,0:T(8,128)(2,1)S(1)}, u32[]{:S(2)}, u32[]{:S(2)}) %collective-permute-start.13) | collective-permute-done | bytes 1048608 | tf_op jit(solution)/shard_map/ppermute | solution.py:100
  66.8 2.8 %collective-permute-start.16 = (bf16[4,128,512]{2,1,0:T(8,128)(2,1)S(1)}, bf16[4,128,512]{2,1,0:T(8,128)(2,1)S(1)}, u32[]{:S(2)}, u32[]{:S(2)}) collective-permute-start(bf16[4,128,512]{2,1,0:T(8,128)(2,1)S(1)} %slice.25), channel_id=1, source_target_pairs={{0,6},{2,0},{4,2},{6,4},{1,7},{3,1},{5,3},{7,5},{8,14},{10,8},{12,... | collective-permute-start | bytes 1572872 | tf_op jit(solution)/shard_map/ppermute | solution.py:109
  69.7 2.2 %collective-permute-start.20 = (bf16[4,128,512]{2,1,0:T(8,128)(2,1)S(1)}, bf16[4,128,512]{2,1,0:T(8,128)(2,1)S(1)}, u32[]{:S(2)}, u32[]{:S(2)}) collective-permute-start(bf16[4,128,512]{2,1,0:T(8,128)(2,1)S(1)} %collective-permute-done.19), channel_id=1, source_target_pairs={{0,56},{8,0},{16,8},{24,16},{32,24},{40,32},{48,40},{56,48},{1,57}... | collective-permute-start | bytes 1572872 | tf_op jit(solution)/shard_map/ppermute | solution.py:100
  74.4 3.9 %collective-permute-done.20 = bf16[4,128,512]{2,1,0:T(8,128)(2,1)S(1)} collective-permute-done((bf16[4,128,512]{2,1,0:T(8,128)(2,1)S(1)}, bf16[4,128,512]{2,1,0:T(8,128)(2,1)S(1)}, u32[]{:S(2)}, u32[]{:S(2)}) %collective-permute-start.20) | collective-permute-done | bytes 524320 | tf_op jit(solution)/shard_map/ppermute | solution.py:100
  78.3 3.4 %collective-permute-start.25 = (bf16[2,128,512]{2,1,0:T(8,128)(2,1)S(1)}, bf16[2,128,512]{2,1,0:T(8,128)(2,1)S(1)}, u32[]{:S(2)}, u32[]{:S(2)}) collective-permute-start(bf16[2,128,512]{2,1,0:T(8,128)(2,1)S(1)} %slice.27), channel_id=1, source_target_pairs={{0,56},{8,0},{16,8},{24,16},{32,24},{40,32},{48,40},{56,48},{1,57}... | collective-permute-start | bytes 786440 | tf_op jit(solution)/shard_map/ppermute | solution.py:109
  82.7 2.4 %copy.6 = bf16[8,4,128,512]{3,2,1,0:T(8,128)(2,1)} copy(bf16[8,4,128,512]{3,2,0,1:T(8,128)(2,1)S(1)} %pad_maximum_fusion) | data formatting | bytes 8388608 | tf_op jit(solution)/shard_map/stack | solution.py:191
  86.2 8.0 %collective-permute-start.26 = (bf16[32,128,512]{2,1,0:T(8,128)(2,1)}, bf16[32,128,512]{2,1,0:T(8,128)(2,1)}, u32[]{:S(2)}, u32[]{:S(2)}) collective-permute-start(bf16[32,128,512]{2,1,0:T(8,128)(2,1)} %bitcast.25.rest_0_), channel_id=1, source_target_pairs={{0,1},{1,0},{2,3},{3,2},{4,5},{5,4},{6,7},{7,6},{8,9},{9,8},{10,11... | collective-permute-start | bytes 12582920 | tf_op jit(solution)/shard_map/ppermute | solution.py:199
  98.3 2.6 %collective-permute-start.27 = (bf16[32,128,512]{2,1,0:T(8,128)(2,1)}, bf16[32,128,512]{2,1,0:T(8,128)(2,1)}, u32[]{:S(2)}, u32[]{:S(2)}) collective-permute-start(bf16[32,128,512]{2,1,0:T(8,128)(2,1)} %bitcast.34.rest_1_), channel_id=1, source_target_pairs={{0,1},{1,0},{2,3},{3,2},{4,5},{5,4},{6,7},{7,6},{8,9},{9,8},{10,11... | collective-permute-start | bytes 12582920 | tf_op jit(solution)/shard_map/ppermute | solution.py:200
  101.8 1.2 %copy-done.2 = bf16[2048,256]{1,0:T(8,128)(2,1)S(1)} copy-done((bf16[2048,256]{1,0:T(8,128)(2,1)S(1)}, bf16[2048,256]{1,0:T(8,128)(2,1)}, u32[]{:S(2)}) %copy-start.2) | copy-done | bytes 1048600
  103.0 1.1 shard_map.55
  104.2 3.9 %collective-permute-done.27.rest_1_ = bf16[32,128,512]{2,1,0:T(8,128)(2,1)} collective-permute-done((bf16[32,128,512]{2,1,0:T(8,128)(2,1)}, bf16[32,128,512]{2,1,0:T(8,128)(2,1)}, u32[]{:S(2)}, u32[]{:S(2)}) %collective-permute-start.27) | collective-permute-done | bytes 4194336 | tf_op jit(solution)/shard_map/ppermute | solution.py:200
  108.1 6.6 %shard_map.56 = f32[4,128,128]{2,1,0:T(8,128)S(1)} custom-call(s32[4]{0:T(128)S(1)} %get-tuple-element.29.rows_ref, s32[4]{0:T(128)S(1)} %clamp_bitcast_fusion.cols_ref, s32[4]{0:T(128)S(1)} %get-tuple-element.23.use_ref, s32[4]{0:T(128)S(1)} %get-tuple-element.28.starts_ref, s32[2]{0:T(128)S(1)} %pad_add_fusion.1.place_ref, ...), custom_call_target="tpu_custom_call" | custom-call | flops 1073741824 | bytes 17039360 | tf_op jit(solution)/shard_map/pallas_call | solution.py:78
  (68 shorter events, 12.0 us)
Async XLA Ops:
  1.0 4.3 %collective-permute-start = (bf16[128,512]{1,0:T(8,128)(2,1)S(1)}, bf16[128,512]{1,0:T(8,128)(2,1)S(1)}, u32[]{:S(2)}, u32[]{:S(2)}) collective-permute-start(bf16[128,512]{1,0:T(8,128)(2,1)S(1)} %broadcast_select_fusion.2), channel_id=1, source_target_pairs={{0,1},{1,0},{2,3},{3,2},{4,5},{5,4},{6,7},{7,6},{8,9},{9,8},{10,11... | collective-permute-start | bytes 393224 | tf_op jit(solution)/shard_map/ppermute | solution.py:165
  6.3 9.1 %collective-permute-start.1 = (bf16[128,512]{1,0:T(8,128)(2,1)S(1)}, bf16[128,512]{1,0:T(8,128)(2,1)S(1)}, u32[]{:S(2)}, u32[]{:S(2)}) collective-permute-start(bf16[128,512]{1,0:T(8,128)(2,1)S(1)} %get-tuple-element.27), channel_id=1, source_target_pairs={{0,56},{8,0},{16,8},{24,16},{32,24},{40,32},{48,40},{56,48},{1,57}... | collective-permute-start | bytes 393224 | tf_op jit(solution)/shard_map/ppermute | solution.py:100
  10.2 7.8 %collective-permute-start.4 = (bf16[128,512]{1,0:T(8,128)(2,1)S(1)}, bf16[128,512]{1,0:T(8,128)(2,1)S(1)}, u32[]{:S(2)}, u32[]{:S(2)}) collective-permute-start(bf16[128,512]{1,0:T(8,128)(2,1)S(1)} %get-tuple-element.27), channel_id=1, source_target_pairs={{0,8},{8,16},{16,24},{24,32},{32,40},{40,48},{48,56},{56,0},{1,9},... | collective-permute-start | bytes 393224 | tf_op jit(solution)/shard_map/ppermute | solution.py:99
  11.2 6.8 %collective-permute-start.9 = (bf16[128,512]{1,0:T(8,128)(2,1)S(1)}, bf16[128,512]{1,0:T(8,128)(2,1)S(1)}, u32[]{:S(2)}, u32[]{:S(2)}) collective-permute-start(bf16[128,512]{1,0:T(8,128)(2,1)S(1)} %broadcast_select_fusion), channel_id=1, source_target_pairs={{0,2},{2,4},{4,6},{6,0},{1,3},{3,5},{5,7},{7,1},{8,10},{10,12},{12... | collective-permute-start | bytes 393224 | tf_op jit(solution)/shard_map/ppermute | solution.py:99
  12.6 25.2 %collective-permute-start.11 = (bf16[2048,256]{1,0:T(8,128)(2,1)}, bf16[2048,256]{1,0:T(8,128)(2,1)S(1)}, u32[]{:S(2)}, u32[]{:S(2)}) collective-permute-start(bf16[2048,256]{1,0:T(8,128)(2,1)} %param.6), channel_id=1, source_target_pairs={{0,64},{64,128},{128,192},{192,0},{1,65},{65,129},{129,193},{193,1... | collective-permute-start | bytes 3145736 | tf_op jit(solution)/shard_map/ppermute | solution.py:175
  13.8 9.6 %collective-permute-start.8 = (bf16[128,512]{1,0:T(8,128)(2,1)S(1)}, bf16[128,512]{1,0:T(8,128)(2,1)S(1)}, u32[]{:S(2)}, u32[]{:S(2)}) collective-permute-start(bf16[128,512]{1,0:T(8,128)(2,1)S(1)} %broadcast_select_fusion), channel_id=1, source_target_pairs={{0,6},{2,0},{4,2},{6,4},{1,7},{3,1},{5,3},{7,5},{8,14},{10,8},{12,... | collective-permute-start | bytes 393224 | tf_op jit(solution)/shard_map/ppermute | solution.py:100
  15.3 4.6 %collective-permute-start.2 = (bf16[128,512]{1,0:T(8,128)(2,1)S(1)}, bf16[128,512]{1,0:T(8,128)(2,1)S(1)}, u32[]{:S(2)}, u32[]{:S(2)}) collective-permute-start(bf16[128,512]{1,0:T(8,128)(2,1)S(1)} %collective-permute-done.1), channel_id=1, source_target_pairs={{0,56},{8,0},{16,8},{24,16},{32,24},{40,32},{48,40},{56,48},{1,57}... | collective-permute-start | bytes 393224 | tf_op jit(solution)/shard_map/ppermute | solution.py:100
  18.0 5.3 %collective-permute-start.5 = (bf16[128,512]{1,0:T(8,128)(2,1)S(1)}, bf16[128,512]{1,0:T(8,128)(2,1)S(1)}, u32[]{:S(2)}, u32[]{:S(2)}) collective-permute-start(bf16[128,512]{1,0:T(8,128)(2,1)S(1)} %collective-permute-done.4), channel_id=1, source_target_pairs={{0,8},{8,16},{16,24},{24,32},{32,40},{40,48},{48,56},{56,0},{1,9},... | collective-permute-start | bytes 393224 | tf_op jit(solution)/shard_map/ppermute | solution.py:99
  18.0 6.6 %collective-permute-start.10 = (bf16[128,512]{1,0:T(8,128)(2,1)S(1)}, bf16[128,512]{1,0:T(8,128)(2,1)S(1)}, u32[]{:S(2)}, u32[]{:S(2)}) collective-permute-start(bf16[128,512]{1,0:T(8,128)(2,1)S(1)} %collective-permute-done.9), channel_id=1, source_target_pairs={{0,2},{2,4},{4,6},{6,0},{1,3},{3,5},{5,7},{7,1},{8,10},{10,12},{12... | collective-permute-start | bytes 393224 | tf_op jit(solution)/shard_map/ppermute | solution.py:104
  20.0 8.7 %collective-permute-start.3 = (bf16[128,512]{1,0:T(8,128)(2,1)S(1)}, bf16[128,512]{1,0:T(8,128)(2,1)S(1)}, u32[]{:S(2)}, u32[]{:S(2)}) collective-permute-start(bf16[128,512]{1,0:T(8,128)(2,1)S(1)} %collective-permute-done.2), channel_id=1, source_target_pairs={{0,56},{8,0},{16,8},{24,16},{32,24},{40,32},{48,40},{56,48},{1,57}... | collective-permute-start | bytes 393224 | tf_op jit(solution)/shard_map/ppermute | solution.py:100
  23.3 5.3 %collective-permute-start.6 = (bf16[128,512]{1,0:T(8,128)(2,1)S(1)}, bf16[128,512]{1,0:T(8,128)(2,1)S(1)}, u32[]{:S(2)}, u32[]{:S(2)}) collective-permute-start(bf16[128,512]{1,0:T(8,128)(2,1)S(1)} %collective-permute-done.5), channel_id=1, source_target_pairs={{0,8},{8,16},{16,24},{24,32},{32,40},{40,48},{48,56},{56,0},{1,9},... | collective-permute-start | bytes 393224 | tf_op jit(solution)/shard_map/ppermute | solution.py:99
  23.4 22.3 %collective-permute-start.12 = (bf16[2048,256]{1,0:T(8,128)(2,1)}, bf16[2048,256]{1,0:T(8,128)(2,1)S(1)}, u32[]{:S(2)}, u32[]{:S(2)}) collective-permute-start(bf16[2048,256]{1,0:T(8,128)(2,1)} %param.6), channel_id=1, source_target_pairs={{0,192},{64,0},{128,64},{192,128},{1,193},{65,1},{129,65},{193,129... | collective-permute-start | bytes 3145736 | tf_op jit(solution)/shard_map/ppermute | solution.py:176
  28.7 5.3 %collective-permute-start.7 = (bf16[128,512]{1,0:T(8,128)(2,1)S(1)}, bf16[128,512]{1,0:T(8,128)(2,1)S(1)}, u32[]{:S(2)}, u32[]{:S(2)}) collective-permute-start(bf16[128,512]{1,0:T(8,128)(2,1)S(1)} %collective-permute-done.6), channel_id=1, source_target_pairs={{0,8},{8,16},{16,24},{24,32},{32,40},{40,48},{48,56},{56,0},{1,9},... | collective-permute-start | bytes 393224 | tf_op jit(solution)/shard_map/ppermute | solution.py:104
  45.6 21.1 %collective-permute-start.13 = (bf16[8,128,512]{2,1,0:T(8,128)(2,1)S(1)}, bf16[8,128,512]{2,1,0:T(8,128)(2,1)S(1)}, u32[]{:S(2)}, u32[]{:S(2)}) collective-permute-start(bf16[8,128,512]{2,1,0:T(8,128)(2,1)S(1)} %bitcast_dynamic-update-slice_fusion.7), channel_id=1, source_target_pairs={{0,6},{2,0},{4,2},{6,4},{1,7},{3,1},{5,3},{7,5},{8,14},{10,8},{12,... | collective-permute-start | bytes 3145736 | tf_op jit(solution)/shard_map/ppermute | solution.py:100
  47.1 22.5 %collective-permute-start.14 = (bf16[8,128,512]{2,1,0:T(8,128)(2,1)S(1)}, bf16[8,128,512]{2,1,0:T(8,128)(2,1)S(1)}, u32[]{:S(2)}, u32[]{:S(2)}) collective-permute-start(bf16[8,128,512]{2,1,0:T(8,128)(2,1)S(1)} %bitcast_dynamic-update-slice_fusion.7), channel_id=1, source_target_pairs={{0,2},{2,4},{4,6},{6,0},{1,3},{3,5},{5,7},{7,1},{8,10},{10,12},{12... | collective-permute-start | bytes 3145736 | tf_op jit(solution)/shard_map/ppermute | solution.py:99
  47.1 9.3 %collective-permute-start.18 = (bf16[4,128,512]{2,1,0:T(8,128)(2,1)S(1)}, bf16[4,128,512]{2,1,0:T(8,128)(2,1)S(1)}, u32[]{:S(2)}, u32[]{:S(2)}) collective-permute-start(bf16[4,128,512]{2,1,0:T(8,128)(2,1)S(1)} %pad_maximum_fusion.1), channel_id=1, source_target_pairs={{0,56},{8,0},{16,8},{24,16},{32,24},{40,32},{48,40},{56,48},{1,57}... | collective-permute-start | bytes 1572872 | tf_op jit(solution)/shard_map/ppermute | solution.py:100
  49.5 10.2 %collective-permute-start.21 = (bf16[4,128,512]{2,1,0:T(8,128)(2,1)S(1)}, bf16[4,128,512]{2,1,0:T(8,128)(2,1)S(1)}, u32[]{:S(2)}, u32[]{:S(2)}) collective-permute-start(bf16[4,128,512]{2,1,0:T(8,128)(2,1)S(1)} %pad_maximum_fusion.1), channel_id=1, source_target_pairs={{0,8},{8,16},{16,24},{24,32},{32,40},{40,48},{48,56},{56,0},{1,9},... | collective-permute-start | bytes 1572872 | tf_op jit(solution)/shard_map/ppermute | solution.py:99
  56.4 13.3 %collective-permute-start.19 = (bf16[4,128,512]{2,1,0:T(8,128)(2,1)S(1)}, bf16[4,128,512]{2,1,0:T(8,128)(2,1)S(1)}, u32[]{:S(2)}, u32[]{:S(2)}) collective-permute-start(bf16[4,128,512]{2,1,0:T(8,128)(2,1)S(1)} %collective-permute-done.18), channel_id=1, source_target_pairs={{0,56},{8,0},{16,8},{24,16},{32,24},{40,32},{48,40},{56,48},{1,57}... | collective-permute-start | bytes 1572872 | tf_op jit(solution)/shard_map/ppermute | solution.py:100
  59.7 12.1 %collective-permute-start.22 = (bf16[4,128,512]{2,1,0:T(8,128)(2,1)S(1)}, bf16[4,128,512]{2,1,0:T(8,128)(2,1)S(1)}, u32[]{:S(2)}, u32[]{:S(2)}) collective-permute-start(bf16[4,128,512]{2,1,0:T(8,128)(2,1)S(1)} %collective-permute-done.21), channel_id=1, source_target_pairs={{0,8},{8,16},{16,24},{24,32},{32,40},{40,48},{48,56},{56,0},{1,9},... | collective-permute-start | bytes 1572872 | tf_op jit(solution)/shard_map/ppermute | solution.py:99
  59.7 25.4 %collective-permute-start.17 = (bf16[2048,256]{1,0:T(8,128)(2,1)S(1)}, bf16[2048,256]{1,0:T(8,128)(2,1)S(1)}, u32[]{:S(2)}, u32[]{:S(2)}) collective-permute-start(bf16[2048,256]{1,0:T(8,128)(2,1)S(1)} %collective-permute-done.11), channel_id=1, source_target_pairs={{0,64},{64,128},{128,192},{192,0},{1,65},{65,129},{129,193},{193,1... | collective-permute-start | bytes 3145736 | tf_op jit(solution)/shard_map/ppermute | solution.py:183
  66.8 15.3 %collective-permute-start.16 = (bf16[4,128,512]{2,1,0:T(8,128)(2,1)S(1)}, bf16[4,128,512]{2,1,0:T(8,128)(2,1)S(1)}, u32[]{:S(2)}, u32[]{:S(2)}) collective-permute-start(bf16[4,128,512]{2,1,0:T(8,128)(2,1)S(1)} %slice.25), channel_id=1, source_target_pairs={{0,6},{2,0},{4,2},{6,4},{1,7},{3,1},{5,3},{7,5},{8,14},{10,8},{12,... | collective-permute-start | bytes 1572872 | tf_op jit(solution)/shard_map/ppermute | solution.py:109
  69.6 12.5 %collective-permute-start.15 = (bf16[4,128,512]{2,1,0:T(8,128)(2,1)S(1)}, bf16[4,128,512]{2,1,0:T(8,128)(2,1)S(1)}, u32[]{:S(2)}, u32[]{:S(2)}) collective-permute-start(bf16[4,128,512]{2,1,0:T(8,128)(2,1)S(1)} %slice.24), channel_id=1, source_target_pairs={{0,2},{2,4},{4,6},{6,0},{1,3},{3,5},{5,7},{7,1},{8,10},{10,12},{12... | collective-permute-start | bytes 1572872 | tf_op jit(solution)/shard_map/ppermute | solution.py:108
  69.7 8.6 %collective-permute-start.20 = (bf16[4,128,512]{2,1,0:T(8,128)(2,1)S(1)}, bf16[4,128,512]{2,1,0:T(8,128)(2,1)S(1)}, u32[]{:S(2)}, u32[]{:S(2)}) collective-permute-start(bf16[4,128,512]{2,1,0:T(8,128)(2,1)S(1)} %collective-permute-done.19), channel_id=1, source_target_pairs={{0,56},{8,0},{16,8},{24,16},{32,24},{40,32},{48,40},{56,48},{1,57}... | collective-permute-start | bytes 1572872 | tf_op jit(solution)/shard_map/ppermute | solution.py:100
  71.9 10.0 %collective-permute-start.23 = (bf16[4,128,512]{2,1,0:T(8,128)(2,1)S(1)}, bf16[4,128,512]{2,1,0:T(8,128)(2,1)S(1)}, u32[]{:S(2)}, u32[]{:S(2)}) collective-permute-start(bf16[4,128,512]{2,1,0:T(8,128)(2,1)S(1)} %collective-permute-done.22), channel_id=1, source_target_pairs={{0,8},{8,16},{16,24},{24,32},{32,40},{40,48},{48,56},{56,0},{1,9},... | collective-permute-start | bytes 1572872 | tf_op jit(solution)/shard_map/ppermute | solution.py:99
  78.3 16.6 %collective-permute-start.25 = (bf16[2,128,512]{2,1,0:T(8,128)(2,1)S(1)}, bf16[2,128,512]{2,1,0:T(8,128)(2,1)S(1)}, u32[]{:S(2)}, u32[]{:S(2)}) collective-permute-start(bf16[2,128,512]{2,1,0:T(8,128)(2,1)S(1)} %slice.27), channel_id=1, source_target_pairs={{0,56},{8,0},{16,8},{24,16},{32,24},{40,32},{48,40},{56,48},{1,57}... | collective-permute-start | bytes 786440 | tf_op jit(solution)/shard_map/ppermute | solution.py:109
  81.9 13.0 %collective-permute-start.24 = (bf16[2,128,512]{2,1,0:T(8,128)(2,1)S(1)}, bf16[2,128,512]{2,1,0:T(8,128)(2,1)S(1)}, u32[]{:S(2)}, u32[]{:S(2)}) collective-permute-start(bf16[2,128,512]{2,1,0:T(8,128)(2,1)S(1)} %slice.26), channel_id=1, source_target_pairs={{0,8},{8,16},{16,24},{24,32},{32,40},{40,48},{48,56},{56,0},{1,9},... | collective-permute-start | bytes 786440 | tf_op jit(solution)/shard_map/ppermute | solution.py:108
  85.2 16.5 %copy-start.4 = (s32[1,1,4]{2,1,0:T(1,128)S(1)}, s32[1,1,4]{2,1,0:T(1,128)}, u32[]{:S(2)}) copy-start(s32[1,1,4]{2,1,0:T(1,128)} %param.8) | copy-start | bytes 52
  85.2 16.5 %copy-start.3 = (s32[1,1,4]{2,1,0:T(1,128)S(1)}, s32[1,1,4]{2,1,0:T(1,128)}, u32[]{:S(2)}) copy-start(s32[1,1,4]{2,1,0:T(1,128)} %param.7) | copy-start | bytes 52
  85.2 16.6 %copy-start = (bf16[2048,256]{1,0:T(8,128)(2,1)S(1)}, bf16[2048,256]{1,0:T(8,128)(2,1)}, u32[]{:S(2)}) copy-start(bf16[2048,256]{1,0:T(8,128)(2,1)} %param.6) | copy-start | bytes 3145732
  86.2 18.0 %collective-permute-start.26 = (bf16[32,128,512]{2,1,0:T(8,128)(2,1)}, bf16[32,128,512]{2,1,0:T(8,128)(2,1)}, u32[]{:S(2)}, u32[]{:S(2)}) collective-permute-start(bf16[32,128,512]{2,1,0:T(8,128)(2,1)} %bitcast.25.rest_0_), channel_id=1, source_target_pairs={{0,1},{1,0},{2,3},{3,2},{4,5},{5,4},{6,7},{7,6},{8,9},{9,8},{10,11... | collective-permute-start | bytes 12582920 | tf_op jit(solution)/shard_map/ppermute | solution.py:199
  98.3 9.7 %collective-permute-start.27 = (bf16[32,128,512]{2,1,0:T(8,128)(2,1)}, bf16[32,128,512]{2,1,0:T(8,128)(2,1)}, u32[]{:S(2)}, u32[]{:S(2)}) collective-permute-start(bf16[32,128,512]{2,1,0:T(8,128)(2,1)} %bitcast.34.rest_1_), channel_id=1, source_target_pairs={{0,1},{1,0},{2,3},{3,2},{4,5},{5,4},{6,7},{7,6},{8,9},{9,8},{10,11... | collective-permute-start | bytes 12582920 | tf_op jit(solution)/shard_map/ppermute | solution.py:200
  101.8 1.2 %copy-start.2 = (bf16[2048,256]{1,0:T(8,128)(2,1)S(1)}, bf16[2048,256]{1,0:T(8,128)(2,1)}, u32[]{:S(2)}) copy-start(bf16[2048,256]{1,0:T(8,128)(2,1)} %copy-done.1) | copy-start | bytes 3145732
  (1 other events, 1.0 us)
